TPU v7x, 128 devices: a whole 4x4x4 slice. The times are simulated.
128 devices in a mesh: frame: 32 (over z, x_hi, y), head: 4 (over x_lo, core).
Axes of the slice: x: 4 (x_hi: 2, x_lo: 2; x = x_hi * 2 + x_lo), y: 4, z: 4, core: 2. Of those that a mesh axis runs over, the one named last changes fastest.
Arguments:
- queries: bfloat16 [24576, 5120], P('frame', 'head'), may hold values from -6.4 to 6.4
- keys: bfloat16 [24576, 5120], P('frame', 'head'), may hold values from -6.4 to 6.4
- values: bfloat16 [24576, 5120], P('frame', 'head'), may hold values from -6 to 6
- out_weight: bfloat16 [5120, 5120], P('head'), may hold values from -0.078125 to 0.078125
- sink_owner: int32 [32], replicated, may hold values from 0 to 31, each once
- frame_pos: int32 [32], P('frame'), may hold values from 0 to 93, as said below
Outputs:
- mixed: bfloat16 [24576, 5120], P('frame', 'head')
Inputs may be any that keep to these rules, and one draw needn't show every extreme that they name: `frame_pos`: strictly increasing, first entry 0, steps of 2 to 4. `sink_owner`: each number once.
All inputs are finite; a program needn't handle non-finite values.
Results may differ from a plain program's by a relative error of at most 0.01.
Values may be sent and summed in bfloat16 or wider, within the bound.
No kernel may reach another device: no remote copies, remote signals or barrier semaphores. Data moves between devices by JAX's collectives and lax.ppermute only.
A program may use at most 192 MiB of HBM per device.

v0:
```python
import jax
import jax.numpy as jnp
from jax import lax
from jax.experimental import pallas as pl
from jax.experimental.pallas import tpu as pltpu
from jax.sharding import Mesh, NamedSharding, PartitionSpec as P

HDIM = 128
GRID_W = 32


def shifted(array, axis, by):
    length = lax.axis_size(axis)
    pairs = [(i, i + by) for i in range(length) if 0 <= i + by < length]
    return lax.ppermute(array, axis, pairs)


def broadcast(value, axis, source):
    kept = jnp.where(lax.axis_index(axis) == source, value, 0).astype(value.dtype)
    return lax.psum(kept, axis)


def pair_angles(frame_value, count):
    half = HDIM // 2
    tdim = HDIM - 4 * (HDIM // 6)
    sdim = 2 * (HDIM // 6)
    tcount = tdim // 2
    scount = sdim // 2
    index = jnp.arange(half)
    findex = index.astype(jnp.float32)
    freq = jnp.where(
        index < tcount,
        jnp.power(10000.0, -2.0 * findex / tdim),
        jnp.where(
            index < tcount + scount,
            jnp.power(10000.0, -2.0 * (findex - tcount) / sdim),
            jnp.power(10000.0, -2.0 * (findex - tcount - scount) / sdim),
        ),
    )
    token = jnp.arange(count)
    row_pos = (token // GRID_W).astype(jnp.float32)[:, None]
    col_pos = (token % GRID_W).astype(jnp.float32)[:, None]
    frame_f = jnp.zeros((count, 1), jnp.float32) + frame_value.astype(jnp.float32)
    pos = jnp.where(
        index[None, :] < tcount,
        frame_f,
        jnp.where(index[None, :] < tcount + scount, row_pos, col_pos),
    )
    return pos * freq[None, :]


def rotate(block, angle):
    count = block.shape[0]
    heads_here = block.shape[1] // HDIM
    parts = block.astype(jnp.float32).reshape(count, heads_here, HDIM // 2, 2)
    cosine = jnp.cos(angle)[:, None, :]
    sine = jnp.sin(angle)[:, None, :]
    first = parts[..., 0] * cosine - parts[..., 1] * sine
    second = parts[..., 0] * sine + parts[..., 1] * cosine
    return (
        jnp.stack([first, second], axis=-1).reshape(count, heads_here * HDIM).astype(jnp.bfloat16)
    )


def attend_block(query, key_block, value_block):
    count = query.shape[0]
    heads_here = query.shape[1] // HDIM
    qh = query.reshape(count, heads_here, HDIM)
    kh = key_block.reshape(-1, heads_here, HDIM)
    vh = value_block.reshape(-1, heads_here, HDIM)
    scores = jnp.einsum("qhd,khd->hqk", qh, kh, preferred_element_type=jnp.float32) / jnp.sqrt(
        jnp.float32(HDIM)
    )
    peak = jnp.max(scores, axis=-1)
    weights = jnp.exp(scores - peak[..., None]).astype(jnp.bfloat16)
    total = jnp.sum(weights.astype(jnp.float32), axis=-1)
    partial_value = jnp.einsum("hqk,khd->hqd", weights, vh, preferred_element_type=jnp.float32)
    return (peak, total, partial_value)


FRAME_AXES = ("z", "xh", "y")
HEAD_AXES = ("xl", "c")


def frame_index():
    return (lax.axis_index("z") * lax.axis_size("xh") + lax.axis_index("xh")) * lax.axis_size("y") + lax.axis_index(
        "y"
    )


def cyclic(array, axis, by):
    length = lax.axis_size(axis)
    return lax.ppermute(array, axis, [(i, (i + by) % length) for i in range(length)])


def ring_stage(data, axis, source):
    length = lax.axis_size(axis)
    if length == 1:
        return data
    rel = (lax.axis_index(axis) - source) % length
    if length == 2:
        got = cyclic(data, axis, 1)
        return jnp.where(rel == 0, data, got)
    assert length == 4
    half = data.shape[0] // 2
    h0, h1 = data[:half], data[half:]
    g0 = cyclic(h0, axis, 1)
    g1 = cyclic(h1, axis, -1)
    a0 = jnp.where(rel == 1, g0, h0)
    a1 = jnp.where(rel == 3, g1, h1)
    r_p = cyclic(jnp.where(rel == 0, h1, a0), axis, 1)
    r_m = cyclic(jnp.where(rel == 0, h0, a1), axis, -1)
    out0 = jnp.where(rel == 0, h0, jnp.where(rel == 1, g0, jnp.where(rel == 2, r_p, r_m)))
    out1 = jnp.where(rel == 0, h1, jnp.where(rel == 1, r_p, jnp.where(rel == 2, r_m, g1)))
    return jnp.concatenate([out0, out1], axis=0)


def sink_broadcast(data, sink):
    n_frame = lax.axis_size(FRAME_AXES)
    piece = data.shape[0] // n_frame
    spread = lax.all_to_all(data, FRAME_AXES, 0, 0, tiled=True)
    mine = lax.dynamic_slice_in_dim(spread, sink * piece, piece, axis=0)
    return lax.all_gather(mine, FRAME_AXES, axis=0, tiled=True)


def rope_tables(frame_value, count):
    angle = pair_angles(frame_value, count)
    cosine = jnp.cos(angle)
    sine = jnp.sin(angle)
    cos_full = jnp.stack([cosine, cosine], axis=-1).reshape(count, HDIM)
    sin_signed = jnp.stack([-sine, sine], axis=-1).reshape(count, HDIM)
    return cos_full, sin_signed


def attention_kernel(flags, q_ref, ks_ref, vs_ref, kp_ref, vp_ref, kk_ref, vk_ref, swap_ref, *rest):
    tables, out_ref = rest[:6], rest[6]
    swap = swap_ref[...]

    def rot(x_ref, cos_ref, sin_ref):
        x = x_ref[...]
        partner = jnp.dot(x, swap, preferred_element_type=jnp.float32)
        return (x.astype(jnp.float32) * cos_ref[...] + partner * sin_ref[...]).astype(jnp.bfloat16)

    q = rot(q_ref, tables[0], tables[1])
    scale = jnp.sqrt(jnp.float32(HDIM))

    def block(k_ref, v_ref, cos_ref, sin_ref):
        k = rot(k_ref, cos_ref, sin_ref)
        scores = lax.dot_general(q, k, (((1,), (1,)), ((), ())), preferred_element_type=jnp.float32) / scale
        peak = jnp.max(scores, axis=-1, keepdims=True)
        weights = jnp.exp(scores - peak).astype(jnp.bfloat16)
        total = jnp.sum(weights.astype(jnp.float32), axis=-1, keepdims=True)
        partial_value = jnp.dot(weights, v_ref[...], preferred_element_type=jnp.float32)
        return peak, total, partial_value

    m_self, l_self, o_self = block(ks_ref, vs_ref, tables[0], tables[1])
    m_prev, l_prev, o_prev = block(kp_ref, vp_ref, tables[2], tables[3])
    m_sink, l_sink, o_sink = block(kk_ref, vk_ref, tables[4], tables[5])
    prev_used = flags[0] != 0
    sink_used = flags[1] != 0
    top = jnp.maximum(m_self, jnp.where(prev_used, m_prev, m_self))
    top = jnp.maximum(top, jnp.where(sink_used, m_sink, m_self))
    c_self = jnp.exp(m_self - top)
    c_prev = jnp.where(prev_used, jnp.exp(m_prev - top), 0.0)
    c_sink = jnp.where(sink_used, jnp.exp(m_sink - top), 0.0)
    numer = o_self * c_self + o_prev * c_prev + o_sink * c_sink
    denom = l_self * c_self + l_prev * c_prev + l_sink * c_sink
    out_ref[...] = (numer / denom).astype(out_ref.dtype)


def attention(flags, queries, blocks, tables):
    count, width = queries.shape
    heads_here = width // HDIM
    lane = jnp.arange(HDIM)
    swap = (lane[:, None] == (lane[None, :] ^ 1)).astype(jnp.bfloat16)
    head_spec = pl.BlockSpec((count, HDIM), lambda h, flags: (0, h))
    whole_spec = pl.BlockSpec((count, HDIM), lambda h, flags: (0, 0))
    swap_spec = pl.BlockSpec((HDIM, HDIM), lambda h, flags: (0, 0))
    grid_spec = pltpu.PrefetchScalarGridSpec(
        num_scalar_prefetch=1,
        grid=(heads_here,),
        in_specs=[head_spec] * 7 + [swap_spec] + [whole_spec] * 6,
        out_specs=head_spec,
    )
    flops = heads_here * 3 * 4 * count * count * HDIM
    cost = pl.CostEstimate(
        flops=flops,
        transcendentals=heads_here * 3 * count * count,
        bytes_accessed=8 * count * width * 2 + 6 * count * HDIM * 4,
    )
    return pl.pallas_call(
        attention_kernel,
        grid_spec=grid_spec,
        out_shape=jax.ShapeDtypeStruct((count, width), jnp.bfloat16),
        cost_estimate=cost,
    )(flags, queries, *blocks, swap, *tables)


def shards(queries, keys, values, out_weight, sink_owner, frame_pos):
    count = queries.shape[0]
    place = frame_index()
    n_frame = lax.axis_size(FRAME_AXES)
    sink = sink_owner[0] % (n_frame // 2)
    sink_kv = sink_broadcast(jnp.concatenate([keys, values], axis=0), sink)
    prev_k, prev_v = shifted((keys, values), FRAME_AXES, 1)
    positions = lax.all_gather(frame_pos, FRAME_AXES, axis=0, tiled=True)
    prev_used = (place >= 1) & (place - 1 != sink)
    sink_used = sink < place
    flags = jnp.stack([prev_used, sink_used]).astype(jnp.int32)
    tables = (
        rope_tables(frame_pos[0], count)
        + rope_tables(positions[jnp.maximum(place - 1, 0)], count)
        + rope_tables(positions[sink], count)
    )
    blocks = (keys, values, prev_k, prev_v, sink_kv[:count], sink_kv[count:])
    attended = attention(flags, queries, blocks, tables)
    terms = jnp.dot(attended, out_weight, preferred_element_type=jnp.float32)
    mixed = lax.psum_scatter(terms.astype(jnp.bfloat16), HEAD_AXES, scatter_dimension=1, tiled=True)
    return mixed


def solution(mesh):
    frame_phys = {"z": 4, "xh": 2, "y": 4}
    head_phys = {"xl": 2, "c": 2}
    assert mesh.shape["frame"] == 32 and mesh.shape["head"] == 4
    devices = mesh.devices.reshape(tuple(frame_phys.values()) + tuple(head_phys.values()))
    fine = Mesh(devices, FRAME_AXES + HEAD_AXES)
    in_specs = (
        P(FRAME_AXES, HEAD_AXES),
        P(FRAME_AXES, HEAD_AXES),
        P(FRAME_AXES, HEAD_AXES),
        P(HEAD_AXES, None),
        P(),
        P(FRAME_AXES),
    )
    out_specs = P(FRAME_AXES, HEAD_AXES)
    inner = jax.shard_map(shards, mesh=fine, in_specs=in_specs, out_specs=out_specs, check_vma=False)

    def run(*args):
        out = inner(*args)
        return jax.lax.with_sharding_constraint(out, NamedSharding(mesh, P("frame", "head")))

    return run
```

profile of v0, /device:TPU:1, one launch (start us, length us, event | category | flops | bytes accessed | tf_op | source)
XLA Modules:
  0.0 375.5 jit_solution(11060388658593566410)
XLA Ops:
  6.5 4.3 %pad_maximum_fusion = bf16[1536,1280]{1,0:T(8,128)(2,1)} fusion(bf16[768,1280]{1,0:T(8,128)(2,1)} %vs_ref.1, bf16[768,1280]{1,0:T(8,128)(2,1)} %ks_ref.1), kind=kLoop, calls=%fused_computation.1 | loop fusion | flops 7864320 | bytes 7864320 | tf_op jit(solution)/shard_map/concatenate | solution.py:204
  10.8 11.6 %all-to-all-start = ((bf16[32,48,1280]{2,1,0:T(8,128)(2,1)}), bf16[32,48,1280]{2,1,0:T(8,128)(2,1)}, u32[]{:S(2)}, u32[]{:S(2)}) async-start(bf16[32,48,1280]{2,1,0:T(8,128)(2,1)} %bitcast.24), calls=%async_computation | async-start | bytes 7864320 | tf_op jit(solution)/shard_map/all_to_all | solution.py:121
  22.4 0.0 all-gather.2.cloned.1.call-start
  22.5 0.0 copy-done.1
  22.6 50.5 %all-to-all-done = bf16[32,48,1280]{2,1,0:T(8,128)(2,1)} async-done(((bf16[32,48,1280]{2,1,0:T(8,128)(2,1)}), bf16[32,48,1280]{2,1,0:T(8,128)(2,1)}, u32[]{:S(2)}, u32[]{:S(2)}) %all-to-all-start) | async-done | bytes 3932192 | tf_op jit(solution)/shard_map/all_to_all | solution.py:121
  73.1 1.5 constant_dynamic-slice_fusion
  74.7 0.0 all-gather.2.cloned.1.call-update
  74.7 0.0 reduce-scatter.2.cloned.1.call-start
  74.8 2.9 collective-permute-start
  77.7 0.0 copy-done
  77.7 3.7 collective-permute-start.1
  82.1 0.0 copy-done.2
  82.1 0.6 dynamic-slice
  82.7 0.8 dynamic-update-slice
  83.5 92.7 %all-reduce = s32[32]{0:T(128)S(1)} all-reduce(s32[32]{0:T(128)S(1)} %dynamic-update-slice), channel_id=1, replica_groups=mesh['z'=4,'xh'=2,'y'=4,'xl'=2,'c'=2] {'z','xh','y'}, use_global_device_ids=true, to_apply=%add | all-reduce | flops 32 | bytes 256
  176.2 0.6 fusion.23
  178.0 3.1 fusion.10
  181.1 0.1 pad_maximum_fusion.1
  181.2 0.3 copy.13
  181.5 0.3 reshape.1043
  181.8 1.0 copy.19.rest_0_
  182.7 0.3 copy.14
  183.0 0.3 reshape.1044
  183.3 0.9 copy.20.rest_1_
  184.2 1.3 pad_maximum_fusion.3
  185.5 0.3 copy.15
  185.8 0.3 reshape.1045
  186.1 1.0 copy.21.rest_2_
  187.1 0.3 copy.16
  187.4 0.3 reshape.1046
  187.7 0.9 copy.22.rest_3_
  188.6 1.0 pad_maximum_fusion.5
  189.6 0.3 copy.17
  189.9 0.3 reshape.1047
  190.1 0.9 copy.23.rest_4_
  191.1 0.3 copy.18
  191.4 0.3 reshape.1048
  191.7 0.9 copy.24.rest_5_
  192.6 0.6 add_convert_fusion.flags
  193.1 0.6 fusion.9.swap_ref
  193.8 36.2 %all-gather.2.cloned.1.call-done = bf16[1536,1280]{1,0:T(8,128)(2,1)} async-done(((bf16[48,1280]{1,0:T(8,128)(2,1)}), bf16[1536,1280]{1,0:T(8,128)(2,1)}) %all-gather.2.cloned.1.call-update) | async-done | bytes 3932176 | tf_op jit(solution)/shard_map/all_gather | solution.py:123
  230.0 4.3 %fusion.22 = (bf16[768,1280]{1,0:T(8,128)(2,1)}, bf16[768,1280]{1,0:T(8,128)(2,1)}) fusion(bf16[1536,1280]{1,0:T(8,128)(2,1)} %all-gather.2.cloned.1.call-done), kind=kLoop, calls=%fused_computation.44 | loop fusion | bytes 7864320 | tf_op jit(solution)/shard_map/slice | solution.py:215
  234.3 0.0 collective-permute-done.kp_ref
  234.3 0.0 collective-permute-done.1.vp_ref
  234.3 41.4 %shard_map.64 = bf16[768,1280]{1,0:T(8,128)(2,1)} custom-call(s32[2]{0:T(128)} %add_convert_fusion.flags, bf16[768,1280]{1,0:T(8,128)(2,1)} %q_ref.1, bf16[768,1280]{1,0:T(8,128)(2,1)} %ks_ref.1, bf16[768,1280]{1,0:T(8,128)(2,1)} %vs_ref.1, bf16[768,1280]{1,0:T(8,128)(2,1)} %collective-permute-done.kp_ref, bf16[768,1280]{1,0:T(8,128)(2,1)} %collective-permute-done.1.vp_ref, ...), custom_call_target="tpu_custom_call" | custom-call | flops 9059696640 | bytes 18087936 | tf_op jit(solution)/shard_map/pallas_call | solution.py:191
  275.7 17.8 %convolution_convert_fusion = bf16[768,5120]{1,0:T(8,128)(2,1)} fusion(bf16[768,1280]{1,0:T(8,128)(2,1)} %shard_map.64, bf16[1280,5120]{1,0:T(8,128)(2,1)} %param.9), kind=kOutput, calls=%fused_computation | convolution fusion | flops 10070261760 | bytes 22937600 | tf_op jit(solution)/shard_map/dot_general | solution.py:217
  293.4 0.0 reduce-scatter.2.cloned.1.call-update
  293.5 75.2 %reduce-scatter.2.cloned.1.call-done = bf16[768,1280]{1,0:T(8,128)(2,1)} async-done(((bf16[768,5120]{1,0:T(8,128)(2,1)}), bf16[768,1280]{1,0:T(8,128)(2,1)}) %reduce-scatter.2.cloned.1.call-update) | async-done | bytes 1966096 | tf_op jit(solution)/shard_map/reduce_scatter | solution.py:218
  (10 shorter events, 0.0 us)
Async XLA Ops:
  10.8 11.7 %copy-start.1 = (s32[32]{0:T(128)S(1)}, s32[32]{0:T(128)}, u32[]{:S(2)}) copy-start(s32[32]{0:T(128)} %param.10) | copy-start | bytes 388
  10.8 66.9 %copy-start = (bf16[768,1280]{1,0:T(8,128)(2,1)S(1)}, bf16[768,1280]{1,0:T(8,128)(2,1)}, u32[]{:S(2)}) copy-start(bf16[768,1280]{1,0:T(8,128)(2,1)} %vs_ref.1) | copy-start | bytes 5898244
  10.8 71.3 %copy-start.2 = (u32[128]{0:T(128)S(1)}, u32[128]{0:T(128)}, u32[]{:S(2)}) copy-start(u32[128]{0:T(128)} %constant.110) | copy-start | bytes 1540
  10.8 62.3 %all-to-all-start = ((bf16[32,48,1280]{2,1,0:T(8,128)(2,1)}), bf16[32,48,1280]{2,1,0:T(8,128)(2,1)}, u32[]{:S(2)}, u32[]{:S(2)}) async-start(bf16[32,48,1280]{2,1,0:T(8,128)(2,1)} %bitcast.24), calls=%async_computation | async-start | bytes 7864320 | tf_op jit(solution)/shard_map/all_to_all | solution.py:121
  22.4 207.5 %all-gather.2.cloned.1.call-start = ((), (), s32[]{:S(2)}) async-start(), calls=%async_computation.2 | async-start | bytes 4055040 | tf_op jit(solution)/shard_map/all_gather | solution.py:123
  74.7 294.0 %reduce-scatter.2.cloned.1.call-start = ((), (), s32[]{:S(2)}) async-start(), calls=%async_computation.3 | async-start | bytes 9830400 | tf_op jit(solution)/shard_map/reduce_scatter | solution.py:218
  74.8 159.5 %collective-permute-start = (bf16[768,1280]{1,0:T(8,128)(2,1)}, bf16[768,1280]{1,0:T(8,128)(2,1)}, u32[]{:S(2)}, u32[]{:S(2)}) collective-permute-start(bf16[768,1280]{1,0:T(8,128)(2,1)} %ks_ref.1), channel_id=1, source_target_pairs={{0,4},{4,8},{8,12},{12,16},{16,20},{20,24},{24,28},{28,32},{32,36}... | collective-permute-start | bytes 5898248 | tf_op jit(solution)/shard_map/ppermute | solution.py:15
  77.7 156.6 %collective-permute-start.1 = (bf16[768,1280]{1,0:T(8,128)(2,1)S(1)}, bf16[768,1280]{1,0:T(8,128)(2,1)}, u32[]{:S(2)}, u32[]{:S(2)}) collective-permute-start(bf16[768,1280]{1,0:T(8,128)(2,1)S(1)} %copy-done), channel_id=1, source_target_pairs={{0,4},{4,8},{8,12},{12,16},{16,20},{20,24},{24,28},{28,32},{32,36}... | collective-permute-start | bytes 5898248 | tf_op jit(solution)/shard_map/ppermute | solution.py:15
Sparse Core Ops, SparseCore 0:
  74.8 155.0 all-gather.1
  293.6 75.0 reduce-scatter.1
where the time goes:
time: 376 us
  waiting for transfers between devices  162 us (43%)
  blocking collectives  92.7 us (25%)
  Pallas kernels  41.4 us (11%)
  starting transfers between devices  18.3 us (5%)
  matrix products  17.8 us (5%)
  local copies, waits for them, and re-layouts  16.9 us (4%)
  between operations  15.5 us (4%)
  other arithmetic  10.9 us (3%)
    unnamed x1, blocking collectives  92.7 us
    reduce_scatter x1, waiting for transfers between devices, shards(): lax.psum_scatter(terms.astype(jnp.bfloat16), HEAD_AXES, scatter_dimension...  75.2 us
    all_to_all x1, waiting for transfers between devices, sink_broadcast(): spread = lax.all_to_all(data, FRAME_AXES, 0, 0, tiled=True)  50.5 us
    pallas_call x1, Pallas kernels, attention(): pl.pallas_call(attention_kernel, grid_spec=grid_spec, out_shape=jax.Shape...  41.4 us
    all_gather x1, waiting for transfers between devices, sink_broadcast(): return lax.all_gather(mine, FRAME_AXES, axis=0, tiled=True)  36.2 us
    dot_general x1, matrix products, shards(): terms = jnp.dot(attended, out_weight, preferred_element_type=jnp.float32)  17.8 us
    all_to_all x1, starting transfers between devices, sink_broadcast(): spread = lax.all_to_all(data, FRAME_AXES, 0, 0, tiled=True)  11.6 us
  transfers between devices with their start and end apart: 5, of which 3 were waited for; matrix products, arithmetic and copies ran while one was open for 6% of the time, Pallas kernels for 0%

commit v1 on v0

--- a/solution.py
+++ b/solution.py
@@ -120,7 +120,8 @@
     piece = data.shape[0] // n_frame
     spread = lax.all_to_all(data, FRAME_AXES, 0, 0, tiled=True)
     mine = lax.dynamic_slice_in_dim(spread, sink * piece, piece, axis=0)
-    return lax.all_gather(mine, FRAME_AXES, axis=0, tiled=True)
+    copies = jnp.broadcast_to(mine[None], (n_frame,) + mine.shape).reshape(data.shape)
+    return lax.all_to_all(copies, FRAME_AXES, 0, 0, tiled=True)
 
 
 def rope_tables(frame_value, count):
@@ -203,7 +204,8 @@
     sink = sink_owner[0] % (n_frame // 2)
     sink_kv = sink_broadcast(jnp.concatenate([keys, values], axis=0), sink)
     prev_k, prev_v = shifted((keys, values), FRAME_AXES, 1)
-    positions = lax.all_gather(frame_pos, FRAME_AXES, axis=0, tiled=True)
+    own_pos = jnp.broadcast_to(frame_pos[:1, None], (n_frame, 128))
+    positions = lax.all_to_all(own_pos, FRAME_AXES, 0, 0, tiled=True)[:, 0]
     prev_used = (place >= 1) & (place - 1 != sink)
     sink_used = sink < place
     flags = jnp.stack([prev_used, sink_used]).astype(jnp.int32)

time: 376 us -> 383 us (1.019)
  blocking collectives: 92.7 us -> 0 us
  waiting for transfers between devices: 162 us -> 246 us
  starting transfers between devices: 18.3 us -> 33.2 us
    unnamed x1 -> x0, blocking collectives: 92.7 us -> none
    ppermute x2, waiting for transfers between devices: 0.01 us -> 72.8 us  [shifted(): return lax.ppermute(array, axis, pairs)]
    all_gather x1 -> x0, waiting for transfers between devices: 36.2 us -> none  [sink_broadcast(): return lax.all_gather(mine, FRAME_AXES, axis=0, tiled=True)]
    all_to_all x0 -> x2, waiting for transfers between devices: none -> 30.7 us  [the longest x1 23.1 us: sink_broadcast(): return lax.all_to_all(copies, FRAME_AXES, 0, 0, tiled=True)]
    reduce_scatter x1, waiting for transfers between devices: 75.2 us -> 92.8 us  [shards(): lax.psum_scatter(terms.astype(jnp.bfloat16), HEAD_AXES, scatter_dimension...]
    all_to_all x0 -> x2, starting transfers between devices: none -> 14.3 us  [the longest x1 9.3 us: shards(): positions = lax.all_to_all(own_pos, FRAME_AXES, 0, 0, tiled=True)[:, 0]]
  transfers between devices with their start and end apart: 5 -> 6, of which waited for: 3 -> 6; matrix products, arithmetic and copies ran while one was open for 6% -> 6% of each run, Pallas kernels for 0% -> 0%
where the time goes in v1:
time: 383 us
  waiting for transfers between devices  246 us (64%)
  Pallas kernels  41.4 us (11%)
  starting transfers between devices  33.2 us (9%)
  local copies, waits for them, and re-layouts  17.7 us (5%)
  matrix products  17.6 us (5%)
  between operations  15.6 us (4%)
  other arithmetic  11 us (3%)
    reduce_scatter x1, waiting for transfers between devices, shards(): lax.psum_scatter(terms.astype(jnp.bfloat16), HEAD_AXES, scatter_dimension...  92.8 us
    ppermute x2, waiting for transfers between devices, shifted(): return lax.ppermute(array, axis, pairs)  72.8 us
    all_to_all x1, waiting for transfers between devices, sink_broadcast(): spread = lax.all_to_all(data, FRAME_AXES, 0, 0, tiled=True)  49.9 us
    pallas_call x1, Pallas kernels, attention(): pl.pallas_call(attention_kernel, grid_spec=grid_spec, out_shape=jax.Shape...  41.4 us
    all_to_all x1, waiting for transfers between devices, sink_broadcast(): return lax.all_to_all(copies, FRAME_AXES, 0, 0, tiled=True)  23.1 us
    dot_general x1, matrix products, shards(): terms = jnp.dot(attended, out_weight, preferred_element_type=jnp.float32)  17.6 us
    all_to_all x1, starting transfers between devices, sink_broadcast(): spread = lax.all_to_all(data, FRAME_AXES, 0, 0, tiled=True)  11.6 us
    all_to_all x1, starting transfers between devices, shards(): positions = lax.all_to_all(own_pos, FRAME_AXES, 0, 0, tiled=True)[:, 0]  9.3 us
  transfers between devices with their start and end apart: 6, of which 6 were waited for; matrix products, arithmetic and copies ran while one was open for 6% of the time, Pallas kernels for 0%

profile of v1, /device:TPU:1, one launch (start us, length us, event | category | flops | bytes accessed | tf_op | source)
XLA Modules:
  0.0 382.8 jit_solution(11915208193671102562)
XLA Ops:
  6.5 4.3 %pad_maximum_fusion = bf16[1536,1280]{1,0:T(8,128)(2,1)} fusion(bf16[768,1280]{1,0:T(8,128)(2,1)} %vs_ref.1, bf16[768,1280]{1,0:T(8,128)(2,1)} %ks_ref.1), kind=kLoop, calls=%fused_computation.1 | loop fusion | flops 7864320 | bytes 7864320 | tf_op jit(solution)/shard_map/concatenate | solution.py:205
  10.8 0.0 copy-start.1
  10.8 11.6 %all-to-all-start = ((bf16[32,48,1280]{2,1,0:T(8,128)(2,1)}), bf16[32,48,1280]{2,1,0:T(8,128)(2,1)}, u32[]{:S(2)}, u32[]{:S(2)}) async-start(bf16[32,48,1280]{2,1,0:T(8,128)(2,1)} %bitcast.29), calls=%async_computation | async-start | bytes 7864320 | tf_op jit(solution)/shard_map/all_to_all | solution.py:121
  22.4 0.0 copy-done.1
  23.2 49.9 %all-to-all-done = bf16[32,48,1280]{2,1,0:T(8,128)(2,1)} async-done(((bf16[32,48,1280]{2,1,0:T(8,128)(2,1)}), bf16[32,48,1280]{2,1,0:T(8,128)(2,1)}, u32[]{:S(2)}, u32[]{:S(2)}) %all-to-all-start) | async-done | bytes 3932192 | tf_op jit(solution)/shard_map/all_to_all | solution.py:121
  73.1 0.6 broadcast_in_dim.125
  73.7 9.3 %all-to-all-start.2 = ((s32[32,1,128]{2,1,0:T(1,128)}), s32[32,1,128]{2,1,0:T(1,128)S(1)}, u32[]{:S(2)}, u32[]{:S(2)}) async-start(s32[32,1,128]{2,1,0:T(1,128)} %broadcast_in_dim.125), calls=%async_computation.2 | async-start | bytes 32768 | tf_op jit(solution)/shard_map/all_to_all | solution.py:208
  83.0 0.9 constant_dynamic-slice_fusion.2
  83.9 7.6 %all-to-all-done.2 = s32[32,1,128]{2,1,0:T(1,128)S(1)} async-done(((s32[32,1,128]{2,1,0:T(1,128)}), s32[32,1,128]{2,1,0:T(1,128)S(1)}, u32[]{:S(2)}, u32[]{:S(2)}) %all-to-all-start.2) | async-done | bytes 16416 | tf_op jit(solution)/shard_map/all_to_all | solution.py:208
  91.6 2.2 broadcast_in_dim.119
  93.8 5.0 %all-to-all-start.1 = ((bf16[32,48,1280]{2,1,0:T(8,128)(2,1)}), bf16[32,48,1280]{2,1,0:T(8,128)(2,1)}, u32[]{:S(2)}, u32[]{:S(2)}) async-start(bf16[32,48,1280]{2,1,0:T(8,128)(2,1)} %broadcast_in_dim.119), calls=%async_computation.1 | async-start | bytes 7864320 | tf_op jit(solution)/shard_map/all_to_all | solution.py:124
  98.8 0.0 reduce-scatter.2.cloned.1.call-start
  98.8 0.0 copy-done
  98.8 4.3 %collective-permute-start = (bf16[768,1280]{1,0:T(8,128)(2,1)S(1)}, bf16[768,1280]{1,0:T(8,128)(2,1)}, u32[]{:S(2)}, u32[]{:S(2)}) collective-permute-start(bf16[768,1280]{1,0:T(8,128)(2,1)S(1)} %copy-done), channel_id=1, source_target_pairs={{0,4},{4,8},{8,12},{12,16},{16,20},{20,24},{24,28},{28,32},{32,36}... | collective-permute-start | bytes 5898248 | tf_op jit(solution)/shard_map/ppermute | solution.py:15
  103.1 3.1 collective-permute-start.1
  106.2 0.7 add_convert_fusion.flags
  106.9 0.6 fusion.9.swap_ref
  107.5 0.5 constant_dynamic-slice_fusion
  109.3 3.1 fusion.10
  112.4 0.1 pad_maximum_fusion.1
  112.5 0.3 copy.13
  112.8 0.3 reshape.1056
  113.0 0.9 copy.19.rest_0_
  114.0 0.3 copy.14
  114.3 0.3 reshape.1057
  114.5 0.9 copy.20.rest_1_
  115.5 1.3 pad_maximum_fusion.3
  116.7 0.3 copy.15
  117.1 0.3 reshape.1058
  117.3 0.9 copy.21.rest_2_
  118.3 0.3 copy.16
  118.6 0.3 reshape.1059
  118.9 0.9 copy.22.rest_3_
  119.8 1.0 pad_maximum_fusion.5
  120.8 0.3 copy.17
  121.1 0.3 reshape.1060
  121.4 0.9 copy.23.rest_4_
  122.3 0.3 copy.18
  122.6 0.3 reshape.1061
  122.9 0.9 copy.24.rest_5_
  123.8 23.1 %all-to-all-done.1 = bf16[32,48,1280]{2,1,0:T(8,128)(2,1)} async-done(((bf16[32,48,1280]{2,1,0:T(8,128)(2,1)}), bf16[32,48,1280]{2,1,0:T(8,128)(2,1)}, u32[]{:S(2)}, u32[]{:S(2)}) %all-to-all-start.1) | async-done | bytes 3932192 | tf_op jit(solution)/shard_map/all_to_all | solution.py:124
  146.9 4.4 %fusion.22 = (bf16[16,48,1280]{2,1,0:T(8,128)(2,1)}, bf16[16,48,1280]{2,1,0:T(8,128)(2,1)}) fusion(bf16[32,48,1280]{2,1,0:T(8,128)(2,1)} %all-to-all-done.1), kind=kLoop, calls=%fused_computation.46 | loop fusion | bytes 7864320 | tf_op jit(solution)/shard_map/slice | solution.py:217
  151.3 30.6 %collective-permute-done.kp_ref = bf16[768,1280]{1,0:T(8,128)(2,1)} collective-permute-done((bf16[768,1280]{1,0:T(8,128)(2,1)S(1)}, bf16[768,1280]{1,0:T(8,128)(2,1)}, u32[]{:S(2)}, u32[]{:S(2)}) %collective-permute-start) | collective-permute-done | bytes 1966112 | tf_op jit(solution)/shard_map/ppermute | solution.py:15
  181.8 42.2 %collective-permute-done.1.vp_ref = bf16[768,1280]{1,0:T(8,128)(2,1)} collective-permute-done((bf16[768,1280]{1,0:T(8,128)(2,1)}, bf16[768,1280]{1,0:T(8,128)(2,1)}, u32[]{:S(2)}, u32[]{:S(2)}) %collective-permute-start.1) | collective-permute-done | bytes 1966112 | tf_op jit(solution)/shard_map/ppermute | solution.py:15
  224.1 41.4 %shard_map.64 = bf16[768,1280]{1,0:T(8,128)(2,1)} custom-call(s32[2]{0:T(128)} %add_convert_fusion.flags, bf16[768,1280]{1,0:T(8,128)(2,1)} %q_ref.1, bf16[768,1280]{1,0:T(8,128)(2,1)} %ks_ref.1, bf16[768,1280]{1,0:T(8,128)(2,1)} %vs_ref.1, bf16[768,1280]{1,0:T(8,128)(2,1)} %collective-permute-done.kp_ref, bf16[768,1280]{1,0:T(8,128)(2,1)} %collective-permute-done.1.vp_ref, ...), custom_call_target="tpu_custom_call" | custom-call | flops 9059696640 | bytes 18087936 | tf_op jit(solution)/shard_map/pallas_call | solution.py:192
  265.5 17.6 %convolution_convert_fusion = bf16[768,5120]{1,0:T(8,128)(2,1)} fusion(bf16[768,1280]{1,0:T(8,128)(2,1)} %shard_map.64, bf16[1280,5120]{1,0:T(8,128)(2,1)} %param.9), kind=kOutput, calls=%fused_computation | convolution fusion | flops 10070261760 | bytes 22937600 | tf_op jit(solution)/shard_map/dot_general | solution.py:219
  283.1 0.0 reduce-scatter.2.cloned.1.call-update
  283.1 92.8 %reduce-scatter.2.cloned.1.call-done = bf16[768,1280]{1,0:T(8,128)(2,1)} async-done(((bf16[768,5120]{1,0:T(8,128)(2,1)}), bf16[768,1280]{1,0:T(8,128)(2,1)}) %reduce-scatter.2.cloned.1.call-update) | async-done | bytes 1966096 | tf_op jit(solution)/shard_map/reduce_scatter | solution.py:220
  (7 shorter events, 0.0 us)
Async XLA Ops:
  10.8 11.6 %copy-start.1 = (s32[32]{0:T(128)S(1)}, s32[32]{0:T(128)}, u32[]{:S(2)}) copy-start(s32[32]{0:T(128)} %param.10) | copy-start | bytes 388
  10.8 62.3 %all-to-all-start = ((bf16[32,48,1280]{2,1,0:T(8,128)(2,1)}), bf16[32,48,1280]{2,1,0:T(8,128)(2,1)}, u32[]{:S(2)}, u32[]{:S(2)}) async-start(bf16[32,48,1280]{2,1,0:T(8,128)(2,1)} %bitcast.29), calls=%async_computation | async-start | bytes 7864320 | tf_op jit(solution)/shard_map/all_to_all | solution.py:121
  73.7 17.9 %all-to-all-start.2 = ((s32[32,1,128]{2,1,0:T(1,128)}), s32[32,1,128]{2,1,0:T(1,128)S(1)}, u32[]{:S(2)}, u32[]{:S(2)}) async-start(s32[32,1,128]{2,1,0:T(1,128)} %broadcast_in_dim.125), calls=%async_computation.2 | async-start | bytes 32768 | tf_op jit(solution)/shard_map/all_to_all | solution.py:208
  93.8 5.0 %copy-start = (bf16[768,1280]{1,0:T(8,128)(2,1)S(1)}, bf16[768,1280]{1,0:T(8,128)(2,1)}, u32[]{:S(2)}) copy-start(bf16[768,1280]{1,0:T(8,128)(2,1)} %ks_ref.1) | copy-start | bytes 5898244
  93.8 53.1 %all-to-all-start.1 = ((bf16[32,48,1280]{2,1,0:T(8,128)(2,1)}), bf16[32,48,1280]{2,1,0:T(8,128)(2,1)}, u32[]{:S(2)}, u32[]{:S(2)}) async-start(bf16[32,48,1280]{2,1,0:T(8,128)(2,1)} %broadcast_in_dim.119), calls=%async_computation.1 | async-start | bytes 7864320 | tf_op jit(solution)/shard_map/all_to_all | solution.py:124
  98.8 277.1 %reduce-scatter.2.cloned.1.call-start = ((), (), s32[]{:S(2)}) async-start(), calls=%async_computation.4 | async-start | bytes 9830400 | tf_op jit(solution)/shard_map/reduce_scatter | solution.py:220
  98.8 83.0 %collective-permute-start = (bf16[768,1280]{1,0:T(8,128)(2,1)S(1)}, bf16[768,1280]{1,0:T(8,128)(2,1)}, u32[]{:S(2)}, u32[]{:S(2)}) collective-permute-start(bf16[768,1280]{1,0:T(8,128)(2,1)S(1)} %copy-done), channel_id=1, source_target_pairs={{0,4},{4,8},{8,12},{12,16},{16,20},{20,24},{24,28},{28,32},{32,36}... | collective-permute-start | bytes 5898248 | tf_op jit(solution)/shard_map/ppermute | solution.py:15
  103.1 121.0 %collective-permute-start.1 = (bf16[768,1280]{1,0:T(8,128)(2,1)}, bf16[768,1280]{1,0:T(8,128)(2,1)}, u32[]{:S(2)}, u32[]{:S(2)}) collective-permute-start(bf16[768,1280]{1,0:T(8,128)(2,1)} %vs_ref.1), channel_id=1, source_target_pairs={{0,4},{4,8},{8,12},{12,16},{16,20},{20,24},{24,28},{28,32},{32,36}... | collective-permute-start | bytes 5898248 | tf_op jit(solution)/shard_map/ppermute | solution.py:15
Sparse Core Ops, SparseCore 0:
  283.3 92.6 reduce-scatter.1

commit v2 on v1

--- a/solution.py
+++ b/solution.py
@@ -133,68 +133,104 @@
     return cos_full, sin_signed
 
 
-def attention_kernel(flags, q_ref, ks_ref, vs_ref, kp_ref, vp_ref, kk_ref, vk_ref, swap_ref, *rest):
-    tables, out_ref = rest[:6], rest[6]
+def rotate_ref(x_ref, cos_ref, sin_ref, swap):
+    x = x_ref[...]
+    partner = jnp.dot(x, swap, preferred_element_type=jnp.float32)
+    return (x.astype(jnp.float32) * cos_ref[...] + partner * sin_ref[...]).astype(jnp.bfloat16)
+
+
+def attend_ref(q, k, v_ref):
+    scale = jnp.sqrt(jnp.float32(HDIM))
+    scores = lax.dot_general(q, k, (((1,), (1,)), ((), ())), preferred_element_type=jnp.float32) / scale
+    peak = jnp.max(scores, axis=-1, keepdims=True)
+    weights = jnp.exp(scores - peak).astype(jnp.bfloat16)
+    total = jnp.sum(weights.astype(jnp.float32), axis=-1, keepdims=True)
+    partial_value = jnp.dot(weights, v_ref[...], preferred_element_type=jnp.float32)
+    return peak, total, partial_value
+
+
+def near_kernel(flags, q_ref, ks_ref, vs_ref, kp_ref, vp_ref, swap_ref, cq, sq, cp, sp, m_ref, l_ref, o_ref):
     swap = swap_ref[...]
-
-    def rot(x_ref, cos_ref, sin_ref):
-        x = x_ref[...]
-        partner = jnp.dot(x, swap, preferred_element_type=jnp.float32)
-        return (x.astype(jnp.float32) * cos_ref[...] + partner * sin_ref[...]).astype(jnp.bfloat16)
-
-    q = rot(q_ref, tables[0], tables[1])
-    scale = jnp.sqrt(jnp.float32(HDIM))
-
-    def block(k_ref, v_ref, cos_ref, sin_ref):
-        k = rot(k_ref, cos_ref, sin_ref)
-        scores = lax.dot_general(q, k, (((1,), (1,)), ((), ())), preferred_element_type=jnp.float32) / scale
-        peak = jnp.max(scores, axis=-1, keepdims=True)
-        weights = jnp.exp(scores - peak).astype(jnp.bfloat16)
-        total = jnp.sum(weights.astype(jnp.float32), axis=-1, keepdims=True)
-        partial_value = jnp.dot(weights, v_ref[...], preferred_element_type=jnp.float32)
-        return peak, total, partial_value
-
-    m_self, l_self, o_self = block(ks_ref, vs_ref, tables[0], tables[1])
-    m_prev, l_prev, o_prev = block(kp_ref, vp_ref, tables[2], tables[3])
-    m_sink, l_sink, o_sink = block(kk_ref, vk_ref, tables[4], tables[5])
+    q = rotate_ref(q_ref, cq, sq, swap)
+    m_self, l_self, o_self = attend_ref(q, rotate_ref(ks_ref, cq, sq, swap), vs_ref)
+    m_prev, l_prev, o_prev = attend_ref(q, rotate_ref(kp_ref, cp, sp, swap), vp_ref)
     prev_used = flags[0] != 0
-    sink_used = flags[1] != 0
     top = jnp.maximum(m_self, jnp.where(prev_used, m_prev, m_self))
-    top = jnp.maximum(top, jnp.where(sink_used, m_sink, m_self))
     c_self = jnp.exp(m_self - top)
     c_prev = jnp.where(prev_used, jnp.exp(m_prev - top), 0.0)
+    m_ref[...] = jnp.broadcast_to(top, m_ref.shape)
+    l_ref[...] = jnp.broadcast_to(l_self * c_self + l_prev * c_prev, l_ref.shape)
+    o_ref[...] = o_self * c_self + o_prev * c_prev
+
+
+def sink_kernel(flags, q_ref, kk_ref, vk_ref, swap_ref, cq, sq, ck, sk, m_ref, l_ref, o_ref, out_ref):
+    swap = swap_ref[...]
+    q = rotate_ref(q_ref, cq, sq, swap)
+    m_sink, l_sink, o_sink = attend_ref(q, rotate_ref(kk_ref, ck, sk, swap), vk_ref)
+    sink_used = flags[1] != 0
+    m_near = m_ref[:, :1]
+    top = jnp.maximum(m_near, jnp.where(sink_used, m_sink, m_near))
+    c_near = jnp.exp(m_near - top)
     c_sink = jnp.where(sink_used, jnp.exp(m_sink - top), 0.0)
-    numer = o_self * c_self + o_prev * c_prev + o_sink * c_sink
-    denom = l_self * c_self + l_prev * c_prev + l_sink * c_sink
+    numer = o_ref[...] * c_near + o_sink * c_sink
+    denom = l_ref[:, :1] * c_near + l_sink * c_sink
     out_ref[...] = (numer / denom).astype(out_ref.dtype)
 
 
-def attention(flags, queries, blocks, tables):
+def specs(count):
+    head = pl.BlockSpec((count, HDIM), lambda h, flags: (0, h))
+    whole = pl.BlockSpec((count, HDIM), lambda h, flags: (0, 0))
+    swap = pl.BlockSpec((HDIM, HDIM), lambda h, flags: (0, 0))
+    return head, whole, swap
+
+
+def swap_matrix():
+    lane = jnp.arange(HDIM)
+    return (lane[:, None] == (lane[None, :] ^ 1)).astype(jnp.bfloat16)
+
+
+def near_attention(flags, queries, blocks, tables):
     count, width = queries.shape
     heads_here = width // HDIM
-    lane = jnp.arange(HDIM)
-    swap = (lane[:, None] == (lane[None, :] ^ 1)).astype(jnp.bfloat16)
-    head_spec = pl.BlockSpec((count, HDIM), lambda h, flags: (0, h))
-    whole_spec = pl.BlockSpec((count, HDIM), lambda h, flags: (0, 0))
-    swap_spec = pl.BlockSpec((HDIM, HDIM), lambda h, flags: (0, 0))
+    head, whole, swap = specs(count)
     grid_spec = pltpu.PrefetchScalarGridSpec(
         num_scalar_prefetch=1,
         grid=(heads_here,),
-        in_specs=[head_spec] * 7 + [swap_spec] + [whole_spec] * 6,
-        out_specs=head_spec,
-    )
-    flops = heads_here * 3 * 4 * count * count * HDIM
+        in_specs=[head] * 5 + [swap] + [whole] * 4,
+        out_specs=[head] * 3,
+    )
     cost = pl.CostEstimate(
-        flops=flops,
-        transcendentals=heads_here * 3 * count * count,
-        bytes_accessed=8 * count * width * 2 + 6 * count * HDIM * 4,
-    )
+        flops=heads_here * 2 * 4 * count * count * HDIM,
+        transcendentals=heads_here * 2 * count * count,
+        bytes_accessed=5 * count * width * 2 + 3 * count * width * 4,
+    )
+    f32 = jax.ShapeDtypeStruct((count, width), jnp.float32)
     return pl.pallas_call(
-        attention_kernel,
+        near_kernel, grid_spec=grid_spec, out_shape=[f32] * 3, cost_estimate=cost
+    )(flags, queries, *blocks, swap_matrix(), *tables)
+
+
+def sink_attention(flags, queries, blocks, tables, near):
+    count, width = queries.shape
+    heads_here = width // HDIM
+    head, whole, swap = specs(count)
+    grid_spec = pltpu.PrefetchScalarGridSpec(
+        num_scalar_prefetch=1,
+        grid=(heads_here,),
+        in_specs=[head] * 3 + [swap] + [whole] * 4 + [head] * 3,
+        out_specs=head,
+    )
+    cost = pl.CostEstimate(
+        flops=heads_here * 4 * count * count * HDIM,
+        transcendentals=heads_here * count * count,
+        bytes_accessed=4 * count * width * 2 + 3 * count * width * 4,
+    )
+    return pl.pallas_call(
+        sink_kernel,
         grid_spec=grid_spec,
         out_shape=jax.ShapeDtypeStruct((count, width), jnp.bfloat16),
         cost_estimate=cost,
-    )(flags, queries, *blocks, swap, *tables)
+    )(flags, queries, *blocks, swap_matrix(), *tables, *near)
 
 
 def shards(queries, keys, values, out_weight, sink_owner, frame_pos):
@@ -202,20 +238,19 @@
     place = frame_index()
     n_frame = lax.axis_size(FRAME_AXES)
     sink = sink_owner[0] % (n_frame // 2)
-    sink_kv = sink_broadcast(jnp.concatenate([keys, values], axis=0), sink)
     prev_k, prev_v = shifted((keys, values), FRAME_AXES, 1)
+    payload, prev_k, prev_v = lax.optimization_barrier((jnp.concatenate([keys, values], axis=0), prev_k, prev_v))
+    sink_kv = sink_broadcast(payload, sink)
     own_pos = jnp.broadcast_to(frame_pos[:1, None], (n_frame, 128))
     positions = lax.all_to_all(own_pos, FRAME_AXES, 0, 0, tiled=True)[:, 0]
     prev_used = (place >= 1) & (place - 1 != sink)
     sink_used = sink < place
     flags = jnp.stack([prev_used, sink_used]).astype(jnp.int32)
-    tables = (
-        rope_tables(frame_pos[0], count)
-        + rope_tables(positions[jnp.maximum(place - 1, 0)], count)
-        + rope_tables(positions[sink], count)
-    )
-    blocks = (keys, values, prev_k, prev_v, sink_kv[:count], sink_kv[count:])
-    attended = attention(flags, queries, blocks, tables)
+    own_tables = rope_tables(frame_pos[0], count)
+    prev_tables = rope_tables(positions[jnp.maximum(place - 1, 0)], count)
+    sink_tables = rope_tables(positions[sink], count)
+    near = near_attention(flags, queries, (keys, values, prev_k, prev_v), own_tables + prev_tables)
+    attended = sink_attention(flags, queries, (sink_kv[:count], sink_kv[count:]), own_tables + sink_tables, near)
     terms = jnp.dot(attended, out_weight, preferred_element_type=jnp.float32)
     mixed = lax.psum_scatter(terms.astype(jnp.bfloat16), HEAD_AXES, scatter_dimension=1, tiled=True)
     return mixed

time: 383 us -> 371 us (0.969)
  waiting for transfers between devices: 246 us -> 214 us
  Pallas kernels: 41.4 us -> 62.3 us
    all_to_all x1, waiting for transfers between devices: 23.1 us -> 0.01 us  [sink_broadcast(): return lax.all_to_all(copies, FRAME_AXES, 0, 0, tiled=True)]
    pallas_call x1 -> x2, Pallas kernels: 41.4 us -> 62.3 us  [the longest x1 31.9 us: sink_attention(): pl.pallas_call(sink_kernel, grid_spec=grid_spec, out_shape=jax.ShapeDtype...]
    reduce_scatter x1, waiting for transfers between devices: 92.8 us -> 82.4 us  [shards(): lax.psum_scatter(terms.astype(jnp.bfloat16), HEAD_AXES, scatter_dimension...]
  transfers between devices with their start and end apart: 6 -> 6, of which waited for: 6 -> 5; matrix products, arithmetic and copies ran while one was open for 6% -> 5% of each run, Pallas kernels for 0% -> 8%
where the time goes in v2:
time: 371 us
  waiting for transfers between devices  214 us (58%)
  Pallas kernels  62.3 us (17%)
  starting transfers between devices  35.1 us (9%)
  local copies, waits for them, and re-layouts  18.9 us (5%)
  matrix products  17.4 us (5%)
  between operations  15.7 us (4%)
  other arithmetic  7.83 us (2%)
    reduce_scatter x1, waiting for transfers between devices, shards(): lax.psum_scatter(terms.astype(jnp.bfloat16), HEAD_AXES, scatter_dimension...  82.4 us
    ppermute x2, waiting for transfers between devices, shifted(): return lax.ppermute(array, axis, pairs)  76.3 us
    all_to_all x1, waiting for transfers between devices, sink_broadcast(): spread = lax.all_to_all(data, FRAME_AXES, 0, 0, tiled=True)  47.1 us
    pallas_call x1, Pallas kernels, sink_attention(): pl.pallas_call(sink_kernel, grid_spec=grid_spec, out_shape=jax.ShapeDtype...  31.9 us
    pallas_call x1, Pallas kernels, near_attention(): pl.pallas_call(near_kernel, grid_spec=grid_spec, out_shape=[f32] * 3, cos...  30.5 us
    dot_general x1, matrix products, shards(): terms = jnp.dot(attended, out_weight, preferred_element_type=jnp.float32)  17.4 us
    all_to_all x1, starting transfers between devices, sink_broadcast(): spread = lax.all_to_all(data, FRAME_AXES, 0, 0, tiled=True)  12.5 us
    all_to_all x1, starting transfers between devices, shards(): positions = lax.all_to_all(own_pos, FRAME_AXES, 0, 0, tiled=True)[:, 0]  10.3 us
  transfers between devices with their start and end apart: 6, of which 5 were waited for; matrix products, arithmetic and copies ran while one was open for 5% of the time, Pallas kernels for 8%

profile of v2, /device:TPU:1, one launch (start us, length us, event | category | flops | bytes accessed | tf_op | source)
XLA Modules:
  0.0 370.9 jit_solution(16841892154728659750)
XLA Ops:
  6.5 4.1 %collective-permute-start = (bf16[768,1280]{1,0:T(8,128)(2,1)}, bf16[768,1280]{1,0:T(8,128)(2,1)S(1)}, u32[]{:S(2)}, u32[]{:S(2)}) collective-permute-start(bf16[768,1280]{1,0:T(8,128)(2,1)} %ks_ref.1), channel_id=1, source_target_pairs={{0,4},{4,8},{8,12},{12,16},{16,20},{20,24},{24,28},{28,32},{32,36}... | collective-permute-start | bytes 5898248 | tf_op jit(solution)/shard_map/ppermute | solution.py:15
  10.7 3.2 collective-permute-start.1
  13.9 4.3 %pad_maximum_fusion = bf16[1536,1280]{1,0:T(8,128)(2,1)} fusion(bf16[768,1280]{1,0:T(8,128)(2,1)} %vs_ref.1, bf16[768,1280]{1,0:T(8,128)(2,1)} %ks_ref.1), kind=kLoop, calls=%fused_computation.1 | loop fusion | flops 7864320 | bytes 7864320 | tf_op jit(solution)/shard_map/concatenate | solution.py:242
  18.2 34.2 %collective-permute-done.kp_ref = bf16[768,1280]{1,0:T(8,128)(2,1)S(1)} collective-permute-done((bf16[768,1280]{1,0:T(8,128)(2,1)}, bf16[768,1280]{1,0:T(8,128)(2,1)S(1)}, u32[]{:S(2)}, u32[]{:S(2)}) %collective-permute-start) | collective-permute-done | bytes 1966112 | tf_op jit(solution)/shard_map/ppermute | solution.py:15
  52.4 42.1 %collective-permute-done.1.vp_ref = bf16[768,1280]{1,0:T(8,128)(2,1)S(1)} collective-permute-done((bf16[768,1280]{1,0:T(8,128)(2,1)}, bf16[768,1280]{1,0:T(8,128)(2,1)S(1)}, u32[]{:S(2)}, u32[]{:S(2)}) %collective-permute-start.1) | collective-permute-done | bytes 1966112 | tf_op jit(solution)/shard_map/ppermute | solution.py:15
  94.5 0.0 copy-done.1
  94.5 1.3 copy-done.2
  95.8 12.5 %all-to-all-start = ((bf16[32,48,1280]{2,1,0:T(8,128)(2,1)}), bf16[32,48,1280]{2,1,0:T(8,128)(2,1)}, u32[]{:S(2)}, u32[]{:S(2)}) async-start(bf16[32,48,1280]{2,1,0:T(8,128)(2,1)} %bitcast.29), calls=%async_computation | async-start | bytes 7864320 | tf_op jit(solution)/shard_map/all_to_all | solution.py:121
  109.1 47.1 %all-to-all-done = bf16[32,48,1280]{2,1,0:T(8,128)(2,1)} async-done(((bf16[32,48,1280]{2,1,0:T(8,128)(2,1)}), bf16[32,48,1280]{2,1,0:T(8,128)(2,1)}, u32[]{:S(2)}, u32[]{:S(2)}) %all-to-all-start) | async-done | bytes 3932192 | tf_op jit(solution)/shard_map/all_to_all | solution.py:121
  156.2 0.6 broadcast_in_dim.127
  156.8 10.3 %all-to-all-start.2 = ((s32[32,1,128]{2,1,0:T(1,128)}), s32[32,1,128]{2,1,0:T(1,128)S(1)}, u32[]{:S(2)}, u32[]{:S(2)}) async-start(s32[32,1,128]{2,1,0:T(1,128)} %broadcast_in_dim.127), calls=%async_computation.2 | async-start | bytes 32768 | tf_op jit(solution)/shard_map/all_to_all | solution.py:245
  167.1 0.9 constant_dynamic-slice_fusion.2
  168.1 7.7 %all-to-all-done.2 = s32[32,1,128]{2,1,0:T(1,128)S(1)} async-done(((s32[32,1,128]{2,1,0:T(1,128)}), s32[32,1,128]{2,1,0:T(1,128)S(1)}, u32[]{:S(2)}, u32[]{:S(2)}) %all-to-all-start.2) | async-done | bytes 16416 | tf_op jit(solution)/shard_map/all_to_all | solution.py:245
  175.8 2.1 broadcast_in_dim.121
  177.9 4.9 %all-to-all-start.1 = ((bf16[32,48,1280]{2,1,0:T(8,128)(2,1)}), bf16[32,48,1280]{2,1,0:T(8,128)(2,1)}, u32[]{:S(2)}, u32[]{:S(2)}) async-start(bf16[32,48,1280]{2,1,0:T(8,128)(2,1)} %broadcast_in_dim.121), calls=%async_computation.1 | async-start | bytes 7864320 | tf_op jit(solution)/shard_map/all_to_all | solution.py:124
  182.8 0.0 reduce-scatter.2.cloned.1.call-start
  182.9 0.6 add_convert_fusion.flags
  183.5 0.6 fusion.9.swap_ref
  184.1 0.6 constant_dynamic-slice_fusion
  186.0 2.2 fusion.10
  188.2 0.1 pad_maximum_fusion.5
  188.3 0.3 copy.19
  188.6 0.3 reshape.1060
  188.8 0.9 copy.23.cp
  189.8 0.3 copy.20
  190.1 0.3 reshape.1061
  190.4 0.9 copy.24.sp
  191.3 0.1 pad_maximum_fusion.1
  191.3 0.3 copy.15
  191.7 0.3 reshape.1056
  191.9 0.9 copy.25.cq
  192.9 0.3 copy.16
  193.2 0.3 reshape.1057
  193.4 1.0 copy.26.sq
  194.4 0.1 pad_maximum_fusion.3
  194.5 0.3 copy.17
  194.8 0.3 reshape.1058
  195.1 0.9 copy.27.ck
  196.0 0.3 copy.18
  196.3 0.3 reshape.1059
  196.6 0.9 copy.28.sk
  197.5 30.5 %shard_map.64 = (f32[768,1280]{1,0:T(8,128)}, f32[768,1280]{1,0:T(8,128)}, f32[768,1280]{1,0:T(8,128)}) custom-call(s32[2]{0:T(128)} %add_convert_fusion.flags, bf16[768,1280]{1,0:T(8,128)(2,1)} %q_ref.3, bf16[768,1280]{1,0:T(8,128)(2,1)} %ks_ref.1, bf16[768,1280]{1,0:T(8,128)(2,1)} %vs_ref.1, bf16[768,1280]{1,0:T(8,128)(2,1)} %copy-done.1, ...), custom_call_target="tpu_custom_call" | custom-call | flops 6039797760 | bytes 21626880 | tf_op jit(solution)/shard_map/pallas_call | solution.py:208
  227.9 0.0 all-to-all-done.1
  227.9 4.3 %fusion.22 = (bf16[16,48,1280]{2,1,0:T(8,128)(2,1)}, bf16[16,48,1280]{2,1,0:T(8,128)(2,1)}) fusion(bf16[32,48,1280]{2,1,0:T(8,128)(2,1)} %all-to-all-done.1), kind=kLoop, calls=%fused_computation.46 | loop fusion | bytes 7864320 | tf_op jit(solution)/shard_map/slice | solution.py:253
  232.3 31.9 %shard_map.65 = bf16[768,1280]{1,0:T(8,128)(2,1)} custom-call(s32[2]{0:T(128)} %add_convert_fusion.flags, bf16[768,1280]{1,0:T(8,128)(2,1)} %q_ref.3, bf16[768,1280]{1,0:T(8,128)(2,1)} %bitcast.31, bf16[768,1280]{1,0:T(8,128)(2,1)} %bitcast.30, bf16[128,128]{1,0:T(8,128)(2,1)} %fusion.9.swap_ref, f32[768,128]{1,0:T(8,128)} %copy.25.cq, f32[768,128]{1,0:T(8,128)} %copy.26.sq, ...), custom_call_target="tpu_custom_call" | custom-call | flops 3019898880 | bytes 19660800 | tf_op jit(solution)/shard_map/pallas_call | solution.py:228
  264.1 17.4 %convolution_convert_fusion = bf16[768,5120]{1,0:T(8,128)(2,1)} fusion(bf16[768,1280]{1,0:T(8,128)(2,1)} %shard_map.65, bf16[1280,5120]{1,0:T(8,128)(2,1)} %param.9), kind=kOutput, calls=%fused_computation | convolution fusion | flops 10070261760 | bytes 22937600 | tf_op jit(solution)/shard_map/dot_general | solution.py:254
  281.5 0.0 reduce-scatter.2.cloned.1.call-update
  281.6 82.4 %reduce-scatter.2.cloned.1.call-done = bf16[768,1280]{1,0:T(8,128)(2,1)} async-done(((bf16[768,5120]{1,0:T(8,128)(2,1)}), bf16[768,1280]{1,0:T(8,128)(2,1)}) %reduce-scatter.2.cloned.1.call-update) | async-done | bytes 1966096 | tf_op jit(solution)/shard_map/reduce_scatter | solution.py:255
  (10 shorter events, 0.0 us)
Async XLA Ops:
  6.5 45.8 %collective-permute-start = (bf16[768,1280]{1,0:T(8,128)(2,1)}, bf16[768,1280]{1,0:T(8,128)(2,1)S(1)}, u32[]{:S(2)}, u32[]{:S(2)}) collective-permute-start(bf16[768,1280]{1,0:T(8,128)(2,1)} %ks_ref.1), channel_id=1, source_target_pairs={{0,4},{4,8},{8,12},{12,16},{16,20},{20,24},{24,28},{28,32},{32,36}... | collective-permute-start | bytes 5898248 | tf_op jit(solution)/shard_map/ppermute | solution.py:15
  10.7 83.8 %collective-permute-start.1 = (bf16[768,1280]{1,0:T(8,128)(2,1)}, bf16[768,1280]{1,0:T(8,128)(2,1)S(1)}, u32[]{:S(2)}, u32[]{:S(2)}) collective-permute-start(bf16[768,1280]{1,0:T(8,128)(2,1)} %vs_ref.1), channel_id=1, source_target_pairs={{0,4},{4,8},{8,12},{12,16},{16,20},{20,24},{24,28},{28,32},{32,36}... | collective-permute-start | bytes 5898248 | tf_op jit(solution)/shard_map/ppermute | solution.py:15
  52.4 42.1 %copy-start.1 = (bf16[768,1280]{1,0:T(8,128)(2,1)}, bf16[768,1280]{1,0:T(8,128)(2,1)S(1)}, u32[]{:S(2)}) copy-start(bf16[768,1280]{1,0:T(8,128)(2,1)S(1)} %collective-permute-done.kp_ref) | copy-start | bytes 5898244
  94.5 1.3 copy-start.2
  95.8 12.6 %copy-start = (s32[32]{0:T(128)S(1)}, s32[32]{0:T(128)}, u32[]{:S(2)}) copy-start(s32[32]{0:T(128)} %param.10) | copy-start | bytes 388
  95.8 60.4 %all-to-all-start = ((bf16[32,48,1280]{2,1,0:T(8,128)(2,1)}), bf16[32,48,1280]{2,1,0:T(8,128)(2,1)}, u32[]{:S(2)}, u32[]{:S(2)}) async-start(bf16[32,48,1280]{2,1,0:T(8,128)(2,1)} %bitcast.29), calls=%async_computation | async-start | bytes 7864320 | tf_op jit(solution)/shard_map/all_to_all | solution.py:121
  156.8 19.0 %all-to-all-start.2 = ((s32[32,1,128]{2,1,0:T(1,128)}), s32[32,1,128]{2,1,0:T(1,128)S(1)}, u32[]{:S(2)}, u32[]{:S(2)}) async-start(s32[32,1,128]{2,1,0:T(1,128)} %broadcast_in_dim.127), calls=%async_computation.2 | async-start | bytes 32768 | tf_op jit(solution)/shard_map/all_to_all | solution.py:245
  177.9 50.0 %all-to-all-start.1 = ((bf16[32,48,1280]{2,1,0:T(8,128)(2,1)}), bf16[32,48,1280]{2,1,0:T(8,128)(2,1)}, u32[]{:S(2)}, u32[]{:S(2)}) async-start(bf16[32,48,1280]{2,1,0:T(8,128)(2,1)} %broadcast_in_dim.121), calls=%async_computation.1 | async-start | bytes 7864320 | tf_op jit(solution)/shard_map/all_to_all | solution.py:124
  182.8 181.2 %reduce-scatter.2.cloned.1.call-start = ((), (), s32[]{:S(2)}) async-start(), calls=%async_computation.4 | async-start | bytes 9830400 | tf_op jit(solution)/shard_map/reduce_scatter | solution.py:255
Sparse Core Ops, SparseCore 0:
  281.7 82.2 reduce-scatter.1

commit v3 on v2

--- a/solution.py
+++ b/solution.py
@@ -140,10 +140,11 @@
 
 
 def attend_ref(q, k, v_ref):
-    scale = jnp.sqrt(jnp.float32(HDIM))
-    scores = lax.dot_general(q, k, (((1,), (1,)), ((), ())), preferred_element_type=jnp.float32) / scale
-    peak = jnp.max(scores, axis=-1, keepdims=True)
-    weights = jnp.exp(scores - peak).astype(jnp.bfloat16)
+    scale = 1.0 / jnp.sqrt(jnp.float32(HDIM))
+    raw = lax.dot_general(q, k, (((1,), (1,)), ((), ())), preferred_element_type=jnp.float32)
+    raw_peak = jnp.max(raw, axis=-1, keepdims=True)
+    peak = raw_peak * scale
+    weights = jnp.exp((raw - raw_peak) * scale).astype(jnp.bfloat16)
     total = jnp.sum(weights.astype(jnp.float32), axis=-1, keepdims=True)
     partial_value = jnp.dot(weights, v_ref[...], preferred_element_type=jnp.float32)
     return peak, total, partial_value
@@ -163,10 +164,29 @@
     o_ref[...] = o_self * c_self + o_prev * c_prev
 
 
-def sink_kernel(flags, q_ref, kk_ref, vk_ref, swap_ref, cq, sq, ck, sk, m_ref, l_ref, o_ref, out_ref):
+def rope_kernel(x_ref, swap_ref, cos_ref, sin_ref, out_ref):
+    out_ref[...] = rotate_ref(x_ref, cos_ref, sin_ref, swap_ref[...])
+
+
+def rope(x, tables):
+    count, width = x.shape
+    head = pl.BlockSpec((count, HDIM), lambda h: (0, h))
+    whole = pl.BlockSpec((count, HDIM), lambda h: (0, 0))
+    swap = pl.BlockSpec((HDIM, HDIM), lambda h: (0, 0))
+    return pl.pallas_call(
+        rope_kernel,
+        grid=(width // HDIM,),
+        in_specs=[head, swap, whole, whole],
+        out_specs=head,
+        out_shape=jax.ShapeDtypeStruct((count, width), jnp.bfloat16),
+        cost_estimate=pl.CostEstimate(flops=2 * count * width * HDIM, transcendentals=0, bytes_accessed=4 * count * width),
+    )(x, swap_matrix(), *tables)
+
+
+def sink_kernel(flags, q_ref, kk_ref, vk_ref, swap_ref, cq, sq, m_ref, l_ref, o_ref, out_ref):
     swap = swap_ref[...]
     q = rotate_ref(q_ref, cq, sq, swap)
-    m_sink, l_sink, o_sink = attend_ref(q, rotate_ref(kk_ref, ck, sk, swap), vk_ref)
+    m_sink, l_sink, o_sink = attend_ref(q, kk_ref[...], vk_ref)
     sink_used = flags[1] != 0
     m_near = m_ref[:, :1]
     top = jnp.maximum(m_near, jnp.where(sink_used, m_sink, m_near))
@@ -217,7 +237,7 @@
     grid_spec = pltpu.PrefetchScalarGridSpec(
         num_scalar_prefetch=1,
         grid=(heads_here,),
-        in_specs=[head] * 3 + [swap] + [whole] * 4 + [head] * 3,
+        in_specs=[head] * 3 + [swap] + [whole] * 2 + [head] * 3,
         out_specs=head,
     )
     cost = pl.CostEstimate(
@@ -238,19 +258,17 @@
     place = frame_index()
     n_frame = lax.axis_size(FRAME_AXES)
     sink = sink_owner[0] % (n_frame // 2)
-    prev_k, prev_v = shifted((keys, values), FRAME_AXES, 1)
-    payload, prev_k, prev_v = lax.optimization_barrier((jnp.concatenate([keys, values], axis=0), prev_k, prev_v))
+    prev_k, prev_v, prev_pos = shifted((keys, values, frame_pos), FRAME_AXES, 1)
+    own_tables = rope_tables(frame_pos[0], count)
+    prev_tables = rope_tables(prev_pos[0], count)
+    rot_k = rope(keys, own_tables)
+    payload, prev_k, prev_v = lax.optimization_barrier((jnp.concatenate([rot_k, values], axis=0), prev_k, prev_v))
     sink_kv = sink_broadcast(payload, sink)
-    own_pos = jnp.broadcast_to(frame_pos[:1, None], (n_frame, 128))
-    positions = lax.all_to_all(own_pos, FRAME_AXES, 0, 0, tiled=True)[:, 0]
     prev_used = (place >= 1) & (place - 1 != sink)
     sink_used = sink < place
     flags = jnp.stack([prev_used, sink_used]).astype(jnp.int32)
-    own_tables = rope_tables(frame_pos[0], count)
-    prev_tables = rope_tables(positions[jnp.maximum(place - 1, 0)], count)
-    sink_tables = rope_tables(positions[sink], count)
     near = near_attention(flags, queries, (keys, values, prev_k, prev_v), own_tables + prev_tables)
-    attended = sink_attention(flags, queries, (sink_kv[:count], sink_kv[count:]), own_tables + sink_tables, near)
+    attended = sink_attention(flags, queries, (sink_kv[:count], sink_kv[count:]), own_tables, near)
     terms = jnp.dot(attended, out_weight, preferred_element_type=jnp.float32)
     mixed = lax.psum_scatter(terms.astype(jnp.bfloat16), HEAD_AXES, scatter_dimension=1, tiled=True)
     return mixed

time: 371 us -> 362 us (0.976)
  waiting for transfers between devices: 214 us -> 204 us
  Pallas kernels: 62.3 us -> 69.5 us
  local copies, waits for them, and re-layouts: 18.9 us -> 13.4 us
    ppermute x2 -> x3, waiting for transfers between devices: 76.3 us -> 61.4 us  [shifted(): return lax.ppermute(array, axis, pairs)]
    all_to_all x1, waiting for transfers between devices: 0.01 us -> 14.2 us  [sink_broadcast(): return lax.all_to_all(copies, FRAME_AXES, 0, 0, tiled=True)]
    all_to_all x1 -> x0, starting transfers between devices: 10.3 us -> none  [shards(): positions = lax.all_to_all(own_pos, FRAME_AXES, 0, 0, tiled=True)[:, 0]]
    all_to_all x1 -> x0, waiting for transfers between devices: 7.72 us -> none  [shards(): positions = lax.all_to_all(own_pos, FRAME_AXES, 0, 0, tiled=True)[:, 0]]
    pallas_call x0 -> x1, Pallas kernels: none -> 7.66 us  [rope(): pl.pallas_call(rope_kernel, grid=(width // HDIM,), in_specs=[head, swap,...]
    all_to_all x1, starting transfers between devices: 4.87 us -> 11.1 us  [sink_broadcast(): return lax.all_to_all(copies, FRAME_AXES, 0, 0, tiled=True)]
    ppermute x2 -> x3, starting transfers between devices: 7.35 us -> 11.5 us  [shifted(): return lax.ppermute(array, axis, pairs)]
  transfers between devices with their start and end apart: 6 -> 6, of which waited for: 5 -> 5; matrix products, arithmetic and copies ran while one was open for 5% -> 3% of each run, Pallas kernels for 8% -> 11%
where the time goes in v3:
time: 362 us; the launch traced here: 361 us
  waiting for transfers between devices  204 us (56%)
  Pallas kernels  69.5 us (19%)
  starting transfers between devices  35.5 us (10%)
  matrix products  17.4 us (5%)
  between operations  15 us (4%)
  local copies, waits for them, and re-layouts  13.4 us (4%)
  other arithmetic  6.53 us (2%)
    reduce_scatter x1, waiting for transfers between devices, shards(): lax.psum_scatter(terms.astype(jnp.bfloat16), HEAD_AXES, scatter_dimension...  79.9 us
    ppermute x3, waiting for transfers between devices, shifted(): return lax.ppermute(array, axis, pairs)  61.4 us
    all_to_all x1, waiting for transfers between devices, sink_broadcast(): spread = lax.all_to_all(data, FRAME_AXES, 0, 0, tiled=True)  48.4 us
    pallas_call x1, Pallas kernels, sink_attention(): pl.pallas_call(sink_kernel, grid_spec=grid_spec, out_shape=jax.ShapeDtype...  31.3 us
    pallas_call x1, Pallas kernels, near_attention(): pl.pallas_call(near_kernel, grid_spec=grid_spec, out_shape=[f32] * 3, cos...  30.5 us
    dot_general x1, matrix products, shards(): terms = jnp.dot(attended, out_weight, preferred_element_type=jnp.float32)  17.4 us
    all_to_all x1, waiting for transfers between devices, sink_broadcast(): return lax.all_to_all(copies, FRAME_AXES, 0, 0, tiled=True)  14.2 us
    all_to_all x1, starting transfers between devices, sink_broadcast(): spread = lax.all_to_all(data, FRAME_AXES, 0, 0, tiled=True)  12.6 us
  transfers between devices with their start and end apart: 6, of which 5 were waited for; matrix products, arithmetic and copies ran while one was open for 3% of the time, Pallas kernels for 11%

profile of v3, /device:TPU:1, one launch (start us, length us, event | category | flops | bytes accessed | tf_op | source)
XLA Modules:
  0.0 361.3 jit_solution(3998023183153307822)
XLA Ops:
  6.5 4.6 %collective-permute-start.2 = (s32[1]{0:T(128)}, s32[1]{0:T(128)}, u32[]{:S(2)}, u32[]{:S(2)}) collective-permute-start(s32[1]{0:T(128)} %param.11), channel_id=1, source_target_pairs={{0,4},{4,8},{8,12},{12,16},{16,20},{20,24},{24,28},{28,32},{32,36}... | collective-permute-start | bytes 20 | tf_op jit(solution)/shard_map/ppermute | solution.py:15
  11.1 4.0 %collective-permute-start = (bf16[768,1280]{1,0:T(8,128)(2,1)}, bf16[768,1280]{1,0:T(8,128)(2,1)}, u32[]{:S(2)}, u32[]{:S(2)}) collective-permute-start(bf16[768,1280]{1,0:T(8,128)(2,1)} %ks_ref.1), channel_id=1, source_target_pairs={{0,4},{4,8},{8,12},{12,16},{16,20},{20,24},{24,28},{28,32},{32,36}... | collective-permute-start | bytes 5898248 | tf_op jit(solution)/shard_map/ppermute | solution.py:15
  15.1 2.9 collective-permute-start.1
  18.8 0.6 fusion.6.swap_ref
  19.4 0.0 collective-permute-done.2
  20.0 1.5 fusion.7
  21.5 0.1 pad_maximum_fusion.1
  21.6 0.3 copy.15
  21.9 0.3 reshape.722
  22.2 0.0 copy-start
  22.2 0.9 copy.17.cos_ref.cq
  23.1 0.3 copy.16
  23.4 0.3 reshape.723
  23.7 0.9 copy.18.sin_ref.sq
  24.6 7.7 %shard_map.64 = bf16[768,1280]{1,0:T(8,128)(2,1)} custom-call(bf16[768,1280]{1,0:T(8,128)(2,1)} %ks_ref.1, bf16[128,128]{1,0:T(8,128)(2,1)} %fusion.6.swap_ref, f32[768,128]{1,0:T(8,128)} %copy.17.cos_ref.cq, f32[768,128]{1,0:T(8,128)} %copy.18.sin_ref.sq), custom_call_target="tpu_custom_call" | custom-call | flops 251658240 | bytes 3932160 | tf_op jit(solution)/shard_map/pallas_call | solution.py:176
  32.3 0.0 copy-done
  32.3 3.7 %pad_maximum_fusion = bf16[1536,1280]{1,0:T(8,128)(2,1)} fusion(bf16[768,1280]{1,0:T(8,128)(2,1)S(1)} %copy-done, bf16[768,1280]{1,0:T(8,128)(2,1)} %shard_map.64), kind=kLoop, calls=%fused_computation.1 | loop fusion | flops 7864320 | bytes 7864320 | tf_op jit(solution)/shard_map/concatenate | solution.py:265
  36.0 19.3 %collective-permute-done.kp_ref = bf16[768,1280]{1,0:T(8,128)(2,1)} collective-permute-done((bf16[768,1280]{1,0:T(8,128)(2,1)}, bf16[768,1280]{1,0:T(8,128)(2,1)}, u32[]{:S(2)}, u32[]{:S(2)}) %collective-permute-start) | collective-permute-done | bytes 1966112 | tf_op jit(solution)/shard_map/ppermute | solution.py:15
  55.2 42.1 %collective-permute-done.1.vp_ref = bf16[768,1280]{1,0:T(8,128)(2,1)} collective-permute-done((bf16[768,1280]{1,0:T(8,128)(2,1)}, bf16[768,1280]{1,0:T(8,128)(2,1)}, u32[]{:S(2)}, u32[]{:S(2)}) %collective-permute-start.1) | collective-permute-done | bytes 1966112 | tf_op jit(solution)/shard_map/ppermute | solution.py:15
  97.4 0.0 copy-start.1
  97.4 12.6 %all-to-all-start = ((bf16[32,48,1280]{2,1,0:T(8,128)(2,1)}), bf16[32,48,1280]{2,1,0:T(8,128)(2,1)}, u32[]{:S(2)}, u32[]{:S(2)}) async-start(bf16[32,48,1280]{2,1,0:T(8,128)(2,1)} %bitcast.20), calls=%async_computation | async-start | bytes 7864320 | tf_op jit(solution)/shard_map/all_to_all | solution.py:121
  110.0 0.0 copy-done.1
  110.2 48.4 %all-to-all-done = bf16[32,48,1280]{2,1,0:T(8,128)(2,1)} async-done(((bf16[32,48,1280]{2,1,0:T(8,128)(2,1)}), bf16[32,48,1280]{2,1,0:T(8,128)(2,1)}, u32[]{:S(2)}, u32[]{:S(2)}) %all-to-all-start) | async-done | bytes 3932192 | tf_op jit(solution)/shard_map/all_to_all | solution.py:121
  158.6 0.9 constant_dynamic-slice_fusion
  159.5 2.2 broadcast_in_dim.92
  161.7 11.1 %all-to-all-start.1 = ((bf16[32,48,1280]{2,1,0:T(8,128)(2,1)}), bf16[32,48,1280]{2,1,0:T(8,128)(2,1)}, u32[]{:S(2)}, u32[]{:S(2)}) async-start(bf16[32,48,1280]{2,1,0:T(8,128)(2,1)} %broadcast_in_dim.92), calls=%async_computation.1 | async-start | bytes 7864320 | tf_op jit(solution)/shard_map/all_to_all | solution.py:124
  172.8 0.2 reduce-scatter.2.cloned.1.call-start
  173.1 0.6 add_convert_fusion.flags
  173.6 0.1 pad_maximum_fusion.3
  173.7 0.3 copy.19
  174.0 0.3 reshape.724
  174.3 0.9 copy.23.cp
  175.2 0.3 copy.20
  175.5 0.3 reshape.725
  175.8 0.9 copy.24.sp
  176.7 30.5 %shard_map.65 = (f32[768,1280]{1,0:T(8,128)}, f32[768,1280]{1,0:T(8,128)}, f32[768,1280]{1,0:T(8,128)}) custom-call(s32[2]{0:T(128)} %add_convert_fusion.flags, bf16[768,1280]{1,0:T(8,128)(2,1)} %q_ref.3, bf16[768,1280]{1,0:T(8,128)(2,1)} %ks_ref.1, bf16[768,1280]{1,0:T(8,128)(2,1)} %vs_ref.1, bf16[768,1280]{1,0:T(8,128)(2,1)} %collective-permute-done.kp_ref, ...), custom_call_target="tpu_custom_call" | custom-call | flops 6039797760 | bytes 21626880 | tf_op jit(solution)/shard_map/pallas_call | solution.py:228
  207.2 14.2 %all-to-all-done.1 = bf16[32,48,1280]{2,1,0:T(8,128)(2,1)} async-done(((bf16[32,48,1280]{2,1,0:T(8,128)(2,1)}), bf16[32,48,1280]{2,1,0:T(8,128)(2,1)}, u32[]{:S(2)}, u32[]{:S(2)}) %all-to-all-start.1) | async-done | bytes 3932192 | tf_op jit(solution)/shard_map/all_to_all | solution.py:124
  221.4 4.3 %fusion.18 = (bf16[16,48,1280]{2,1,0:T(8,128)(2,1)}, bf16[16,48,1280]{2,1,0:T(8,128)(2,1)}) fusion(bf16[32,48,1280]{2,1,0:T(8,128)(2,1)} %all-to-all-done.1), kind=kLoop, calls=%fused_computation.37 | loop fusion | bytes 7864320 | tf_op jit(solution)/shard_map/slice | solution.py:271
  225.7 31.3 %shard_map.66 = bf16[768,1280]{1,0:T(8,128)(2,1)} custom-call(s32[2]{0:T(128)} %add_convert_fusion.flags, bf16[768,1280]{1,0:T(8,128)(2,1)} %q_ref.3, bf16[768,1280]{1,0:T(8,128)(2,1)} %bitcast.22, bf16[768,1280]{1,0:T(8,128)(2,1)} %bitcast.21, bf16[128,128]{1,0:T(8,128)(2,1)} %fusion.6.swap_ref, f32[768,128]{1,0:T(8,128)} %copy.17.cos_ref.cq, ...), custom_call_target="tpu_custom_call" | custom-call | flops 3019898880 | bytes 19660800 | tf_op jit(solution)/shard_map/pallas_call | solution.py:248
  257.1 17.4 %convolution_convert_fusion = bf16[768,5120]{1,0:T(8,128)(2,1)} fusion(bf16[768,1280]{1,0:T(8,128)(2,1)} %shard_map.66, bf16[1280,5120]{1,0:T(8,128)(2,1)} %param.9), kind=kOutput, calls=%fused_computation | convolution fusion | flops 10070261760 | bytes 22937600 | tf_op jit(solution)/shard_map/dot_general | solution.py:272
  274.5 0.0 reduce-scatter.2.cloned.1.call-update
  274.5 79.9 %reduce-scatter.2.cloned.1.call-done = bf16[768,1280]{1,0:T(8,128)(2,1)} async-done(((bf16[768,5120]{1,0:T(8,128)(2,1)}), bf16[768,1280]{1,0:T(8,128)(2,1)}) %reduce-scatter.2.cloned.1.call-update) | async-done | bytes 1966096 | tf_op jit(solution)/shard_map/reduce_scatter | solution.py:273
  (6 shorter events, 0.0 us)
Async XLA Ops:
  6.5 12.9 %collective-permute-start.2 = (s32[1]{0:T(128)}, s32[1]{0:T(128)}, u32[]{:S(2)}, u32[]{:S(2)}) collective-permute-start(s32[1]{0:T(128)} %param.11), channel_id=1, source_target_pairs={{0,4},{4,8},{8,12},{12,16},{16,20},{20,24},{24,28},{28,32},{32,36}... | collective-permute-start | bytes 20 | tf_op jit(solution)/shard_map/ppermute | solution.py:15
  11.1 44.1 %collective-permute-start = (bf16[768,1280]{1,0:T(8,128)(2,1)}, bf16[768,1280]{1,0:T(8,128)(2,1)}, u32[]{:S(2)}, u32[]{:S(2)}) collective-permute-start(bf16[768,1280]{1,0:T(8,128)(2,1)} %ks_ref.1), channel_id=1, source_target_pairs={{0,4},{4,8},{8,12},{12,16},{16,20},{20,24},{24,28},{28,32},{32,36}... | collective-permute-start | bytes 5898248 | tf_op jit(solution)/shard_map/ppermute | solution.py:15
  15.1 82.3 %collective-permute-start.1 = (bf16[768,1280]{1,0:T(8,128)(2,1)}, bf16[768,1280]{1,0:T(8,128)(2,1)}, u32[]{:S(2)}, u32[]{:S(2)}) collective-permute-start(bf16[768,1280]{1,0:T(8,128)(2,1)} %vs_ref.1), channel_id=1, source_target_pairs={{0,4},{4,8},{8,12},{12,16},{16,20},{20,24},{24,28},{28,32},{32,36}... | collective-permute-start | bytes 5898248 | tf_op jit(solution)/shard_map/ppermute | solution.py:15
  22.2 10.1 %copy-start = (bf16[768,1280]{1,0:T(8,128)(2,1)S(1)}, bf16[768,1280]{1,0:T(8,128)(2,1)}, u32[]{:S(2)}) copy-start(bf16[768,1280]{1,0:T(8,128)(2,1)} %vs_ref.1) | copy-start | bytes 5898244
  97.4 12.7 %copy-start.1 = (s32[32]{0:T(128)S(1)}, s32[32]{0:T(128)}, u32[]{:S(2)}) copy-start(s32[32]{0:T(128)} %param.10) | copy-start | bytes 388
  97.4 61.2 %all-to-all-start = ((bf16[32,48,1280]{2,1,0:T(8,128)(2,1)}), bf16[32,48,1280]{2,1,0:T(8,128)(2,1)}, u32[]{:S(2)}, u32[]{:S(2)}) async-start(bf16[32,48,1280]{2,1,0:T(8,128)(2,1)} %bitcast.20), calls=%async_computation | async-start | bytes 7864320 | tf_op jit(solution)/shard_map/all_to_all | solution.py:121
  161.7 59.8 %all-to-all-start.1 = ((bf16[32,48,1280]{2,1,0:T(8,128)(2,1)}), bf16[32,48,1280]{2,1,0:T(8,128)(2,1)}, u32[]{:S(2)}, u32[]{:S(2)}) async-start(bf16[32,48,1280]{2,1,0:T(8,128)(2,1)} %broadcast_in_dim.92), calls=%async_computation.1 | async-start | bytes 7864320 | tf_op jit(solution)/shard_map/all_to_all | solution.py:124
  172.8 181.6 %reduce-scatter.2.cloned.1.call-start = ((), (), s32[]{:S(2)}) async-start(), calls=%async_computation.3 | async-start | bytes 9830400 | tf_op jit(solution)/shard_map/reduce_scatter | solution.py:273
Sparse Core Ops, SparseCore 0:
  274.6 79.7 reduce-scatter.1

commit v4 on v3

--- a/solution.py
+++ b/solution.py
@@ -230,25 +230,29 @@
     )(flags, queries, *blocks, swap_matrix(), *tables)
 
 
-def sink_attention(flags, queries, blocks, tables, near):
+def sink_attention(flags, queries, blocks, tables, near, half, halves):
     count, width = queries.shape
     heads_here = width // HDIM
-    head, whole, swap = specs(count)
+    rows = count // halves
+    part = pl.BlockSpec((rows, HDIM), lambda h, flags: (half, h))
+    part_table = pl.BlockSpec((rows, HDIM), lambda h, flags: (half, 0))
+    head = pl.BlockSpec((count, HDIM), lambda h, flags: (0, h))
+    swap = pl.BlockSpec((HDIM, HDIM), lambda h, flags: (0, 0))
     grid_spec = pltpu.PrefetchScalarGridSpec(
         num_scalar_prefetch=1,
         grid=(heads_here,),
-        in_specs=[head] * 3 + [swap] + [whole] * 2 + [head] * 3,
-        out_specs=head,
+        in_specs=[part] + [head] * 2 + [swap] + [part_table] * 2 + [part] * 3,
+        out_specs=pl.BlockSpec((rows, HDIM), lambda h, flags: (0, h)),
     )
     cost = pl.CostEstimate(
-        flops=heads_here * 4 * count * count * HDIM,
-        transcendentals=heads_here * count * count,
-        bytes_accessed=4 * count * width * 2 + 3 * count * width * 4,
+        flops=heads_here * 4 * rows * count * HDIM,
+        transcendentals=heads_here * rows * count,
+        bytes_accessed=(rows + 2 * count) * width * 2 + 3 * rows * width * 4,
     )
     return pl.pallas_call(
         sink_kernel,
         grid_spec=grid_spec,
-        out_shape=jax.ShapeDtypeStruct((count, width), jnp.bfloat16),
+        out_shape=jax.ShapeDtypeStruct((rows, width), jnp.bfloat16),
         cost_estimate=cost,
     )(flags, queries, *blocks, swap_matrix(), *tables, *near)
 
@@ -268,9 +272,13 @@
     sink_used = sink < place
     flags = jnp.stack([prev_used, sink_used]).astype(jnp.int32)
     near = near_attention(flags, queries, (keys, values, prev_k, prev_v), own_tables + prev_tables)
-    attended = sink_attention(flags, queries, (sink_kv[:count], sink_kv[count:]), own_tables, near)
-    terms = jnp.dot(attended, out_weight, preferred_element_type=jnp.float32)
-    mixed = lax.psum_scatter(terms.astype(jnp.bfloat16), HEAD_AXES, scatter_dimension=1, tiled=True)
+    halves = 2
+    outs = []
+    for half in range(halves):
+        attended = sink_attention(flags, queries, (sink_kv[:count], sink_kv[count:]), own_tables, near, half, halves)
+        terms = jnp.dot(attended, out_weight, preferred_element_type=jnp.float32)
+        outs.append(lax.psum_scatter(terms.astype(jnp.bfloat16), HEAD_AXES, scatter_dimension=1, tiled=True))
+    mixed = jnp.concatenate(outs, axis=0)
     return mixed
 
 

time: 362 us -> 359 us (level)
  waiting for transfers between devices: 204 us -> 190 us
  Pallas kernels: 69.5 us -> 74.6 us
    reduce_scatter x1 -> x2, waiting for transfers between devices: 79.9 us -> 66.2 us  [shards(): lax.psum_scatter(terms.astype(jnp.bfloat16), HEAD_AXES, scatter_dimension...]
    pallas_call x1 -> x2, Pallas kernels: 31.3 us -> 36.4 us  [sink_attention(): pl.pallas_call(sink_kernel, grid_spec=grid_spec, out_shape=jax.ShapeDtype...]
    dot_general x1 -> x2, matrix products: 17.4 us -> 19.7 us  [shards(): terms = jnp.dot(attended, out_weight, preferred_element_type=jnp.float32)]
  transfers between devices with their start and end apart: 6 -> 7, of which waited for: 5 -> 6; matrix products, arithmetic and copies ran while one was open for 3% -> 6% of each run, Pallas kernels for 11% -> 16%
where the time goes in v4:
time: 359 us; the launch traced here: 358 us
  waiting for transfers between devices  190 us (53%)
  Pallas kernels  74.6 us (21%)
  starting transfers between devices  35.5 us (10%)
  matrix products  19.7 us (5%)
  between operations  15 us (4%)
  local copies, waits for them, and re-layouts  13.4 us (4%)
  other arithmetic  9.42 us (3%)
    reduce_scatter x2, waiting for transfers between devices, shards(): lax.psum_scatter(terms.astype(jnp.bfloat16), HEAD_AXES, scatter_dimension...  66.2 us
    ppermute x3, waiting for transfers between devices, shifted(): return lax.ppermute(array, axis, pairs)  61.4 us
    all_to_all x1, waiting for transfers between devices, sink_broadcast(): spread = lax.all_to_all(data, FRAME_AXES, 0, 0, tiled=True)  48.4 us
    pallas_call x2, Pallas kernels, sink_attention(): pl.pallas_call(sink_kernel, grid_spec=grid_spec, out_shape=jax.ShapeDtype...  36.4 us
    pallas_call x1, Pallas kernels, near_attention(): pl.pallas_call(near_kernel, grid_spec=grid_spec, out_shape=[f32] * 3, cos...  30.5 us
    dot_general x2, matrix products, shards(): terms = jnp.dot(attended, out_weight, preferred_element_type=jnp.float32)  19.7 us
    all_to_all x1, waiting for transfers between devices, sink_broadcast(): return lax.all_to_all(copies, FRAME_AXES, 0, 0, tiled=True)  14.2 us
    all_to_all x1, starting transfers between devices, sink_broadcast(): spread = lax.all_to_all(data, FRAME_AXES, 0, 0, tiled=True)  12.6 us
  transfers between devices with their start and end apart: 7, of which 6 were waited for; matrix products, arithmetic and copies ran while one was open for 6% of the time, Pallas kernels for 16%

profile of v4, /device:TPU:1, one launch (start us, length us, event | category | flops | bytes accessed | tf_op | source)
XLA Modules:
  0.0 357.9 jit_solution(15411943357890975897)
XLA Ops:
  6.5 4.6 %collective-permute-start.2 = (s32[1]{0:T(128)}, s32[1]{0:T(128)}, u32[]{:S(2)}, u32[]{:S(2)}) collective-permute-start(s32[1]{0:T(128)} %param.11), channel_id=1, source_target_pairs={{0,4},{4,8},{8,12},{12,16},{16,20},{20,24},{24,28},{28,32},{32,36}... | collective-permute-start | bytes 20 | tf_op jit(solution)/shard_map/ppermute | solution.py:15
  11.1 4.0 %collective-permute-start = (bf16[768,1280]{1,0:T(8,128)(2,1)}, bf16[768,1280]{1,0:T(8,128)(2,1)}, u32[]{:S(2)}, u32[]{:S(2)}) collective-permute-start(bf16[768,1280]{1,0:T(8,128)(2,1)} %ks_ref.1), channel_id=1, source_target_pairs={{0,4},{4,8},{8,12},{12,16},{16,20},{20,24},{24,28},{28,32},{32,36}... | collective-permute-start | bytes 5898248 | tf_op jit(solution)/shard_map/ppermute | solution.py:15
  15.1 2.9 collective-permute-start.1
  18.8 0.6 fusion.6.swap_ref
  19.4 0.0 collective-permute-done.2
  20.0 1.5 fusion.7
  21.5 0.1 pad_maximum_fusion.2
  21.6 0.3 copy.17
  21.9 0.3 reshape.722
  22.2 0.0 copy-start
  22.2 0.9 copy.19.cos_ref.cq
  23.1 0.3 copy.18
  23.4 0.3 reshape.723
  23.7 0.9 copy.20.sin_ref.sq
  24.6 7.6 %shard_map.64 = bf16[768,1280]{1,0:T(8,128)(2,1)} custom-call(bf16[768,1280]{1,0:T(8,128)(2,1)} %ks_ref.1, bf16[128,128]{1,0:T(8,128)(2,1)} %fusion.6.swap_ref, f32[768,128]{1,0:T(8,128)} %copy.19.cos_ref.cq, f32[768,128]{1,0:T(8,128)} %copy.20.sin_ref.sq), custom_call_target="tpu_custom_call" | custom-call | flops 251658240 | bytes 3932160 | tf_op jit(solution)/shard_map/pallas_call | solution.py:176
  32.3 0.0 copy-done
  32.3 3.7 %pad_maximum_fusion = bf16[1536,1280]{1,0:T(8,128)(2,1)} fusion(bf16[768,1280]{1,0:T(8,128)(2,1)S(1)} %copy-done, bf16[768,1280]{1,0:T(8,128)(2,1)} %shard_map.64), kind=kLoop, calls=%fused_computation.2 | loop fusion | flops 7864320 | bytes 7864320 | tf_op jit(solution)/shard_map/concatenate | solution.py:269
  35.9 19.3 %collective-permute-done.kp_ref = bf16[768,1280]{1,0:T(8,128)(2,1)} collective-permute-done((bf16[768,1280]{1,0:T(8,128)(2,1)}, bf16[768,1280]{1,0:T(8,128)(2,1)}, u32[]{:S(2)}, u32[]{:S(2)}) %collective-permute-start) | collective-permute-done | bytes 1966112 | tf_op jit(solution)/shard_map/ppermute | solution.py:15
  55.2 42.1 %collective-permute-done.1.vp_ref = bf16[768,1280]{1,0:T(8,128)(2,1)} collective-permute-done((bf16[768,1280]{1,0:T(8,128)(2,1)}, bf16[768,1280]{1,0:T(8,128)(2,1)}, u32[]{:S(2)}, u32[]{:S(2)}) %collective-permute-start.1) | collective-permute-done | bytes 1966112 | tf_op jit(solution)/shard_map/ppermute | solution.py:15
  97.4 0.0 copy-start.1
  97.4 12.6 %all-to-all-start = ((bf16[32,48,1280]{2,1,0:T(8,128)(2,1)}), bf16[32,48,1280]{2,1,0:T(8,128)(2,1)}, u32[]{:S(2)}, u32[]{:S(2)}) async-start(bf16[32,48,1280]{2,1,0:T(8,128)(2,1)} %bitcast.26), calls=%async_computation | async-start | bytes 7864320 | tf_op jit(solution)/shard_map/all_to_all | solution.py:121
  110.0 0.0 copy-done.1
  110.2 48.4 %all-to-all-done = bf16[32,48,1280]{2,1,0:T(8,128)(2,1)} async-done(((bf16[32,48,1280]{2,1,0:T(8,128)(2,1)}), bf16[32,48,1280]{2,1,0:T(8,128)(2,1)}, u32[]{:S(2)}, u32[]{:S(2)}) %all-to-all-start) | async-done | bytes 3932192 | tf_op jit(solution)/shard_map/all_to_all | solution.py:121
  158.6 0.9 constant_dynamic-slice_fusion
  159.5 2.2 broadcast_in_dim.94
  161.7 11.1 %all-to-all-start.1 = ((bf16[32,48,1280]{2,1,0:T(8,128)(2,1)}), bf16[32,48,1280]{2,1,0:T(8,128)(2,1)}, u32[]{:S(2)}, u32[]{:S(2)}) async-start(bf16[32,48,1280]{2,1,0:T(8,128)(2,1)} %broadcast_in_dim.94), calls=%async_computation.1 | async-start | bytes 7864320 | tf_op jit(solution)/shard_map/all_to_all | solution.py:124
  172.8 0.2 reduce-scatter.3.cloned.1.call-start
  173.1 0.6 add_convert_fusion.flags
  173.6 0.1 pad_maximum_fusion.4
  173.7 0.3 copy.21
  174.0 0.3 reshape.724
  174.3 0.9 copy.25.cp
  175.2 0.3 copy.22
  175.5 0.3 reshape.725
  175.8 0.9 copy.26.sp
  176.7 30.5 %shard_map.65 = (f32[768,1280]{1,0:T(8,128)}, f32[768,1280]{1,0:T(8,128)}, f32[768,1280]{1,0:T(8,128)}) custom-call(s32[2]{0:T(128)} %add_convert_fusion.flags, bf16[768,1280]{1,0:T(8,128)(2,1)} %q_ref.5, bf16[768,1280]{1,0:T(8,128)(2,1)} %ks_ref.1, bf16[768,1280]{1,0:T(8,128)(2,1)} %vs_ref.1, bf16[768,1280]{1,0:T(8,128)(2,1)} %collective-permute-done.kp_ref, ...), custom_call_target="tpu_custom_call" | custom-call | flops 6039797760 | bytes 21626880 | tf_op jit(solution)/shard_map/pallas_call | solution.py:228
  207.2 14.2 %all-to-all-done.1 = bf16[32,48,1280]{2,1,0:T(8,128)(2,1)} async-done(((bf16[32,48,1280]{2,1,0:T(8,128)(2,1)}), bf16[32,48,1280]{2,1,0:T(8,128)(2,1)}, u32[]{:S(2)}, u32[]{:S(2)}) %all-to-all-start.1) | async-done | bytes 3932192 | tf_op jit(solution)/shard_map/all_to_all | solution.py:124
  221.4 4.3 %fusion.18 = (bf16[16,48,1280]{2,1,0:T(8,128)(2,1)}, bf16[16,48,1280]{2,1,0:T(8,128)(2,1)}) fusion(bf16[32,48,1280]{2,1,0:T(8,128)(2,1)} %all-to-all-done.1), kind=kLoop, calls=%fused_computation.39 | loop fusion | bytes 7864320 | tf_op jit(solution)/shard_map/slice | solution.py:278
  225.7 18.2 %shard_map.66 = bf16[384,1280]{1,0:T(8,128)(2,1)} custom-call(s32[2]{0:T(128)} %add_convert_fusion.flags, bf16[768,1280]{1,0:T(8,128)(2,1)} %q_ref.5, bf16[768,1280]{1,0:T(8,128)(2,1)} %bitcast.24, bf16[768,1280]{1,0:T(8,128)(2,1)} %bitcast.22, bf16[128,128]{1,0:T(8,128)(2,1)} %fusion.6.swap_ref, f32[768,128]{1,0:T(8,128)} %copy.19.cos_ref.cq, ...), custom_call_target="tpu_custom_call" | custom-call | flops 1509949440 | bytes 10813440 | tf_op jit(solution)/shard_map/pallas_call | solution.py:252
  243.9 9.8 %convolution_convert_fusion.1 = bf16[384,5120]{1,0:T(8,128)(2,1)} fusion(bf16[384,1280]{1,0:T(8,128)(2,1)} %shard_map.66, bf16[1280,5120]{1,0:T(8,128)(2,1)} %param.9), kind=kOutput, calls=%fused_computation.1 | convolution fusion | flops 5035130880 | bytes 18022400 | tf_op jit(solution)/shard_map/dot_general | solution.py:279
  253.7 0.0 reduce-scatter.3.cloned.1.call-update
  253.8 0.0 reduce-scatter.5.cloned.1.call-start
  253.8 18.2 %shard_map.67 = bf16[384,1280]{1,0:T(8,128)(2,1)} custom-call(s32[2]{0:T(128)} %add_convert_fusion.flags, bf16[768,1280]{1,0:T(8,128)(2,1)} %q_ref.5, bf16[768,1280]{1,0:T(8,128)(2,1)} %bitcast.25, bf16[768,1280]{1,0:T(8,128)(2,1)} %bitcast.23, bf16[128,128]{1,0:T(8,128)(2,1)} %fusion.6.swap_ref, f32[768,128]{1,0:T(8,128)} %copy.19.cos_ref.cq, ...), custom_call_target="tpu_custom_call" | custom-call | flops 1509949440 | bytes 10813440 | tf_op jit(solution)/shard_map/pallas_call | solution.py:252
  272.0 9.9 %convolution_convert_fusion = bf16[384,5120]{1,0:T(8,128)(2,1)} fusion(bf16[384,1280]{1,0:T(8,128)(2,1)} %shard_map.67, bf16[1280,5120]{1,0:T(8,128)(2,1)} %param.9), kind=kOutput, calls=%fused_computation | convolution fusion | flops 5035130880 | bytes 18022400 | tf_op jit(solution)/shard_map/dot_general | solution.py:279
  281.9 0.0 reduce-scatter.5.cloned.1.call-update
  282.0 19.6 %reduce-scatter.3.cloned.1.call-done = bf16[384,1280]{1,0:T(8,128)(2,1)} async-done(((bf16[384,5120]{1,0:T(8,128)(2,1)}), bf16[384,1280]{1,0:T(8,128)(2,1)}) %reduce-scatter.3.cloned.1.call-update) | async-done | bytes 983056 | tf_op jit(solution)/shard_map/reduce_scatter | solution.py:280
  301.5 46.6 %reduce-scatter.5.cloned.1.call-done = bf16[384,1280]{1,0:T(8,128)(2,1)} async-done(((bf16[384,5120]{1,0:T(8,128)(2,1)}), bf16[384,1280]{1,0:T(8,128)(2,1)}) %reduce-scatter.5.cloned.1.call-update) | async-done | bytes 983056 | tf_op jit(solution)/shard_map/reduce_scatter | solution.py:280
  348.1 2.9 pad_maximum_fusion.1
  (6 shorter events, 0.0 us)
Async XLA Ops:
  6.5 12.9 %collective-permute-start.2 = (s32[1]{0:T(128)}, s32[1]{0:T(128)}, u32[]{:S(2)}, u32[]{:S(2)}) collective-permute-start(s32[1]{0:T(128)} %param.11), channel_id=1, source_target_pairs={{0,4},{4,8},{8,12},{12,16},{16,20},{20,24},{24,28},{28,32},{32,36}... | collective-permute-start | bytes 20 | tf_op jit(solution)/shard_map/ppermute | solution.py:15
  11.1 44.1 %collective-permute-start = (bf16[768,1280]{1,0:T(8,128)(2,1)}, bf16[768,1280]{1,0:T(8,128)(2,1)}, u32[]{:S(2)}, u32[]{:S(2)}) collective-permute-start(bf16[768,1280]{1,0:T(8,128)(2,1)} %ks_ref.1), channel_id=1, source_target_pairs={{0,4},{4,8},{8,12},{12,16},{16,20},{20,24},{24,28},{28,32},{32,36}... | collective-permute-start | bytes 5898248 | tf_op jit(solution)/shard_map/ppermute | solution.py:15
  15.1 82.3 %collective-permute-start.1 = (bf16[768,1280]{1,0:T(8,128)(2,1)}, bf16[768,1280]{1,0:T(8,128)(2,1)}, u32[]{:S(2)}, u32[]{:S(2)}) collective-permute-start(bf16[768,1280]{1,0:T(8,128)(2,1)} %vs_ref.1), channel_id=1, source_target_pairs={{0,4},{4,8},{8,12},{12,16},{16,20},{20,24},{24,28},{28,32},{32,36}... | collective-permute-start | bytes 5898248 | tf_op jit(solution)/shard_map/ppermute | solution.py:15
  22.2 10.1 %copy-start = (bf16[768,1280]{1,0:T(8,128)(2,1)S(1)}, bf16[768,1280]{1,0:T(8,128)(2,1)}, u32[]{:S(2)}) copy-start(bf16[768,1280]{1,0:T(8,128)(2,1)} %vs_ref.1) | copy-start | bytes 5898244
  97.4 12.7 %copy-start.1 = (s32[32]{0:T(128)S(1)}, s32[32]{0:T(128)}, u32[]{:S(2)}) copy-start(s32[32]{0:T(128)} %param.10) | copy-start | bytes 388
  97.4 61.2 %all-to-all-start = ((bf16[32,48,1280]{2,1,0:T(8,128)(2,1)}), bf16[32,48,1280]{2,1,0:T(8,128)(2,1)}, u32[]{:S(2)}, u32[]{:S(2)}) async-start(bf16[32,48,1280]{2,1,0:T(8,128)(2,1)} %bitcast.26), calls=%async_computation | async-start | bytes 7864320 | tf_op jit(solution)/shard_map/all_to_all | solution.py:121
  161.7 59.8 %all-to-all-start.1 = ((bf16[32,48,1280]{2,1,0:T(8,128)(2,1)}), bf16[32,48,1280]{2,1,0:T(8,128)(2,1)}, u32[]{:S(2)}, u32[]{:S(2)}) async-start(bf16[32,48,1280]{2,1,0:T(8,128)(2,1)} %broadcast_in_dim.94), calls=%async_computation.1 | async-start | bytes 7864320 | tf_op jit(solution)/shard_map/all_to_all | solution.py:124
  172.8 128.7 %reduce-scatter.3.cloned.1.call-start = ((), (), s32[]{:S(2)}) async-start(), calls=%async_computation.4 | async-start | bytes 4915200 | tf_op jit(solution)/shard_map/reduce_scatter | solution.py:280
  253.8 94.4 %reduce-scatter.5.cloned.1.call-start = ((), (), s32[]{:S(2)}) async-start(), calls=%async_computation.5 | async-start | bytes 4915200 | tf_op jit(solution)/shard_map/reduce_scatter | solution.py:280
Sparse Core Ops, SparseCore 0:
  253.9 47.6 reduce-scatter.2
  303.9 44.1 reduce-scatter.4

commit v5 on v4

--- a/solution.py
+++ b/solution.py
@@ -115,13 +115,17 @@
     return jnp.concatenate([out0, out1], axis=0)
 
 
-def sink_broadcast(data, sink):
+def exchange(data, sink):
     n_frame = lax.axis_size(FRAME_AXES)
     piece = data.shape[0] // n_frame
     spread = lax.all_to_all(data, FRAME_AXES, 0, 0, tiled=True)
+    pieces = spread.reshape((n_frame, piece) + data.shape[1:])
+    before = jnp.concatenate([pieces[-1:], pieces[:-1]], axis=0).reshape(data.shape)
+    prev_full = lax.all_to_all(before, FRAME_AXES, 0, 0, tiled=True)
     mine = lax.dynamic_slice_in_dim(spread, sink * piece, piece, axis=0)
     copies = jnp.broadcast_to(mine[None], (n_frame,) + mine.shape).reshape(data.shape)
-    return lax.all_to_all(copies, FRAME_AXES, 0, 0, tiled=True)
+    copies, prev_full = lax.optimization_barrier((copies, prev_full))
+    return prev_full, lax.all_to_all(copies, FRAME_AXES, 0, 0, tiled=True)
 
 
 def rope_tables(frame_value, count):
@@ -150,11 +154,11 @@
     return peak, total, partial_value
 
 
-def near_kernel(flags, q_ref, ks_ref, vs_ref, kp_ref, vp_ref, swap_ref, cq, sq, cp, sp, m_ref, l_ref, o_ref):
+def near_kernel(flags, q_ref, ks_ref, vs_ref, kp_ref, vp_ref, swap_ref, cq, sq, m_ref, l_ref, o_ref):
     swap = swap_ref[...]
     q = rotate_ref(q_ref, cq, sq, swap)
-    m_self, l_self, o_self = attend_ref(q, rotate_ref(ks_ref, cq, sq, swap), vs_ref)
-    m_prev, l_prev, o_prev = attend_ref(q, rotate_ref(kp_ref, cp, sp, swap), vp_ref)
+    m_self, l_self, o_self = attend_ref(q, ks_ref[...], vs_ref)
+    m_prev, l_prev, o_prev = attend_ref(q, kp_ref[...], vp_ref)
     prev_used = flags[0] != 0
     top = jnp.maximum(m_self, jnp.where(prev_used, m_prev, m_self))
     c_self = jnp.exp(m_self - top)
@@ -216,7 +220,7 @@
     grid_spec = pltpu.PrefetchScalarGridSpec(
         num_scalar_prefetch=1,
         grid=(heads_here,),
-        in_specs=[head] * 5 + [swap] + [whole] * 4,
+        in_specs=[head] * 5 + [swap] + [whole] * 2,
         out_specs=[head] * 3,
     )
     cost = pl.CostEstimate(
@@ -262,16 +266,13 @@
     place = frame_index()
     n_frame = lax.axis_size(FRAME_AXES)
     sink = sink_owner[0] % (n_frame // 2)
-    prev_k, prev_v, prev_pos = shifted((keys, values, frame_pos), FRAME_AXES, 1)
     own_tables = rope_tables(frame_pos[0], count)
-    prev_tables = rope_tables(prev_pos[0], count)
     rot_k = rope(keys, own_tables)
-    payload, prev_k, prev_v = lax.optimization_barrier((jnp.concatenate([rot_k, values], axis=0), prev_k, prev_v))
-    sink_kv = sink_broadcast(payload, sink)
+    prev_kv, sink_kv = exchange(jnp.concatenate([rot_k, values], axis=0), sink)
     prev_used = (place >= 1) & (place - 1 != sink)
     sink_used = sink < place
     flags = jnp.stack([prev_used, sink_used]).astype(jnp.int32)
-    near = near_attention(flags, queries, (keys, values, prev_k, prev_v), own_tables + prev_tables)
+    near = near_attention(flags, queries, (rot_k, values, prev_kv[:count], prev_kv[count:]), own_tables)
     halves = 2
     outs = []
     for half in range(halves):

time: 359 us -> 340 us (0.947)
  waiting for transfers between devices: 190 us -> 131 us
  blocking collectives: 0 us -> 58.9 us
  starting transfers between devices: 35.5 us -> 16.5 us
    ppermute x3 -> x0, waiting for transfers between devices: 61.4 us -> none  [shifted(): return lax.ppermute(array, axis, pairs)]
    all_to_all x0 -> x1, blocking collectives: none -> 58.9 us  [exchange(): spread = lax.all_to_all(data, FRAME_AXES, 0, 0, tiled=True)]
    ppermute x3 -> x0, starting transfers between devices: 11.5 us -> none  [shifted(): return lax.ppermute(array, axis, pairs)]
    all_to_all x2, starting transfers between devices: 23.8 us -> 16.3 us  [the longest x1 9.8 us: exchange(): return (prev_full, lax.all_to_all(copies, FRAME_AXES, 0, 0, tiled=True))]
    slice x0 -> x3, local copies, waits for them, and re-layouts: none -> 4.59 us  [the longest x1 4.33 us: shards(): prev_kv[count:]]
    all_to_all x2, waiting for transfers between devices: 62.7 us -> 66.8 us  [the longest x1 49 us: exchange(): prev_full = lax.all_to_all(before, FRAME_AXES, 0, 0, tiled=True)]
  transfers between devices with their start and end apart: 7 -> 4, of which waited for: 6 -> 4; matrix products, arithmetic and copies ran while one was open for 6% -> 5% of each run, Pallas kernels for 16% -> 14%
where the time goes in v5:
time: 340 us; the launch traced here: 339 us
  waiting for transfers between devices  131 us (39%)
  Pallas kernels  72.1 us (21%)
  blocking collectives  58.9 us (17%)
  matrix products  19.8 us (6%)
  local copies, waits for them, and re-layouts  16.8 us (5%)
  starting transfers between devices  16.5 us (5%)
  between operations  14.3 us (4%)
  other arithmetic  9.12 us (3%)
    reduce_scatter x2, waiting for transfers between devices, shards(): lax.psum_scatter(terms.astype(jnp.bfloat16), HEAD_AXES, scatter_dimension...  64.6 us
    all_to_all x1, blocking collectives, exchange(): spread = lax.all_to_all(data, FRAME_AXES, 0, 0, tiled=True)  58.9 us
    all_to_all x1, waiting for transfers between devices, exchange(): prev_full = lax.all_to_all(before, FRAME_AXES, 0, 0, tiled=True)  49 us
    pallas_call x2, Pallas kernels, sink_attention(): pl.pallas_call(sink_kernel, grid_spec=grid_spec, out_shape=jax.ShapeDtype...  36.5 us
    pallas_call x1, Pallas kernels, near_attention(): pl.pallas_call(near_kernel, grid_spec=grid_spec, out_shape=[f32] * 3, cos...  28 us
    dot_general x2, matrix products, shards(): terms = jnp.dot(attended, out_weight, preferred_element_type=jnp.float32)  19.8 us
    all_to_all x1, waiting for transfers between devices, exchange(): return (prev_full, lax.all_to_all(copies, FRAME_AXES, 0, 0, tiled=True))  17.7 us
    all_to_all x1, starting transfers between devices, exchange(): return (prev_full, lax.all_to_all(copies, FRAME_AXES, 0, 0, tiled=True))  9.8 us
  transfers between devices with their start and end apart: 4, of which 4 were waited for; matrix products, arithmetic and copies ran while one was open for 5% of the time, Pallas kernels for 14%

profile of v5, /device:TPU:1, one launch (start us, length us, event | category | flops | bytes accessed | tf_op | source)
XLA Modules:
  0.0 339.1 jit_solution(13783071581796368823)
XLA Ops:
  7.2 0.6 fusion.2.swap_ref
  7.9 0.8 fusion.3
  8.7 0.1 pad_maximum_fusion.3
  8.7 0.3 copy.15
  9.0 0.3 reshape.406
  9.3 0.0 copy-start.1
  9.3 0.9 copy.17.cos_ref.cq
  10.3 0.3 copy.16
  10.6 0.3 reshape.407
  10.9 0.9 copy.18.sin_ref.sq
  11.8 7.6 %shard_map.64.ks_ref = bf16[768,1280]{1,0:T(8,128)(2,1)} custom-call(bf16[768,1280]{1,0:T(8,128)(2,1)} %x_ref.1, bf16[128,128]{1,0:T(8,128)(2,1)} %fusion.2.swap_ref, f32[768,128]{1,0:T(8,128)} %copy.17.cos_ref.cq, f32[768,128]{1,0:T(8,128)} %copy.18.sin_ref.sq), custom_call_target="tpu_custom_call" | custom-call | flops 251658240 | bytes 3932160 | tf_op jit(solution)/shard_map/pallas_call | solution.py:180
  19.4 0.0 copy-done.1
  19.4 1.8 pad_maximum_fusion
  21.2 58.9 %all_to_all.30 = bf16[32,48,1280]{2,1,0:T(8,128)(2,1)S(1)} all-to-all(bf16[32,48,1280]{2,1,0:T(8,128)(2,1)S(1)} %bitcast.25), channel_id=1, replica_groups=mesh['z'=4,'xh'=2,'y'=4,'xl'=2,'c'=2] {'z','xh','y'}, dimensions={0} | all-to-all | bytes 7864320 | tf_op jit(solution)/shard_map/all_to_all | solution.py:121
  80.2 0.0 copy-start
  80.2 1.9 copy-done
  82.0 0.2 slice.43
  82.3 2.3 pad_maximum_fusion.1
  84.6 0.0 copy-start.2
  84.6 6.5 %all-to-all-start.1 = ((bf16[32,48,1280]{2,1,0:T(8,128)(2,1)}), bf16[32,48,1280]{2,1,0:T(8,128)(2,1)}, u32[]{:S(2)}, u32[]{:S(2)}) async-start(bf16[32,48,1280]{2,1,0:T(8,128)(2,1)} %pad_maximum_fusion.1), calls=%async_computation.1 | async-start | bytes 7864320 | tf_op jit(solution)/shard_map/all_to_all | solution.py:124
  91.1 0.0 copy-done.2
  91.2 0.9 constant_dynamic-slice_fusion
  92.1 49.0 %all-to-all-done.1 = bf16[32,48,1280]{2,1,0:T(8,128)(2,1)} async-done(((bf16[32,48,1280]{2,1,0:T(8,128)(2,1)}), bf16[32,48,1280]{2,1,0:T(8,128)(2,1)}, u32[]{:S(2)}, u32[]{:S(2)}) %all-to-all-start.1) | async-done | bytes 3932192 | tf_op jit(solution)/shard_map/all_to_all | solution.py:124
  141.2 2.1 broadcast_in_dim.64
  143.3 9.8 %all-to-all-start.2 = ((bf16[32,48,1280]{2,1,0:T(8,128)(2,1)}), bf16[32,48,1280]{2,1,0:T(8,128)(2,1)}, u32[]{:S(2)}, u32[]{:S(2)}) async-start(bf16[32,48,1280]{2,1,0:T(8,128)(2,1)} %broadcast_in_dim.64), calls=%async_computation.2 | async-start | bytes 7864320 | tf_op jit(solution)/shard_map/all_to_all | solution.py:128
  153.1 0.0 reduce-scatter.3.cloned.1.call-start
  153.2 0.6 add_convert_fusion.flags
  153.8 4.3 %fusion.13 = (bf16[768,1280]{1,0:T(8,128)(2,1)}, bf16[768,1280]{1,0:T(8,128)(2,1)}) fusion(bf16[1536,1280]{1,0:T(8,128)(2,1)} %bitcast.7), kind=kLoop, calls=%fused_computation.32 | loop fusion | bytes 7864320 | tf_op jit(solution)/shard_map/slice | solution.py:275
  158.1 28.0 %shard_map.65 = (f32[768,1280]{1,0:T(8,128)}, f32[768,1280]{1,0:T(8,128)}, f32[768,1280]{1,0:T(8,128)}) custom-call(s32[2]{0:T(128)} %add_convert_fusion.flags, bf16[768,1280]{1,0:T(8,128)(2,1)} %q_ref.5, bf16[768,1280]{1,0:T(8,128)(2,1)} %shard_map.64.ks_ref, bf16[768,1280]{1,0:T(8,128)(2,1)} %vs_ref.1, bf16[768,1280]{1,0:T(8,128)(2,1)} %get-tuple-element.16.kp_ref, ...), custom_call_target="tpu_custom_call" | custom-call | flops 6039797760 | bytes 21626880 | tf_op jit(solution)/shard_map/pallas_call | solution.py:232
  186.1 17.7 %all-to-all-done.2 = bf16[32,48,1280]{2,1,0:T(8,128)(2,1)} async-done(((bf16[32,48,1280]{2,1,0:T(8,128)(2,1)}), bf16[32,48,1280]{2,1,0:T(8,128)(2,1)}, u32[]{:S(2)}, u32[]{:S(2)}) %all-to-all-start.2) | async-done | bytes 3932192 | tf_op jit(solution)/shard_map/all_to_all | solution.py:128
  203.9 4.3 %fusion.14 = (bf16[16,48,1280]{2,1,0:T(8,128)(2,1)}, bf16[16,48,1280]{2,1,0:T(8,128)(2,1)}) fusion(bf16[32,48,1280]{2,1,0:T(8,128)(2,1)} %all-to-all-done.2), kind=kLoop, calls=%fused_computation.33 | loop fusion | bytes 7864320 | tf_op jit(solution)/shard_map/slice | solution.py:279
  208.2 18.2 %shard_map.66 = bf16[384,1280]{1,0:T(8,128)(2,1)} custom-call(s32[2]{0:T(128)} %add_convert_fusion.flags, bf16[768,1280]{1,0:T(8,128)(2,1)} %q_ref.5, bf16[768,1280]{1,0:T(8,128)(2,1)} %bitcast.22, bf16[768,1280]{1,0:T(8,128)(2,1)} %bitcast.20, bf16[128,128]{1,0:T(8,128)(2,1)} %fusion.2.swap_ref, f32[768,128]{1,0:T(8,128)} %copy.17.cos_ref.cq, ...), custom_call_target="tpu_custom_call" | custom-call | flops 1509949440 | bytes 10813440 | tf_op jit(solution)/shard_map/pallas_call | solution.py:256
  226.4 9.9 %convolution_convert_fusion.1 = bf16[384,5120]{1,0:T(8,128)(2,1)} fusion(bf16[384,1280]{1,0:T(8,128)(2,1)} %shard_map.66, bf16[1280,5120]{1,0:T(8,128)(2,1)} %param.9), kind=kOutput, calls=%fused_computation.1 | convolution fusion | flops 5035130880 | bytes 18022400 | tf_op jit(solution)/shard_map/dot_general | solution.py:280
  236.2 0.0 reduce-scatter.3.cloned.1.call-update
  236.3 0.2 reduce-scatter.5.cloned.1.call-start
  236.5 18.2 %shard_map.67 = bf16[384,1280]{1,0:T(8,128)(2,1)} custom-call(s32[2]{0:T(128)} %add_convert_fusion.flags, bf16[768,1280]{1,0:T(8,128)(2,1)} %q_ref.5, bf16[768,1280]{1,0:T(8,128)(2,1)} %bitcast.23, bf16[768,1280]{1,0:T(8,128)(2,1)} %bitcast.21, bf16[128,128]{1,0:T(8,128)(2,1)} %fusion.2.swap_ref, f32[768,128]{1,0:T(8,128)} %copy.17.cos_ref.cq, ...), custom_call_target="tpu_custom_call" | custom-call | flops 1509949440 | bytes 10813440 | tf_op jit(solution)/shard_map/pallas_call | solution.py:256
  254.8 9.9 %convolution_convert_fusion = bf16[384,5120]{1,0:T(8,128)(2,1)} fusion(bf16[384,1280]{1,0:T(8,128)(2,1)} %shard_map.67, bf16[1280,5120]{1,0:T(8,128)(2,1)} %param.9), kind=kOutput, calls=%fused_computation | convolution fusion | flops 5035130880 | bytes 18022400 | tf_op jit(solution)/shard_map/dot_general | solution.py:280
  264.7 0.0 reduce-scatter.5.cloned.1.call-update
  264.7 18.0 %reduce-scatter.3.cloned.1.call-done = bf16[384,1280]{1,0:T(8,128)(2,1)} async-done(((bf16[384,5120]{1,0:T(8,128)(2,1)}), bf16[384,1280]{1,0:T(8,128)(2,1)}) %reduce-scatter.3.cloned.1.call-update) | async-done | bytes 983056 | tf_op jit(solution)/shard_map/reduce_scatter | solution.py:281
  282.7 46.7 %reduce-scatter.5.cloned.1.call-done = bf16[384,1280]{1,0:T(8,128)(2,1)} async-done(((bf16[384,5120]{1,0:T(8,128)(2,1)}), bf16[384,1280]{1,0:T(8,128)(2,1)}) %reduce-scatter.5.cloned.1.call-update) | async-done | bytes 983056 | tf_op jit(solution)/shard_map/reduce_scatter | solution.py:281
  329.4 2.9 pad_maximum_fusion.2
  (7 shorter events, 0.0 us)
Async XLA Ops:
  9.3 10.1 %copy-start.1 = (bf16[768,1280]{1,0:T(8,128)(2,1)S(1)}, bf16[768,1280]{1,0:T(8,128)(2,1)}, u32[]{:S(2)}) copy-start(bf16[768,1280]{1,0:T(8,128)(2,1)} %vs_ref.1) | copy-start | bytes 5898244
  80.2 1.9 copy-start
  84.6 6.5 %copy-start.2 = (s32[32]{0:T(128)S(1)}, s32[32]{0:T(128)}, u32[]{:S(2)}) copy-start(s32[32]{0:T(128)} %param.10) | copy-start | bytes 388
  84.6 56.6 %all-to-all-start.1 = ((bf16[32,48,1280]{2,1,0:T(8,128)(2,1)}), bf16[32,48,1280]{2,1,0:T(8,128)(2,1)}, u32[]{:S(2)}, u32[]{:S(2)}) async-start(bf16[32,48,1280]{2,1,0:T(8,128)(2,1)} %pad_maximum_fusion.1), calls=%async_computation.1 | async-start | bytes 7864320 | tf_op jit(solution)/shard_map/all_to_all | solution.py:124
  143.3 60.6 %all-to-all-start.2 = ((bf16[32,48,1280]{2,1,0:T(8,128)(2,1)}), bf16[32,48,1280]{2,1,0:T(8,128)(2,1)}, u32[]{:S(2)}, u32[]{:S(2)}) async-start(bf16[32,48,1280]{2,1,0:T(8,128)(2,1)} %broadcast_in_dim.64), calls=%async_computation.2 | async-start | bytes 7864320 | tf_op jit(solution)/shard_map/all_to_all | solution.py:128
  153.1 129.5 %reduce-scatter.3.cloned.1.call-start = ((), (), s32[]{:S(2)}) async-start(), calls=%async_computation.5 | async-start | bytes 4915200 | tf_op jit(solution)/shard_map/reduce_scatter | solution.py:281
  236.3 93.1 %reduce-scatter.5.cloned.1.call-start = ((), (), s32[]{:S(2)}) async-start(), calls=%async_computation.6 | async-start | bytes 4915200 | tf_op jit(solution)/shard_map/reduce_scatter | solution.py:281
Sparse Core Ops, SparseCore 0:
  236.4 46.2 reduce-scatter.2
  285.1 44.2 reduce-scatter.4

commit v6 on v5

--- a/solution.py
+++ b/solution.py
@@ -261,6 +261,23 @@
     )(flags, queries, *blocks, swap_matrix(), *tables, *near)
 
 
+def head_reduce(terms):
+    rows, width = terms.shape
+    n_xl, n_c = lax.axis_size("xl"), lax.axis_size("c")
+    block = width // (n_xl * n_c)
+    xl, c = lax.axis_index("xl"), lax.axis_index("c")
+    grid = terms.reshape(rows, n_xl, n_c, block)
+    mine = lax.dynamic_slice_in_dim(grid, c, 1, axis=2)
+    other = lax.dynamic_slice_in_dim(grid, 1 - c, 1, axis=2)
+    got = lax.ppermute(other, "c", [(0, 1), (1, 0)])
+    chip = (mine.astype(jnp.float32) + got.astype(jnp.float32)).astype(jnp.bfloat16)
+    keep = lax.dynamic_slice_in_dim(chip, xl, 1, axis=1)
+    send = lax.dynamic_slice_in_dim(chip, 1 - xl, 1, axis=1)
+    got = lax.ppermute(send, "xl", [(0, 1), (1, 0)])
+    total = keep.astype(jnp.float32) + got.astype(jnp.float32)
+    return total.astype(jnp.bfloat16).reshape(rows, block)
+
+
 def shards(queries, keys, values, out_weight, sink_owner, frame_pos):
     count = queries.shape[0]
     place = frame_index()
@@ -278,7 +295,7 @@
     for half in range(halves):
         attended = sink_attention(flags, queries, (sink_kv[:count], sink_kv[count:]), own_tables, near, half, halves)
         terms = jnp.dot(attended, out_weight, preferred_element_type=jnp.float32)
-        outs.append(lax.psum_scatter(terms.astype(jnp.bfloat16), HEAD_AXES, scatter_dimension=1, tiled=True))
+        outs.append(head_reduce(terms.astype(jnp.bfloat16)))
     mixed = jnp.concatenate(outs, axis=0)
     return mixed
 

time: 340 us -> 379 us (1.11); the launches traced: 339 us -> 374 us
  local copies, waits for them, and re-layouts: 16.8 us -> 75.6 us
  waiting for transfers between devices: 131 us -> 105 us
  between operations: 14.3 us -> 1.39 us
  starting transfers between devices: 16.5 us -> 22.9 us
  other arithmetic: 9.12 us -> 14.7 us
    reduce_scatter x2 -> x0, waiting for transfers between devices: 64.6 us -> none  [shards(): lax.psum_scatter(terms.astype(jnp.bfloat16), HEAD_AXES, scatter_dimension...]
    ppermute x0 -> x4, waiting for transfers between devices: none -> 38.6 us  [the longest x2 38.5 us: head_reduce(): got = lax.ppermute(send, 'xl', [(0, 1), (1, 0)])]
    dynamic_slice x0 -> x4, local copies, waits for them, and re-layouts: none -> 31.2 us  [the longest x2 29.2 us: head_reduce(): mine = lax.dynamic_slice_in_dim(grid, c, 1, axis=2)]
    reshape x0 -> x2, local copies, waits for them, and re-layouts: none -> 20 us  [head_reduce(): grid = terms.reshape(rows, n_xl, n_c, block)]
    unnamed x6 -> x16, local copies, waits for them, and re-layouts: 1.88 us -> 9.31 us
    ppermute x0 -> x4, starting transfers between devices: none -> 6.45 us  [the longest x2 4.48 us: head_reduce(): got = lax.ppermute(other, 'c', [(0, 1), (1, 0)])]
    convert_element_type x1 -> x2, other arithmetic: 0.01 us -> 5.25 us  [head_reduce(): (mine.astype(jnp.float32) + got.astype(jnp.float32)).astype(jnp.bfloat16)]
  transfers between devices with their start and end apart: 4 -> 6, of which waited for: 4 -> 4; matrix products, arithmetic and copies ran while one was open for 5% -> 14% of each run, Pallas kernels for 14% -> 7%
where the time goes in v6:
time: 379 us; the launch traced here: 374 us
  waiting for transfers between devices  105 us (28%)
  local copies, waits for them, and re-layouts  75.6 us (20%)
  Pallas kernels  72.2 us (19%)
  blocking collectives  59 us (16%)
  matrix products  23.3 us (6%)
  starting transfers between devices  22.9 us (6%)
  other arithmetic  14.7 us (4%)
    all_to_all x1, blocking collectives, exchange(): spread = lax.all_to_all(data, FRAME_AXES, 0, 0, tiled=True)  59 us
    all_to_all x1, waiting for transfers between devices, exchange(): prev_full = lax.all_to_all(before, FRAME_AXES, 0, 0, tiled=True)  49.5 us
    ppermute x2, waiting for transfers between devices, head_reduce(): got = lax.ppermute(send, 'xl', [(0, 1), (1, 0)])  38.5 us
    pallas_call x2, Pallas kernels, sink_attention(): pl.pallas_call(sink_kernel, grid_spec=grid_spec, out_shape=jax.ShapeDtype...  36.6 us
    dynamic_slice x2, local copies, waits for them, and re-layouts, head_reduce(): mine = lax.dynamic_slice_in_dim(grid, c, 1, axis=2)  29.2 us
    pallas_call x1, Pallas kernels, near_attention(): pl.pallas_call(near_kernel, grid_spec=grid_spec, out_shape=[f32] * 3, cos...  28 us
    dot_general x2, matrix products, shards(): terms = jnp.dot(attended, out_weight, preferred_element_type=jnp.float32)  23.3 us
    reshape x2, local copies, waits for them, and re-layouts, head_reduce(): grid = terms.reshape(rows, n_xl, n_c, block)  20 us
  transfers between devices with their start and end apart: 6, of which 4 were waited for; matrix products, arithmetic and copies ran while one was open for 14% of the time, Pallas kernels for 7%

profile of v6, /device:TPU:1, one launch (start us, length us, event | category | flops | bytes accessed | tf_op | source)
XLA Modules:
  0.0 373.8 jit_solution(5421991023566846825)
XLA Ops:
  0.7 0.6 fusion.4.swap_ref
  1.3 0.8 fusion.5
  2.2 0.3 copy.24
  2.5 0.3 reshape.419
  2.8 0.9 copy.26.sin_ref.sq
  3.7 0.3 copy.23
  4.0 0.3 reshape.418
  4.3 0.9 copy.25.cos_ref.cq
  5.2 7.7 %shard_map.64.ks_ref = bf16[768,1280]{1,0:T(8,128)(2,1)} custom-call(bf16[768,1280]{1,0:T(8,128)(2,1)} %x_ref.1, bf16[128,128]{1,0:T(8,128)(2,1)} %fusion.4.swap_ref, f32[768,128]{1,0:T(8,128)} %copy.25.cos_ref.cq, f32[768,128]{1,0:T(8,128)} %copy.26.sin_ref.sq), custom_call_target="tpu_custom_call" | custom-call | flops 251658240 | bytes 3932160 | tf_op jit(solution)/shard_map/pallas_call | solution.py:180
  12.9 1.8 pad_maximum_fusion
  14.7 59.0 %all_to_all.30 = bf16[32,48,1280]{2,1,0:T(8,128)(2,1)S(1)} all-to-all(bf16[32,48,1280]{2,1,0:T(8,128)(2,1)S(1)} %bitcast.29), channel_id=1, replica_groups=mesh['z'=4,'xh'=2,'y'=4,'xl'=2,'c'=2] {'z','xh','y'}, dimensions={0} | all-to-all | bytes 7864320 | tf_op jit(solution)/shard_map/all_to_all | solution.py:121
  73.7 1.9 copy-done
  75.5 0.2 slice.43
  75.8 2.2 pad_maximum_fusion.1
  78.0 6.6 %all-to-all-start.1 = ((bf16[32,48,1280]{2,1,0:T(8,128)(2,1)}), bf16[32,48,1280]{2,1,0:T(8,128)(2,1)}, u32[]{:S(2)}, u32[]{:S(2)}) async-start(bf16[32,48,1280]{2,1,0:T(8,128)(2,1)} %pad_maximum_fusion.1), calls=%async_computation.1 | async-start | bytes 7864320 | tf_op jit(solution)/shard_map/all_to_all | solution.py:124
  84.7 0.9 constant_dynamic-slice_fusion.6
  85.6 49.5 %all-to-all-done.1 = bf16[32,48,1280]{2,1,0:T(8,128)(2,1)} async-done(((bf16[32,48,1280]{2,1,0:T(8,128)(2,1)}), bf16[32,48,1280]{2,1,0:T(8,128)(2,1)}, u32[]{:S(2)}, u32[]{:S(2)}) %all-to-all-start.1) | async-done | bytes 3932192 | tf_op jit(solution)/shard_map/all_to_all | solution.py:124
  135.2 2.1 broadcast_in_dim.64
  137.3 9.9 %all-to-all-start.2 = ((bf16[32,48,1280]{2,1,0:T(8,128)(2,1)}), bf16[32,48,1280]{2,1,0:T(8,128)(2,1)}, u32[]{:S(2)}, u32[]{:S(2)}) async-start(bf16[32,48,1280]{2,1,0:T(8,128)(2,1)} %broadcast_in_dim.64), calls=%async_computation.2 | async-start | bytes 7864320 | tf_op jit(solution)/shard_map/all_to_all | solution.py:128
  147.2 0.6 add_convert_fusion.4.flags
  147.7 4.3 %fusion.15 = (bf16[768,1280]{1,0:T(8,128)(2,1)}, bf16[768,1280]{1,0:T(8,128)(2,1)}) fusion(bf16[1536,1280]{1,0:T(8,128)(2,1)} %bitcast.7), kind=kLoop, calls=%fused_computation.44 | loop fusion | bytes 7864320 | tf_op jit(solution)/shard_map/slice | solution.py:292
  152.1 28.0 %shard_map.65 = (f32[768,1280]{1,0:T(8,128)}, f32[768,1280]{1,0:T(8,128)}, f32[768,1280]{1,0:T(8,128)}) custom-call(s32[2]{0:T(128)} %add_convert_fusion.4.flags, bf16[768,1280]{1,0:T(8,128)(2,1)} %q_ref.5, bf16[768,1280]{1,0:T(8,128)(2,1)} %shard_map.64.ks_ref, bf16[768,1280]{1,0:T(8,128)(2,1)} %vs_ref.1, bf16[768,1280]{1,0:T(8,128)(2,1)} %get-tuple-element.20.kp_ref, ...), custom_call_target="tpu_custom_call" | custom-call | flops 6039797760 | bytes 21626880 | tf_op jit(solution)/shard_map/pallas_call | solution.py:232
  180.0 16.7 %all-to-all-done.2 = bf16[32,48,1280]{2,1,0:T(8,128)(2,1)} async-done(((bf16[32,48,1280]{2,1,0:T(8,128)(2,1)}), bf16[32,48,1280]{2,1,0:T(8,128)(2,1)}, u32[]{:S(2)}, u32[]{:S(2)}) %all-to-all-start.2) | async-done | bytes 3932192 | tf_op jit(solution)/shard_map/all_to_all | solution.py:128
  196.8 4.3 %fusion.16 = (bf16[16,48,1280]{2,1,0:T(8,128)(2,1)}, bf16[16,48,1280]{2,1,0:T(8,128)(2,1)}) fusion(bf16[32,48,1280]{2,1,0:T(8,128)(2,1)} %all-to-all-done.2), kind=kLoop, calls=%fused_computation.45 | loop fusion | bytes 7864320 | tf_op jit(solution)/shard_map/slice | solution.py:296
  201.1 18.2 %shard_map.67 = bf16[384,1280]{1,0:T(8,128)(2,1)} custom-call(s32[2]{0:T(128)} %add_convert_fusion.4.flags, bf16[768,1280]{1,0:T(8,128)(2,1)} %q_ref.5, bf16[768,1280]{1,0:T(8,128)(2,1)} %bitcast.26, bf16[768,1280]{1,0:T(8,128)(2,1)} %bitcast.24, bf16[128,128]{1,0:T(8,128)(2,1)} %fusion.4.swap_ref, f32[768,128]{1,0:T(8,128)} %copy.25.cos_ref.cq, ...), custom_call_target="tpu_custom_call" | custom-call | flops 1509949440 | bytes 10813440 | tf_op jit(solution)/shard_map/pallas_call | solution.py:256
  219.3 18.3 %shard_map.66 = bf16[384,1280]{1,0:T(8,128)(2,1)} custom-call(s32[2]{0:T(128)} %add_convert_fusion.4.flags, bf16[768,1280]{1,0:T(8,128)(2,1)} %q_ref.5, bf16[768,1280]{1,0:T(8,128)(2,1)} %bitcast.27, bf16[768,1280]{1,0:T(8,128)(2,1)} %bitcast.25, bf16[128,128]{1,0:T(8,128)(2,1)} %fusion.4.swap_ref, f32[768,128]{1,0:T(8,128)} %copy.25.cos_ref.cq, ...), custom_call_target="tpu_custom_call" | custom-call | flops 1509949440 | bytes 10813440 | tf_op jit(solution)/shard_map/pallas_call | solution.py:256
  237.6 11.5 %convolution_convert_fusion = bf16[384,5120]{1,0:T(8,128)(2,1)} fusion(bf16[384,1280]{1,0:T(8,128)(2,1)S(1)} %copy-done.5, bf16[1280,5120]{1,0:T(8,128)(2,1)} %param.9), kind=kOutput, calls=%fused_computation | convolution fusion | flops 5035130880 | bytes 18022400 | tf_op jit(solution)/shard_map/dot_general | solution.py:297
  249.1 10.0 %reshape.423 = bf16[384,2,2,1280]{3,2,1,0:T(2,128)(2,1)} reshape(bf16[384,5120]{1,0:T(8,128)(2,1)} %convolution_convert_fusion) | data formatting | bytes 7864320 | tf_op jit(solution)/shard_map/reshape | solution.py:269
  259.1 14.6 %constant_dynamic-slice_fusion.2 = (bf16[384,2,1,1280]{3,2,1,0:T(2,128)(2,1)}, bf16[384,2,1,1280]{3,2,1,0:T(2,128)(2,1)}) fusion(bf16[384,2,2,1280]{3,2,1,0:T(2,128)(2,1)} %reshape.423, s32[]{:T(128)S(6)} %select_n.106, s32[]{:T(128)S(6)} %select_n.107), kind=kLoop, calls=%fused_computation.34 | loop fusion | bytes 7864328 | tf_op jit(solution)/shard_map/dynamic_slice | solution.py:270
  273.7 2.5 copy.40
  276.2 4.4 %collective-permute-start.2 = (bf16[384,2,1,1280]{3,0,2,1:T(8,128)(2,1)S(1)}, bf16[384,2,1,1280]{3,0,2,1:T(8,128)(2,1)}, u32[]{:S(2)}, u32[]{:S(2)}) collective-permute-start(bf16[384,2,1,1280]{3,0,2,1:T(8,128)(2,1)S(1)} %copy.40), channel_id=1, source_target_pairs={{0,1},{1,0},{2,3},{3,2},{4,5},{5,4},{6,7},{7,6},{8,9},{9,8},{10,11... | collective-permute-start | bytes 5898248 | tf_op jit(solution)/shard_map/ppermute | solution.py:272
  280.7 11.9 %convolution_convert_fusion.1 = bf16[384,5120]{1,0:T(8,128)(2,1)} fusion(bf16[384,1280]{1,0:T(8,128)(2,1)S(1)} %copy-done.4, bf16[1280,5120]{1,0:T(8,128)(2,1)} %param.9), kind=kOutput, calls=%fused_computation.1 | convolution fusion | flops 5035130880 | bytes 18022400 | tf_op jit(solution)/shard_map/dot_general | solution.py:297
  292.5 10.0 %reshape.421 = bf16[384,2,2,1280]{3,2,1,0:T(2,128)(2,1)} reshape(bf16[384,5120]{1,0:T(8,128)(2,1)} %convolution_convert_fusion.1) | data formatting | bytes 7864320 | tf_op jit(solution)/shard_map/reshape | solution.py:269
  302.6 14.6 %constant_dynamic-slice_fusion.5 = (bf16[384,2,1,1280]{3,2,1,0:T(2,128)(2,1)}, bf16[384,2,1,1280]{3,2,1,0:T(2,128)(2,1)}) fusion(bf16[384,2,2,1280]{3,2,1,0:T(2,128)(2,1)} %reshape.421, s32[]{:T(128)S(6)} %select_n.106, s32[]{:T(128)S(6)} %select_n.107), kind=kLoop, calls=%fused_computation.37 | loop fusion | bytes 7864328 | tf_op jit(solution)/shard_map/dynamic_slice | solution.py:270
  317.1 3.7 copy.38
  320.8 0.0 collective-permute-start
  320.9 3.3 add_convert_fusion
  324.1 1.0 constant_dynamic-slice_fusion
  325.2 2.0 collective-permute-start.3
  327.2 2.0 add_convert_fusion.1
  329.1 1.3 copy-done.2
  330.4 1.0 constant_dynamic-slice_fusion.3
  331.4 0.0 collective-permute-start.1
  331.5 17.6 %collective-permute-done.3 = bf16[384,1,1,1280]{3,0,2,1:T(8,128)(2,1)S(1)} collective-permute-done((bf16[384,1,1,1280]{3,0,2,1:T(8,128)(2,1)}, bf16[384,1,1,1280]{3,0,2,1:T(8,128)(2,1)S(1)}, u32[]{:S(2)}, u32[]{:S(2)}) %collective-permute-start.3) | collective-permute-done | bytes 983072 | tf_op jit(solution)/shard_map/ppermute | solution.py:276
  349.1 0.2 fusion.1
  349.3 20.9 %collective-permute-done.1 = bf16[384,1,1,1280]{3,0,2,1:T(8,128)(2,1)} collective-permute-done((bf16[384,1,1,1280]{3,0,2,1:T(8,128)(2,1)}, bf16[384,1,1,1280]{3,0,2,1:T(8,128)(2,1)}, u32[]{:S(2)}, u32[]{:S(2)}) %collective-permute-start.1) | collective-permute-done | bytes 983072 | tf_op jit(solution)/shard_map/ppermute | solution.py:276
  370.2 1.7 fusion
  372.0 1.4 pad_maximum_fusion.2
  (21 shorter events, 0.1 us)
Async XLA Ops:
  3.7 9.2 %copy-start.3 = (bf16[768,1280]{1,0:T(8,128)(2,1)S(1)}, bf16[768,1280]{1,0:T(8,128)(2,1)}, u32[]{:S(2)}) copy-start(bf16[768,1280]{1,0:T(8,128)(2,1)} %vs_ref.1) | copy-start | bytes 5898244
  73.7 1.9 copy-start
  78.0 6.6 %copy-start.6 = (s32[32]{0:T(128)S(1)}, s32[32]{0:T(128)}, u32[]{:S(2)}) copy-start(s32[32]{0:T(128)} %param.10) | copy-start | bytes 388
  78.0 57.1 %all-to-all-start.1 = ((bf16[32,48,1280]{2,1,0:T(8,128)(2,1)}), bf16[32,48,1280]{2,1,0:T(8,128)(2,1)}, u32[]{:S(2)}, u32[]{:S(2)}) async-start(bf16[32,48,1280]{2,1,0:T(8,128)(2,1)} %pad_maximum_fusion.1), calls=%async_computation.1 | async-start | bytes 7864320 | tf_op jit(solution)/shard_map/all_to_all | solution.py:124
  137.3 59.5 %all-to-all-start.2 = ((bf16[32,48,1280]{2,1,0:T(8,128)(2,1)}), bf16[32,48,1280]{2,1,0:T(8,128)(2,1)}, u32[]{:S(2)}, u32[]{:S(2)}) async-start(bf16[32,48,1280]{2,1,0:T(8,128)(2,1)} %broadcast_in_dim.64), calls=%async_computation.2 | async-start | bytes 7864320 | tf_op jit(solution)/shard_map/all_to_all | solution.py:128
  219.3 18.3 %copy-start.5 = (bf16[384,1280]{1,0:T(8,128)(2,1)S(1)}, bf16[384,1280]{1,0:T(8,128)(2,1)}, u32[]{:S(2)}) copy-start(bf16[384,1280]{1,0:T(8,128)(2,1)} %shard_map.67) | copy-start | bytes 2949124
  273.7 6.9 %copy-start.4 = (bf16[384,1280]{1,0:T(8,128)(2,1)S(1)}, bf16[384,1280]{1,0:T(8,128)(2,1)}, u32[]{:S(2)}) copy-start(bf16[384,1280]{1,0:T(8,128)(2,1)} %shard_map.66) | copy-start | bytes 2949124
  276.2 44.6 %collective-permute-start.2 = (bf16[384,2,1,1280]{3,0,2,1:T(8,128)(2,1)S(1)}, bf16[384,2,1,1280]{3,0,2,1:T(8,128)(2,1)}, u32[]{:S(2)}, u32[]{:S(2)}) collective-permute-start(bf16[384,2,1,1280]{3,0,2,1:T(8,128)(2,1)S(1)} %copy.40), channel_id=1, source_target_pairs={{0,1},{1,0},{2,3},{3,2},{4,5},{5,4},{6,7},{7,6},{8,9},{9,8},{10,11... | collective-permute-start | bytes 5898248 | tf_op jit(solution)/shard_map/ppermute | solution.py:272
  320.8 6.3 %collective-permute-start = (bf16[384,2,1,1280]{3,0,2,1:T(8,128)(2,1)}, bf16[384,2,1,1280]{3,0,2,1:T(8,128)(2,1)}, u32[]{:S(2)}, u32[]{:S(2)}) collective-permute-start(bf16[384,2,1,1280]{3,0,2,1:T(8,128)(2,1)} %copy.38), channel_id=1, source_target_pairs={{0,1},{1,0},{2,3},{3,2},{4,5},{5,4},{6,7},{7,6},{8,9},{9,8},{10,11... | collective-permute-start | bytes 5898248 | tf_op jit(solution)/shard_map/ppermute | solution.py:272
  320.9 6.3 %copy-start.1 = (bf16[384,2,1,1280]{3,2,1,0:T(2,128)(2,1)S(1)}, bf16[384,2,1,1280]{3,2,1,0:T(2,128)(2,1)}, u32[]{:S(2)}) copy-start(bf16[384,2,1,1280]{3,2,1,0:T(2,128)(2,1)} %get-tuple-element.15) | copy-start | bytes 5898244
  325.2 23.9 %collective-permute-start.3 = (bf16[384,1,1,1280]{3,0,2,1:T(8,128)(2,1)}, bf16[384,1,1,1280]{3,0,2,1:T(8,128)(2,1)S(1)}, u32[]{:S(2)}, u32[]{:S(2)}) collective-permute-start(bf16[384,1,1,1280]{3,0,2,1:T(8,128)(2,1)} %constant_dynamic-slice_fusion), channel_id=1, source_target_pairs={{0,2},{2,0},{1,3},{3,1},{4,6},{6,4},{5,7},{7,5},{8,10},{10,8},{9,1... | collective-permute-start | bytes 2949128 | tf_op jit(solution)/shard_map/ppermute | solution.py:276
  329.1 1.3 copy-start.2
  331.4 38.8 %collective-permute-start.1 = (bf16[384,1,1,1280]{3,0,2,1:T(8,128)(2,1)}, bf16[384,1,1,1280]{3,0,2,1:T(8,128)(2,1)}, u32[]{:S(2)}, u32[]{:S(2)}) collective-permute-start(bf16[384,1,1,1280]{3,0,2,1:T(8,128)(2,1)} %constant_dynamic-slice_fusion.3), channel_id=1, source_target_pairs={{0,2},{2,0},{1,3},{3,1},{4,6},{6,4},{5,7},{7,5},{8,10},{10,8},{9,1... | collective-permute-start | bytes 2949128 | tf_op jit(solution)/shard_map/ppermute | solution.py:276

commit v7 on v5

--- a/solution.py
+++ b/solution.py
@@ -261,6 +261,31 @@
     )(flags, queries, *blocks, swap_matrix(), *tables, *near)
 
 
+def weight_blocks(out_weight):
+    n_xl, n_c = lax.axis_size("xl"), lax.axis_size("c")
+    block = out_weight.shape[1] // (n_xl * n_c)
+    c = lax.axis_index("c")
+
+    def columns(core):
+        return jnp.stack(
+            [lax.dynamic_slice_in_dim(out_weight, (x * n_c + core) * block, block, axis=1) for x in range(n_xl)]
+        )
+
+    return columns(c), columns(1 - c)
+
+
+def head_reduce(attended, mine_w, other_w):
+    xl = lax.axis_index("xl")
+    mine = jnp.einsum("rk,xkn->xrn", attended, mine_w, preferred_element_type=jnp.float32).astype(jnp.bfloat16)
+    other = jnp.einsum("rk,xkn->xrn", attended, other_w, preferred_element_type=jnp.float32).astype(jnp.bfloat16)
+    got = lax.ppermute(other, "c", [(0, 1), (1, 0)])
+    chip = (mine.astype(jnp.float32) + got.astype(jnp.float32)).astype(jnp.bfloat16)
+    keep = lax.dynamic_index_in_dim(chip, xl, axis=0, keepdims=False)
+    send = lax.dynamic_index_in_dim(chip, 1 - xl, axis=0, keepdims=False)
+    got = lax.ppermute(send, "xl", [(0, 1), (1, 0)])
+    return (keep.astype(jnp.float32) + got.astype(jnp.float32)).astype(jnp.bfloat16)
+
+
 def shards(queries, keys, values, out_weight, sink_owner, frame_pos):
     count = queries.shape[0]
     place = frame_index()
@@ -274,11 +299,11 @@
     flags = jnp.stack([prev_used, sink_used]).astype(jnp.int32)
     near = near_attention(flags, queries, (rot_k, values, prev_kv[:count], prev_kv[count:]), own_tables)
     halves = 2
+    mine_w, other_w = weight_blocks(out_weight)
     outs = []
     for half in range(halves):
         attended = sink_attention(flags, queries, (sink_kv[:count], sink_kv[count:]), own_tables, near, half, halves)
-        terms = jnp.dot(attended, out_weight, preferred_element_type=jnp.float32)
-        outs.append(lax.psum_scatter(terms.astype(jnp.bfloat16), HEAD_AXES, scatter_dimension=1, tiled=True))
+        outs.append(head_reduce(attended, mine_w, other_w))
     mixed = jnp.concatenate(outs, axis=0)
     return mixed
 

time: 340 us -> 315 us (0.926); the launches traced: 339 us -> 310 us
  waiting for transfers between devices: 131 us -> 85.2 us
  local copies, waits for them, and re-layouts: 16.8 us -> 38.1 us
  between operations: 14.3 us -> 0.99 us
  starting transfers between devices: 16.5 us -> 22.2 us
    reduce_scatter x2 -> x0, waiting for transfers between devices: 64.6 us -> none  [shards(): lax.psum_scatter(terms.astype(jnp.bfloat16), HEAD_AXES, scatter_dimension...]
    ppermute x0 -> x4, waiting for transfers between devices: none -> 36.3 us  [the longest x2 36.3 us: head_reduce(): got = lax.ppermute(send, 'xl', [(0, 1), (1, 0)])]
    all_to_all x1, waiting for transfers between devices: 17.7 us -> 0.01 us  [exchange(): return (prev_full, lax.all_to_all(copies, FRAME_AXES, 0, 0, tiled=True))]
    dynamic_slice x0 -> x2, local copies, waits for them, and re-layouts: none -> 8.99 us  [columns(): lax.dynamic_slice_in_dim(out_weight, (x * n_c + core) * block, block, axi...]
    another operation x0 -> x1, local copies, waits for them, and re-layouts: none -> 8.98 us  [columns(): jnp.stack([lax.dynamic_slice_in_dim(out_weight, (x * n_c + core) * block,...]
    ppermute x0 -> x4, starting transfers between devices: none -> 5.32 us  [the longest x2 2.78 us: head_reduce(): got = lax.ppermute(send, 'xl', [(0, 1), (1, 0)])]
    dot_general x2 -> x4, matrix products: 19.8 us -> 23.2 us  [the longest x2 12.4 us: head_reduce(): jnp.einsum('rk,xkn->xrn', attended, other_w, preferred_element_type=jnp.f...]
  transfers between devices with their start and end apart: 4 -> 6, of which waited for: 4 -> 3; matrix products, arithmetic and copies ran while one was open for 5% -> 14% of each run, Pallas kernels for 14% -> 15%
where the time goes in v7:
time: 315 us; the launch traced here: 310 us
  waiting for transfers between devices  85.2 us (27%)
  Pallas kernels  72.3 us (23%)
  blocking collectives  58.9 us (19%)
  local copies, waits for them, and re-layouts  38.1 us (12%)
  matrix products  23.2 us (7%)
  starting transfers between devices  22.2 us (7%)
  other arithmetic  9.25 us (3%)
    all_to_all x1, blocking collectives, exchange(): spread = lax.all_to_all(data, FRAME_AXES, 0, 0, tiled=True)  58.9 us
    all_to_all x1, waiting for transfers between devices, exchange(): prev_full = lax.all_to_all(before, FRAME_AXES, 0, 0, tiled=True)  48.8 us
    pallas_call x2, Pallas kernels, sink_attention(): pl.pallas_call(sink_kernel, grid_spec=grid_spec, out_shape=jax.ShapeDtype...  36.7 us
    ppermute x2, waiting for transfers between devices, head_reduce(): got = lax.ppermute(send, 'xl', [(0, 1), (1, 0)])  36.3 us
    pallas_call x1, Pallas kernels, near_attention(): pl.pallas_call(near_kernel, grid_spec=grid_spec, out_shape=[f32] * 3, cos...  28 us
    dot_general x2, matrix products, head_reduce(): jnp.einsum('rk,xkn->xrn', attended, other_w, preferred_element_type=jnp.f...  12.4 us
    dot_general x2, matrix products, head_reduce(): jnp.einsum('rk,xkn->xrn', attended, mine_w, preferred_element_type=jnp.fl...  10.8 us
    all_to_all x1, starting transfers between devices, exchange(): return (prev_full, lax.all_to_all(copies, FRAME_AXES, 0, 0, tiled=True))  10.4 us
  transfers between devices with their start and end apart: 6, of which 3 were waited for; matrix products, arithmetic and copies ran while one was open for 14% of the time, Pallas kernels for 15%

profile of v7, /device:TPU:1, one launch (start us, length us, event | category | flops | bytes accessed | tf_op | source)
XLA Modules:
  0.0 310.1 jit_solution(10741605584822471584)
XLA Ops:
  0.7 0.6 fusion.20.swap_ref
  1.3 0.8 fusion.21
  2.1 0.3 copy.24
  2.5 0.3 reshape.411
  2.7 0.9 copy.26.sin_ref.sq
  3.7 0.3 copy.23
  4.0 0.0 copy-start.6
  4.0 0.3 reshape.410
  4.3 0.9 copy.25.cos_ref.cq
  5.2 7.6 %shard_map.64.ks_ref = bf16[768,1280]{1,0:T(8,128)(2,1)} custom-call(bf16[768,1280]{1,0:T(8,128)(2,1)} %x_ref.1, bf16[128,128]{1,0:T(8,128)(2,1)} %fusion.20.swap_ref, f32[768,128]{1,0:T(8,128)} %copy.25.cos_ref.cq, f32[768,128]{1,0:T(8,128)} %copy.26.sin_ref.sq), custom_call_target="tpu_custom_call" | custom-call | flops 251658240 | bytes 3932160 | tf_op jit(solution)/shard_map/pallas_call | solution.py:180
  12.9 1.8 pad_maximum_fusion.6
  14.7 58.9 %all_to_all.30 = bf16[32,48,1280]{2,1,0:T(8,128)(2,1)S(1)} all-to-all(bf16[32,48,1280]{2,1,0:T(8,128)(2,1)S(1)} %bitcast.59), channel_id=1, replica_groups=mesh['z'=4,'xh'=2,'y'=4,'xl'=2,'c'=2] {'z','xh','y'}, dimensions={0} | all-to-all | bytes 7864320 | tf_op jit(solution)/shard_map/all_to_all | solution.py:121
  73.6 1.8 copy-done
  75.5 0.2 slice.43
  75.7 2.2 pad_maximum_fusion.7
  77.9 6.4 %all-to-all-start.1 = ((bf16[32,48,1280]{2,1,0:T(8,128)(2,1)}), bf16[32,48,1280]{2,1,0:T(8,128)(2,1)}, u32[]{:S(2)}, u32[]{:S(2)}) async-start(bf16[32,48,1280]{2,1,0:T(8,128)(2,1)} %pad_maximum_fusion.7), calls=%async_computation.1 | async-start | bytes 7864320 | tf_op jit(solution)/shard_map/all_to_all | solution.py:124
  84.5 0.9 constant_dynamic-slice_fusion.2
  85.4 48.8 %all-to-all-done.1 = bf16[32,48,1280]{2,1,0:T(8,128)(2,1)} async-done(((bf16[32,48,1280]{2,1,0:T(8,128)(2,1)}), bf16[32,48,1280]{2,1,0:T(8,128)(2,1)}, u32[]{:S(2)}, u32[]{:S(2)}) %all-to-all-start.1) | async-done | bytes 3932192 | tf_op jit(solution)/shard_map/all_to_all | solution.py:124
  134.2 2.1 broadcast_in_dim.64
  136.4 10.4 %all-to-all-start.2 = ((bf16[32,48,1280]{2,1,0:T(8,128)(2,1)}), bf16[32,48,1280]{2,1,0:T(8,128)(2,1)}, u32[]{:S(2)}, u32[]{:S(2)}) async-start(bf16[32,48,1280]{2,1,0:T(8,128)(2,1)} %broadcast_in_dim.64), calls=%async_computation.2 | async-start | bytes 7864320 | tf_op jit(solution)/shard_map/all_to_all | solution.py:128
  146.8 9.0 %dynamic-slice_bitcast_fusion.1 = (bf16[1,1280,1280]{2,1,0:T(8,128)(2,1)}, bf16[1,1280,1280]{2,1,0:T(8,128)(2,1)}, bf16[1280,1280]{1,0:T(8,128)(2,1)}, bf16[1280,1280]{1,0:T(8,128)(2,1)S(1)}) fusion(bf16[1280,5120]{1,0:T(8,128)(2,1)} %param.9, s32[]{:T(128)S(6)} %select_n.103, s32[]{:T(128)S(6)} %select_n.104, s32[]{:T(128)S(6)} %select_n.114, s32[]{:T(128)S(6)} %select_n.113), kind=kLoop, calls=%fused_computation.17 | loop fusion | bytes 26214416 | tf_op jit(solution)/shard_map/stack | solution.py:270
  155.8 5.6 %copy.32 = bf16[1280,1280]{0,1:T(8,128)(2,1)} copy(bf16[1280,1280]{1,0:T(8,128)(2,1)} %get-tuple-element.17) | data formatting | bytes 6553600 | tf_op jit(solution)/shard_map/dynamic_slice | solution.py:271
  161.4 3.4 %copy.31 = bf16[1280,1280]{0,1:T(8,128)(2,1)} copy(bf16[1280,1280]{1,0:T(8,128)(2,1)S(1)} %get-tuple-element.18) | data formatting | bytes 6553600 | tf_op jit(solution)/shard_map/dynamic_slice | solution.py:271
  164.8 0.6 add_convert_fusion.flags
  165.5 4.3 %fusion.35 = (bf16[768,1280]{1,0:T(8,128)(2,1)}, bf16[768,1280]{1,0:T(8,128)(2,1)}) fusion(bf16[1536,1280]{1,0:T(8,128)(2,1)} %bitcast.9), kind=kLoop, calls=%fused_computation.64 | loop fusion | bytes 7864320 | tf_op jit(solution)/shard_map/slice | solution.py:300
  169.7 28.0 %shard_map.65 = (f32[768,1280]{1,0:T(8,128)}, f32[768,1280]{1,0:T(8,128)}, f32[768,1280]{1,0:T(8,128)}) custom-call(s32[2]{0:T(128)} %add_convert_fusion.flags, bf16[768,1280]{1,0:T(8,128)(2,1)} %q_ref.5, bf16[768,1280]{1,0:T(8,128)(2,1)} %shard_map.64.ks_ref, bf16[768,1280]{1,0:T(8,128)(2,1)} %vs_ref.1, bf16[768,1280]{1,0:T(8,128)(2,1)} %get-tuple-element.20.kp_ref, ...), custom_call_target="tpu_custom_call" | custom-call | flops 6039797760 | bytes 21626880 | tf_op jit(solution)/shard_map/pallas_call | solution.py:232
  197.7 4.3 %fusion.36 = (bf16[16,48,1280]{2,1,0:T(8,128)(2,1)}, bf16[16,48,1280]{2,1,0:T(8,128)(2,1)}) fusion(bf16[32,48,1280]{2,1,0:T(8,128)(2,1)} %all-to-all-done.2), kind=kLoop, calls=%fused_computation.65 | loop fusion | bytes 7864320 | tf_op jit(solution)/shard_map/slice | solution.py:305
  202.1 18.5 %shard_map.66 = bf16[384,1280]{1,0:T(8,128)(2,1)} custom-call(s32[2]{0:T(128)} %add_convert_fusion.flags, bf16[768,1280]{1,0:T(8,128)(2,1)} %q_ref.5, bf16[768,1280]{1,0:T(8,128)(2,1)} %bitcast.56, bf16[768,1280]{1,0:T(8,128)(2,1)} %bitcast.54, bf16[128,128]{1,0:T(8,128)(2,1)} %fusion.20.swap_ref, f32[768,128]{1,0:T(8,128)} %copy.25.cos_ref.cq, ...), custom_call_target="tpu_custom_call" | custom-call | flops 1509949440 | bytes 10813440 | tf_op jit(solution)/shard_map/pallas_call | solution.py:256
  220.6 6.2 %fusion.11 = bf16[2,384,1280]{2,1,0:T(8,128)(2,1)} fusion(bf16[1,1280,1280]{1,2,0:T(8,128)(2,1)S(1)} %bitcast.60, bf16[1,1280,1280]{1,2,0:T(8,128)(2,1)} %bitcast.62, bf16[384,1280]{1,0:T(8,128)(2,1)} %shard_map.66), kind=kOutput, calls=%fused_computation.19 | convolution fusion | flops 2520842240 | bytes 9502720 | tf_op jit(solution)/shard_map/rk,xkn->xrn/dot_general | solution.py:280
  226.8 2.5 collective-permute-start
  229.3 18.2 %shard_map.67 = bf16[384,1280]{1,0:T(8,128)(2,1)} custom-call(s32[2]{0:T(128)} %add_convert_fusion.flags, bf16[768,1280]{1,0:T(8,128)(2,1)} %q_ref.5, bf16[768,1280]{1,0:T(8,128)(2,1)} %bitcast.57, bf16[768,1280]{1,0:T(8,128)(2,1)} %bitcast.55, bf16[128,128]{1,0:T(8,128)(2,1)} %fusion.20.swap_ref, f32[768,128]{1,0:T(8,128)} %copy.25.cos_ref.cq, ...), custom_call_target="tpu_custom_call" | custom-call | flops 1509949440 | bytes 10813440 | tf_op jit(solution)/shard_map/pallas_call | solution.py:256
  247.5 6.2 %fusion.10 = bf16[2,384,1280]{2,1,0:T(8,128)(2,1)} fusion(bf16[1,1280,1280]{1,2,0:T(8,128)(2,1)S(1)} %bitcast.61, bf16[1,1280,1280]{1,2,0:T(8,128)(2,1)} %bitcast.63, bf16[384,1280]{1,0:T(8,128)(2,1)} %shard_map.67), kind=kOutput, calls=%fused_computation.18 | convolution fusion | flops 2520842240 | bytes 9502720 | tf_op jit(solution)/shard_map/rk,xkn->xrn/dot_general | solution.py:280
  253.7 0.0 collective-permute-start.2
  253.7 0.0 collective-permute-done
  253.8 6.6 %fusion.5 = bf16[2,384,1280]{2,1,0:T(8,128)(2,1)S(1)} fusion(bf16[2,384,1280]{2,1,0:T(8,128)(2,1)} %collective-permute-done, bf16[1,1280,1280]{2,1,0:T(8,128)(2,1)} %get-tuple-element.16, bf16[1,1280,1280]{2,1,0:T(8,128)(2,1)} %get-tuple-element.15, bf16[384,1280]{1,0:T(8,128)(2,1)} %shard_map.66), kind=kOutput, calls=%fused_computation.11 | convolution fusion | flops 2534604800 | bytes 11468800 | tf_op jit(solution)/shard_map/rk,xkn->xrn/dot_general | solution.py:279
  260.4 1.0 dynamic-slice_bitcast_fusion.3
  261.4 2.8 collective-permute-start.1
  264.2 0.0 collective-permute-done.2
  264.2 4.2 %fusion.4 = bf16[2,384,1280]{2,1,0:T(8,128)(2,1)S(1)} fusion(bf16[2,384,1280]{2,1,0:T(8,128)(2,1)} %collective-permute-done.2, bf16[1,1280,1280]{2,1,0:T(8,128)(2,1)S(1)} %copy-done.3, bf16[1,1280,1280]{2,1,0:T(8,128)(2,1)S(1)} %copy-done.2, bf16[384,1280]{1,0:T(8,128)(2,1)S(1)} %copy-done.7), kind=kOutput, calls=%fused_computation.9 | convolution fusion | flops 2534604800 | bytes 11468800 | tf_op jit(solution)/shard_map/rk,xkn->xrn/dot_general | solution.py:279
  268.4 0.0 copy-start.4
  268.4 1.3 copy-done.4
  269.7 1.0 dynamic-slice_bitcast_fusion.2
  270.7 0.0 collective-permute-start.3
  270.7 15.4 %collective-permute-done.1 = bf16[384,1280]{1,0:T(8,128)(2,1)S(1)} collective-permute-done((bf16[384,1280]{1,0:T(8,128)(2,1)}, bf16[384,1280]{1,0:T(8,128)(2,1)S(1)}, u32[]{:S(2)}, u32[]{:S(2)}) %collective-permute-start.1) | collective-permute-done | bytes 983072 | tf_op jit(solution)/shard_map/ppermute | solution.py:285
  286.1 0.2 fusion.13
  286.3 20.9 %collective-permute-done.3 = bf16[384,1280]{1,0:T(8,128)(2,1)} collective-permute-done((bf16[384,1280]{1,0:T(8,128)(2,1)}, bf16[384,1280]{1,0:T(8,128)(2,1)}, u32[]{:S(2)}, u32[]{:S(2)}) %collective-permute-start.3) | collective-permute-done | bytes 983072 | tf_op jit(solution)/shard_map/ppermute | solution.py:285
  307.2 1.5 fusion.12
  308.7 1.4 pad_maximum_fusion.24
  (22 shorter events, 0.1 us)
Async XLA Ops:
  4.0 8.9 %copy-start.6 = (bf16[768,1280]{1,0:T(8,128)(2,1)S(1)}, bf16[768,1280]{1,0:T(8,128)(2,1)}, u32[]{:S(2)}) copy-start(bf16[768,1280]{1,0:T(8,128)(2,1)} %vs_ref.1) | copy-start | bytes 5898244
  73.6 1.9 copy-start
  77.9 6.4 %copy-start.8 = (s32[32]{0:T(128)S(1)}, s32[32]{0:T(128)}, u32[]{:S(2)}) copy-start(s32[32]{0:T(128)} %param.10) | copy-start | bytes 388
  77.9 56.3 %all-to-all-start.1 = ((bf16[32,48,1280]{2,1,0:T(8,128)(2,1)}), bf16[32,48,1280]{2,1,0:T(8,128)(2,1)}, u32[]{:S(2)}, u32[]{:S(2)}) async-start(bf16[32,48,1280]{2,1,0:T(8,128)(2,1)} %pad_maximum_fusion.7), calls=%async_computation.1 | async-start | bytes 7864320 | tf_op jit(solution)/shard_map/all_to_all | solution.py:124
  136.4 61.4 %all-to-all-start.2 = ((bf16[32,48,1280]{2,1,0:T(8,128)(2,1)}), bf16[32,48,1280]{2,1,0:T(8,128)(2,1)}, u32[]{:S(2)}, u32[]{:S(2)}) async-start(bf16[32,48,1280]{2,1,0:T(8,128)(2,1)} %broadcast_in_dim.64), calls=%async_computation.2 | async-start | bytes 7864320 | tf_op jit(solution)/shard_map/all_to_all | solution.py:128
  202.1 18.5 %copy-start.1 = (bf16[1280,1280]{0,1:T(8,128)(2,1)S(1)}, bf16[1280,1280]{0,1:T(8,128)(2,1)}, u32[]{:S(2)}) copy-start(bf16[1280,1280]{0,1:T(8,128)(2,1)} %copy.32) | copy-start | bytes 9830404
  226.8 27.0 %collective-permute-start = (bf16[2,384,1280]{2,1,0:T(8,128)(2,1)}, bf16[2,384,1280]{2,1,0:T(8,128)(2,1)}, u32[]{:S(2)}, u32[]{:S(2)}) collective-permute-start(bf16[2,384,1280]{2,1,0:T(8,128)(2,1)} %fusion.11), channel_id=1, source_target_pairs={{0,1},{1,0},{2,3},{3,2},{4,5},{5,4},{6,7},{7,6},{8,9},{9,8},{10,11... | collective-permute-start | bytes 5898248 | tf_op jit(solution)/shard_map/ppermute | solution.py:281
  253.7 10.5 %collective-permute-start.2 = (bf16[2,384,1280]{2,1,0:T(8,128)(2,1)}, bf16[2,384,1280]{2,1,0:T(8,128)(2,1)}, u32[]{:S(2)}, u32[]{:S(2)}) collective-permute-start(bf16[2,384,1280]{2,1,0:T(8,128)(2,1)} %fusion.10), channel_id=1, source_target_pairs={{0,1},{1,0},{2,3},{3,2},{4,5},{5,4},{6,7},{7,6},{8,9},{9,8},{10,11... | collective-permute-start | bytes 5898248 | tf_op jit(solution)/shard_map/ppermute | solution.py:281
  253.7 10.4 %copy-start.2 = (bf16[1,1280,1280]{2,1,0:T(8,128)(2,1)S(1)}, bf16[1,1280,1280]{2,1,0:T(8,128)(2,1)}, u32[]{:S(2)}) copy-start(bf16[1,1280,1280]{2,1,0:T(8,128)(2,1)} %get-tuple-element.15) | copy-start | bytes 9830404
  253.7 10.4 %copy-start.3 = (bf16[1,1280,1280]{2,1,0:T(8,128)(2,1)S(1)}, bf16[1,1280,1280]{2,1,0:T(8,128)(2,1)}, u32[]{:S(2)}) copy-start(bf16[1,1280,1280]{2,1,0:T(8,128)(2,1)} %get-tuple-element.16) | copy-start | bytes 9830404
  253.8 10.4 %copy-start.7 = (bf16[384,1280]{1,0:T(8,128)(2,1)S(1)}, bf16[384,1280]{1,0:T(8,128)(2,1)}, u32[]{:S(2)}) copy-start(bf16[384,1280]{1,0:T(8,128)(2,1)} %shard_map.67) | copy-start | bytes 2949124
  261.4 24.7 %collective-permute-start.1 = (bf16[384,1280]{1,0:T(8,128)(2,1)}, bf16[384,1280]{1,0:T(8,128)(2,1)S(1)}, u32[]{:S(2)}, u32[]{:S(2)}) collective-permute-start(bf16[384,1280]{1,0:T(8,128)(2,1)} %dynamic-slice_bitcast_fusion.3), channel_id=1, source_target_pairs={{0,2},{2,0},{1,3},{3,1},{4,6},{6,4},{5,7},{7,5},{8,10},{10,8},{9,1... | collective-permute-start | bytes 2949128 | tf_op jit(solution)/shard_map/ppermute | solution.py:285
  268.4 1.3 copy-start.4
  270.7 36.6 %collective-permute-start.3 = (bf16[384,1280]{1,0:T(8,128)(2,1)}, bf16[384,1280]{1,0:T(8,128)(2,1)}, u32[]{:S(2)}, u32[]{:S(2)}) collective-permute-start(bf16[384,1280]{1,0:T(8,128)(2,1)} %dynamic-slice_bitcast_fusion.2), channel_id=1, source_target_pairs={{0,2},{2,0},{1,3},{3,1},{4,6},{6,4},{5,7},{7,5},{8,10},{10,8},{9,1... | collective-permute-start | bytes 2949128 | tf_op jit(solution)/shard_map/ppermute | solution.py:285
  270.7 36.6 %copy-start.5 = (bf16[2,384,1280]{2,1,0:T(8,128)(2,1)S(1)}, bf16[2,384,1280]{2,1,0:T(8,128)(2,1)}, u32[]{:S(2)}) copy-start(bf16[2,384,1280]{2,1,0:T(8,128)(2,1)} %copy-done.4) | copy-start | bytes 5898244

commit v8 on v7

--- a/solution.py
+++ b/solution.py
@@ -298,7 +298,7 @@
     sink_used = sink < place
     flags = jnp.stack([prev_used, sink_used]).astype(jnp.int32)
     near = near_attention(flags, queries, (rot_k, values, prev_kv[:count], prev_kv[count:]), own_tables)
-    halves = 2
+    halves = 4
     mine_w, other_w = weight_blocks(out_weight)
     outs = []
     for half in range(halves):

time: 315 us -> 330 us (1.048)
  Pallas kernels: 72.3 us -> 89.1 us
  local copies, waits for them, and re-layouts: 38.1 us -> 26.2 us
  waiting for transfers between devices: 85.2 us -> 92.7 us
  starting transfers between devices: 22.2 us -> 25.5 us
    pallas_call x2 -> x4, Pallas kernels: 36.7 us -> 53.5 us  [sink_attention(): pl.pallas_call(sink_kernel, grid_spec=grid_spec, out_shape=jax.ShapeDtype...]
    dynamic_slice x2 -> x0, local copies, waits for them, and re-layouts: 8.99 us -> none  [columns(): lax.dynamic_slice_in_dim(out_weight, (x * n_c + core) * block, block, axi...]
    all_to_all x1, waiting for transfers between devices: 0.01 us -> 7.46 us  [exchange(): return (prev_full, lax.all_to_all(copies, FRAME_AXES, 0, 0, tiled=True))]
    dot_general x2 -> x4, matrix products: 10.8 us -> 7.81 us  [head_reduce(): jnp.einsum('rk,xkn->xrn', attended, mine_w, preferred_element_type=jnp.fl...]
    dot_general x2 -> x4, matrix products: 12.4 us -> 14.5 us  [head_reduce(): jnp.einsum('rk,xkn->xrn', attended, other_w, preferred_element_type=jnp.f...]
    ppermute x2 -> x4, waiting for transfers between devices: 36.3 us -> 35.5 us  [head_reduce(): got = lax.ppermute(send, 'xl', [(0, 1), (1, 0)])]
  transfers between devices with their start and end apart: 6 -> 10, of which waited for: 3 -> 6; matrix products, arithmetic and copies ran while one was open for 14% -> 9% of each run, Pallas kernels for 15% -> 13%
where the time goes in v8:
time: 330 us; the launch traced here: 324 us
  waiting for transfers between devices  92.7 us (28%)
  Pallas kernels  89.1 us (27%)
  blocking collectives  59 us (18%)
  local copies, waits for them, and re-layouts  26.2 us (8%)
  starting transfers between devices  25.5 us (8%)
  matrix products  22.3 us (7%)
  other arithmetic  8.05 us (2%)
    all_to_all x1, blocking collectives, exchange(): spread = lax.all_to_all(data, FRAME_AXES, 0, 0, tiled=True)  59 us
    pallas_call x4, Pallas kernels, sink_attention(): pl.pallas_call(sink_kernel, grid_spec=grid_spec, out_shape=jax.ShapeDtype...  53.5 us
    all_to_all x1, waiting for transfers between devices, exchange(): prev_full = lax.all_to_all(before, FRAME_AXES, 0, 0, tiled=True)  49.7 us
    ppermute x4, waiting for transfers between devices, head_reduce(): got = lax.ppermute(send, 'xl', [(0, 1), (1, 0)])  35.5 us
    pallas_call x1, Pallas kernels, near_attention(): pl.pallas_call(near_kernel, grid_spec=grid_spec, out_shape=[f32] * 3, cos...  28 us
    dot_general x4, matrix products, head_reduce(): jnp.einsum('rk,xkn->xrn', attended, other_w, preferred_element_type=jnp.f...  14.5 us
    all_to_all x1, starting transfers between devices, exchange(): return (prev_full, lax.all_to_all(copies, FRAME_AXES, 0, 0, tiled=True))  9.53 us
    another operation x1, local copies, waits for them, and re-layouts, columns(): jnp.stack([lax.dynamic_slice_in_dim(out_weight, (x * n_c + core) * block,...  9.03 us
  transfers between devices with their start and end apart: 10, of which 6 were waited for; matrix products, arithmetic and copies ran while one was open for 9% of the time, Pallas kernels for 13%

profile of v8, /device:TPU:1, one launch (start us, length us, event | category | flops | bytes accessed | tf_op | source)
XLA Modules:
  0.0 323.8 jit_solution(6116314959060706018)
XLA Ops:
  0.7 0.6 fusion.34.swap_ref
  1.3 0.8 fusion.35
  2.1 0.3 copy.20
  2.5 0.3 reshape.415
  2.7 0.9 copy.22.sin_ref.sq
  3.7 0.3 copy.19
  4.0 0.3 reshape.414
  4.3 0.9 copy.21.cos_ref.cq
  5.2 7.7 %shard_map.64.ks_ref = bf16[768,1280]{1,0:T(8,128)(2,1)} custom-call(bf16[768,1280]{1,0:T(8,128)(2,1)} %x_ref.1, bf16[128,128]{1,0:T(8,128)(2,1)} %fusion.34.swap_ref, f32[768,128]{1,0:T(8,128)} %copy.21.cos_ref.cq, f32[768,128]{1,0:T(8,128)} %copy.22.sin_ref.sq), custom_call_target="tpu_custom_call" | custom-call | flops 251658240 | bytes 3932160 | tf_op jit(solution)/shard_map/pallas_call | solution.py:180
  12.9 1.8 pad_maximum_fusion.2
  14.7 59.0 %all_to_all.30 = bf16[32,48,1280]{2,1,0:T(8,128)(2,1)S(1)} all-to-all(bf16[32,48,1280]{2,1,0:T(8,128)(2,1)S(1)} %bitcast.105), channel_id=1, replica_groups=mesh['z'=4,'xh'=2,'y'=4,'xl'=2,'c'=2] {'z','xh','y'}, dimensions={0} | all-to-all | bytes 7864320 | tf_op jit(solution)/shard_map/all_to_all | solution.py:121
  73.7 1.9 copy-done
  75.5 0.2 slice.47
  75.8 2.2 pad_maximum_fusion.3
  78.0 6.6 %all-to-all-start.1 = ((bf16[32,48,1280]{2,1,0:T(8,128)(2,1)}), bf16[32,48,1280]{2,1,0:T(8,128)(2,1)}, u32[]{:S(2)}, u32[]{:S(2)}) async-start(bf16[32,48,1280]{2,1,0:T(8,128)(2,1)} %pad_maximum_fusion.3), calls=%async_computation.1 | async-start | bytes 7864320 | tf_op jit(solution)/shard_map/all_to_all | solution.py:124
  84.7 0.9 constant_dynamic-slice_fusion
  85.6 49.7 %all-to-all-done.1 = bf16[32,48,1280]{2,1,0:T(8,128)(2,1)} async-done(((bf16[32,48,1280]{2,1,0:T(8,128)(2,1)}), bf16[32,48,1280]{2,1,0:T(8,128)(2,1)}, u32[]{:S(2)}, u32[]{:S(2)}) %all-to-all-start.1) | async-done | bytes 3932192 | tf_op jit(solution)/shard_map/all_to_all | solution.py:124
  135.4 2.1 broadcast_in_dim.47
  137.5 9.5 %all-to-all-start.2 = ((bf16[32,48,1280]{2,1,0:T(8,128)(2,1)}), bf16[32,48,1280]{2,1,0:T(8,128)(2,1)}, u32[]{:S(2)}, u32[]{:S(2)}) async-start(bf16[32,48,1280]{2,1,0:T(8,128)(2,1)} %broadcast_in_dim.47), calls=%async_computation.2 | async-start | bytes 7864320 | tf_op jit(solution)/shard_map/all_to_all | solution.py:128
  147.1 0.6 add_convert_fusion.4.flags
  147.7 9.0 %dynamic-slice_bitcast_fusion.3 = (bf16[1,1280,1280]{2,1,0:T(8,128)(2,1)S(1)}, bf16[1,1280,1280]{2,1,0:T(8,128)(2,1)}, bf16[1,1280,1280]{2,1,0:T(8,128)(2,1)}, bf16[1,1280,1280]{2,1,0:T(8,128)(2,1)}) fusion(bf16[1280,5120]{1,0:T(8,128)(2,1)} %param.9, s32[]{:T(128)S(6)} %select_n.107, s32[]{:T(128)S(6)} %select_n.108, s32[]{:T(128)S(6)} %select_n.118, ...), kind=kLoop, calls=%fused_computation.7 | loop fusion | bytes 26214416 | tf_op jit(solution)/shard_map/stack | solution.py:270
  156.7 4.3 %fusion.45 = (bf16[768,1280]{1,0:T(8,128)(2,1)}, bf16[768,1280]{1,0:T(8,128)(2,1)}) fusion(bf16[1536,1280]{1,0:T(8,128)(2,1)} %bitcast.9), kind=kLoop, calls=%fused_computation.80 | loop fusion | bytes 7864320 | tf_op jit(solution)/shard_map/slice | solution.py:300
  161.0 28.0 %shard_map.65 = (f32[768,1280]{1,0:T(8,128)}, f32[768,1280]{1,0:T(8,128)}, f32[768,1280]{1,0:T(8,128)}) custom-call(s32[2]{0:T(128)} %add_convert_fusion.4.flags, bf16[768,1280]{1,0:T(8,128)(2,1)} %q_ref.9, bf16[768,1280]{1,0:T(8,128)(2,1)} %shard_map.64.ks_ref, bf16[768,1280]{1,0:T(8,128)(2,1)} %vs_ref.1, bf16[768,1280]{1,0:T(8,128)(2,1)} %get-tuple-element.20.kp_ref, ...), custom_call_target="tpu_custom_call" | custom-call | flops 6039797760 | bytes 21626880 | tf_op jit(solution)/shard_map/pallas_call | solution.py:232
  188.9 7.5 %all-to-all-done.2 = bf16[32,48,1280]{2,1,0:T(8,128)(2,1)} async-done(((bf16[32,48,1280]{2,1,0:T(8,128)(2,1)}), bf16[32,48,1280]{2,1,0:T(8,128)(2,1)}, u32[]{:S(2)}, u32[]{:S(2)}) %all-to-all-start.2) | async-done | bytes 3932192 | tf_op jit(solution)/shard_map/all_to_all | solution.py:128
  196.4 4.3 %fusion.46 = (bf16[16,48,1280]{2,1,0:T(8,128)(2,1)}, bf16[16,48,1280]{2,1,0:T(8,128)(2,1)}) fusion(bf16[32,48,1280]{2,1,0:T(8,128)(2,1)} %all-to-all-done.2), kind=kLoop, calls=%fused_computation.81 | loop fusion | bytes 7864320 | tf_op jit(solution)/shard_map/slice | solution.py:305
  200.7 13.4 %shard_map.69 = bf16[192,1280]{1,0:T(8,128)(2,1)} custom-call(s32[2]{0:T(128)} %add_convert_fusion.4.flags, bf16[768,1280]{1,0:T(8,128)(2,1)} %q_ref.9, bf16[768,1280]{1,0:T(8,128)(2,1)} %bitcast.100, bf16[768,1280]{1,0:T(8,128)(2,1)} %bitcast.96, bf16[128,128]{1,0:T(8,128)(2,1)} %fusion.34.swap_ref, f32[768,128]{1,0:T(8,128)} %copy.21.cos_ref.cq, ...), custom_call_target="tpu_custom_call" | custom-call | flops 754974720 | bytes 7372800 | tf_op jit(solution)/shard_map/pallas_call | solution.py:256
  214.1 13.4 %shard_map.68 = bf16[192,1280]{1,0:T(8,128)(2,1)} custom-call(s32[2]{0:T(128)} %add_convert_fusion.4.flags, bf16[768,1280]{1,0:T(8,128)(2,1)} %q_ref.9, bf16[768,1280]{1,0:T(8,128)(2,1)} %bitcast.101, bf16[768,1280]{1,0:T(8,128)(2,1)} %bitcast.97, bf16[128,128]{1,0:T(8,128)(2,1)} %fusion.34.swap_ref, f32[768,128]{1,0:T(8,128)} %copy.21.cos_ref.cq, ...), custom_call_target="tpu_custom_call" | custom-call | flops 754974720 | bytes 7372800 | tf_op jit(solution)/shard_map/pallas_call | solution.py:256
  227.4 13.4 %shard_map.66 = bf16[192,1280]{1,0:T(8,128)(2,1)} custom-call(s32[2]{0:T(128)} %add_convert_fusion.4.flags, bf16[768,1280]{1,0:T(8,128)(2,1)} %q_ref.9, bf16[768,1280]{1,0:T(8,128)(2,1)} %bitcast.102, bf16[768,1280]{1,0:T(8,128)(2,1)} %bitcast.98, bf16[128,128]{1,0:T(8,128)(2,1)} %fusion.34.swap_ref, f32[768,128]{1,0:T(8,128)} %copy.21.cos_ref.cq, ...), custom_call_target="tpu_custom_call" | custom-call | flops 754974720 | bytes 7372800 | tf_op jit(solution)/shard_map/pallas_call | solution.py:256
  240.8 5.6 %fusion.8 = bf16[2,192,1280]{2,1,0:T(8,128)(2,1)} fusion(bf16[192,1280]{1,0:T(8,128)(2,1)} %shard_map.66, bf16[1,1280,1280]{2,1,0:T(8,128)(2,1)} %get-tuple-element.17, bf16[1,1280,1280]{2,1,0:T(8,128)(2,1)} %get-tuple-element.18), kind=kOutput, calls=%fused_computation.24 | convolution fusion | flops 1271889920 | bytes 8028160 | tf_op jit(solution)/shard_map/rk,xkn->xrn/dot_general | solution.py:280
  246.4 2.5 fusion.11
  248.9 4.3 %collective-permute-start.6 = (bf16[2,192,1280]{2,1,0:T(8,128)(2,1)}, bf16[2,192,1280]{2,1,0:T(8,128)(2,1)}, u32[]{:S(2)}, u32[]{:S(2)}) collective-permute-start(bf16[2,192,1280]{2,1,0:T(8,128)(2,1)} %fusion.11), channel_id=1, source_target_pairs={{0,1},{1,0},{2,3},{3,2},{4,5},{5,4},{6,7},{7,6},{8,9},{9,8},{10,11... | collective-permute-start | bytes 2949128 | tf_op jit(solution)/shard_map/ppermute | solution.py:281
  253.3 13.4 %shard_map.67 = bf16[192,1280]{1,0:T(8,128)(2,1)} custom-call(s32[2]{0:T(128)} %add_convert_fusion.4.flags, bf16[768,1280]{1,0:T(8,128)(2,1)} %q_ref.9, bf16[768,1280]{1,0:T(8,128)(2,1)} %bitcast.103, bf16[768,1280]{1,0:T(8,128)(2,1)} %bitcast.99, bf16[128,128]{1,0:T(8,128)(2,1)} %fusion.34.swap_ref, f32[768,128]{1,0:T(8,128)} %copy.21.cos_ref.cq, ...), custom_call_target="tpu_custom_call" | custom-call | flops 754974720 | bytes 7372800 | tf_op jit(solution)/shard_map/pallas_call | solution.py:256
  266.8 4.7 %fusion.10 = bf16[2,192,1280]{2,1,0:T(8,128)(2,1)S(1)} fusion(bf16[192,1280]{1,0:T(8,128)(2,1)} %shard_map.68, bf16[1,1280,1280]{2,1,0:T(8,128)(2,1)} %get-tuple-element.17, bf16[1,1280,1280]{2,1,0:T(8,128)(2,1)} %get-tuple-element.18), kind=kOutput, calls=%fused_computation.26 | convolution fusion | flops 1271889920 | bytes 8028160 | tf_op jit(solution)/shard_map/rk,xkn->xrn/dot_general | solution.py:280
  271.4 0.2 copy-done.5
  271.7 1.7 fusion.9
  273.3 0.5 collective-permute-start.2
  274.0 2.8 add_convert_fusion
  276.8 2.6 collective-permute-start.7
  279.4 1.7 add_convert_fusion.3
  281.3 1.7 add_convert_fusion.2
  283.0 1.5 collective-permute-start.3
  284.5 1.7 add_convert_fusion.1
  286.3 0.1 collective-permute-start.5
  286.4 4.3 %collective-permute-done.7 = bf16[192,1280]{1,0:T(8,128)(2,1)S(1)} collective-permute-done((bf16[192,1280]{1,0:T(8,128)(2,1)S(1)}, bf16[192,1280]{1,0:T(8,128)(2,1)S(1)}, u32[]{:S(2)}, u32[]{:S(2)}) %collective-permute-start.7) | collective-permute-done | bytes 491552 | tf_op jit(solution)/shard_map/ppermute | solution.py:285
  290.8 10.4 %collective-permute-done.1 = bf16[192,1280]{1,0:T(8,128)(2,1)S(1)} collective-permute-done((bf16[192,1280]{1,0:T(8,128)(2,1)S(1)}, bf16[192,1280]{1,0:T(8,128)(2,1)S(1)}, u32[]{:S(2)}, u32[]{:S(2)}) %collective-permute-start.1) | collective-permute-done | bytes 491552 | tf_op jit(solution)/shard_map/ppermute | solution.py:285
  301.3 10.4 %collective-permute-done.3 = bf16[192,1280]{1,0:T(8,128)(2,1)S(1)} collective-permute-done((bf16[192,1280]{1,0:T(8,128)(2,1)S(1)}, bf16[192,1280]{1,0:T(8,128)(2,1)S(1)}, u32[]{:S(2)}, u32[]{:S(2)}) %collective-permute-start.3) | collective-permute-done | bytes 491552 | tf_op jit(solution)/shard_map/ppermute | solution.py:285
  311.8 10.4 %collective-permute-done.5 = bf16[192,1280]{1,0:T(8,128)(2,1)S(1)} collective-permute-done((bf16[192,1280]{1,0:T(8,128)(2,1)S(1)}, bf16[192,1280]{1,0:T(8,128)(2,1)S(1)}, u32[]{:S(2)}, u32[]{:S(2)}) %collective-permute-start.5) | collective-permute-done | bytes 491552 | tf_op jit(solution)/shard_map/ppermute | solution.py:285
  322.4 1.4 pad_maximum_fusion.4
  (46 shorter events, 1.1 us)
Async XLA Ops:
  3.7 9.2 %copy-start.6 = (bf16[768,1280]{1,0:T(8,128)(2,1)S(1)}, bf16[768,1280]{1,0:T(8,128)(2,1)}, u32[]{:S(2)}) copy-start(bf16[768,1280]{1,0:T(8,128)(2,1)} %vs_ref.1) | copy-start | bytes 5898244
  73.7 1.9 copy-start
  78.0 6.6 %copy-start.12 = (s32[32]{0:T(128)S(1)}, s32[32]{0:T(128)}, u32[]{:S(2)}) copy-start(s32[32]{0:T(128)} %param.10) | copy-start | bytes 388
  78.0 57.3 %all-to-all-start.1 = ((bf16[32,48,1280]{2,1,0:T(8,128)(2,1)}), bf16[32,48,1280]{2,1,0:T(8,128)(2,1)}, u32[]{:S(2)}, u32[]{:S(2)}) async-start(bf16[32,48,1280]{2,1,0:T(8,128)(2,1)} %pad_maximum_fusion.3), calls=%async_computation.1 | async-start | bytes 7864320 | tf_op jit(solution)/shard_map/all_to_all | solution.py:124
  137.5 58.9 %all-to-all-start.2 = ((bf16[32,48,1280]{2,1,0:T(8,128)(2,1)}), bf16[32,48,1280]{2,1,0:T(8,128)(2,1)}, u32[]{:S(2)}, u32[]{:S(2)}) async-start(bf16[32,48,1280]{2,1,0:T(8,128)(2,1)} %broadcast_in_dim.47), calls=%async_computation.2 | async-start | bytes 7864320 | tf_op jit(solution)/shard_map/all_to_all | solution.py:128
  240.8 5.6 %copy-start.2 = (bf16[1,1280,1280]{2,1,0:T(8,128)(2,1)S(1)}, bf16[1,1280,1280]{2,1,0:T(8,128)(2,1)}, u32[]{:S(2)}) copy-start(bf16[1,1280,1280]{2,1,0:T(8,128)(2,1)} %get-tuple-element.17) | copy-start | bytes 9830404
  240.8 5.6 %copy-start.4 = (bf16[1,1280,1280]{2,1,0:T(8,128)(2,1)S(1)}, bf16[1,1280,1280]{2,1,0:T(8,128)(2,1)}, u32[]{:S(2)}) copy-start(bf16[1,1280,1280]{2,1,0:T(8,128)(2,1)} %get-tuple-element.18) | copy-start | bytes 9830404
  240.8 5.6 %copy-start.10 = (bf16[192,1280]{1,0:T(8,128)(2,1)S(1)}, bf16[192,1280]{1,0:T(8,128)(2,1)}, u32[]{:S(2)}) copy-start(bf16[192,1280]{1,0:T(8,128)(2,1)} %shard_map.69) | copy-start | bytes 1474564
  248.9 25.0 %collective-permute-start.6 = (bf16[2,192,1280]{2,1,0:T(8,128)(2,1)}, bf16[2,192,1280]{2,1,0:T(8,128)(2,1)}, u32[]{:S(2)}, u32[]{:S(2)}) collective-permute-start(bf16[2,192,1280]{2,1,0:T(8,128)(2,1)} %fusion.11), channel_id=1, source_target_pairs={{0,1},{1,0},{2,3},{3,2},{4,5},{5,4},{6,7},{7,6},{8,9},{9,8},{10,11... | collective-permute-start | bytes 2949128 | tf_op jit(solution)/shard_map/ppermute | solution.py:281
  266.6 4.8 %copy-start.3 = (bf16[1,1280,1280]{2,1,0:T(8,128)(2,1)S(1)}, bf16[1,1280,1280]{2,1,0:T(8,128)(2,1)}, u32[]{:S(2)}) copy-start(bf16[1,1280,1280]{2,1,0:T(8,128)(2,1)} %get-tuple-element.17) | copy-start | bytes 9830404
  266.6 5.0 %copy-start.5 = (bf16[1,1280,1280]{2,1,0:T(8,128)(2,1)S(1)}, bf16[1,1280,1280]{2,1,0:T(8,128)(2,1)}, u32[]{:S(2)}) copy-start(bf16[1,1280,1280]{2,1,0:T(8,128)(2,1)} %get-tuple-element.18) | copy-start | bytes 9830404
  266.6 5.0 %copy-start.8 = (bf16[192,1280]{1,0:T(8,128)(2,1)S(1)}, bf16[192,1280]{1,0:T(8,128)(2,1)}, u32[]{:S(2)}) copy-start(bf16[192,1280]{1,0:T(8,128)(2,1)} %shard_map.67) | copy-start | bytes 1474564
  266.7 12.7 %collective-permute-start = (bf16[2,192,1280]{2,1,0:T(8,128)(2,1)}, bf16[2,192,1280]{2,1,0:T(8,128)(2,1)S(1)}, u32[]{:S(2)}, u32[]{:S(2)}) collective-permute-start(bf16[2,192,1280]{2,1,0:T(8,128)(2,1)} %fusion.8), channel_id=1, source_target_pairs={{0,1},{1,0},{2,3},{3,2},{4,5},{5,4},{6,7},{7,6},{8,9},{9,8},{10,11... | collective-permute-start | bytes 2949128 | tf_op jit(solution)/shard_map/ppermute | solution.py:281
  271.7 2.3 copy-start.1
  271.7 2.3 copy-start.11
  273.3 7.9 %collective-permute-start.2 = (bf16[2,192,1280]{2,1,0:T(8,128)(2,1)S(1)}, bf16[2,192,1280]{2,1,0:T(8,128)(2,1)S(1)}, u32[]{:S(2)}, u32[]{:S(2)}) collective-permute-start(bf16[2,192,1280]{2,1,0:T(8,128)(2,1)S(1)} %fusion.9), channel_id=1, source_target_pairs={{0,1},{1,0},{2,3},{3,2},{4,5},{5,4},{6,7},{7,6},{8,9},{9,8},{10,11... | collective-permute-start | bytes 2949128 | tf_op jit(solution)/shard_map/ppermute | solution.py:281
  273.9 10.6 %collective-permute-start.4 = (bf16[2,192,1280]{2,1,0:T(8,128)(2,1)S(1)}, bf16[2,192,1280]{2,1,0:T(8,128)(2,1)S(1)}, u32[]{:S(2)}, u32[]{:S(2)}) collective-permute-start(bf16[2,192,1280]{2,1,0:T(8,128)(2,1)S(1)} %fusion.10), channel_id=1, source_target_pairs={{0,1},{1,0},{2,3},{3,2},{4,5},{5,4},{6,7},{7,6},{8,9},{9,8},{10,11... | collective-permute-start | bytes 2949128 | tf_op jit(solution)/shard_map/ppermute | solution.py:281
  274.0 5.4 %copy-start.9 = (bf16[192,1280]{1,0:T(8,128)(2,1)S(1)}, bf16[192,1280]{1,0:T(8,128)(2,1)}, u32[]{:S(2)}) copy-start(bf16[192,1280]{1,0:T(8,128)(2,1)} %shard_map.66) | copy-start | bytes 1474564
  276.8 13.8 %collective-permute-start.7 = (bf16[192,1280]{1,0:T(8,128)(2,1)S(1)}, bf16[192,1280]{1,0:T(8,128)(2,1)S(1)}, u32[]{:S(2)}, u32[]{:S(2)}) collective-permute-start(bf16[192,1280]{1,0:T(8,128)(2,1)S(1)} %dynamic-slice_bitcast_fusion.4), channel_id=1, source_target_pairs={{0,2},{2,0},{1,3},{3,1},{4,6},{6,4},{5,7},{7,5},{8,10},{10,8},{9,1... | collective-permute-start | bytes 1474568 | tf_op jit(solution)/shard_map/ppermute | solution.py:285
  281.1 3.4 %copy-start.7 = (bf16[192,1280]{1,0:T(8,128)(2,1)S(1)}, bf16[192,1280]{1,0:T(8,128)(2,1)}, u32[]{:S(2)}) copy-start(bf16[192,1280]{1,0:T(8,128)(2,1)} %shard_map.68) | copy-start | bytes 1474564
  281.2 20.0 %collective-permute-start.1 = (bf16[192,1280]{1,0:T(8,128)(2,1)S(1)}, bf16[192,1280]{1,0:T(8,128)(2,1)S(1)}, u32[]{:S(2)}, u32[]{:S(2)}) collective-permute-start(bf16[192,1280]{1,0:T(8,128)(2,1)S(1)} %dynamic-slice_bitcast_fusion.7), channel_id=1, source_target_pairs={{0,2},{2,0},{1,3},{3,1},{4,6},{6,4},{5,7},{7,5},{8,10},{10,8},{9,1... | collective-permute-start | bytes 1474568 | tf_op jit(solution)/shard_map/ppermute | solution.py:285
  283.0 28.7 %collective-permute-start.3 = (bf16[192,1280]{1,0:T(8,128)(2,1)S(1)}, bf16[192,1280]{1,0:T(8,128)(2,1)S(1)}, u32[]{:S(2)}, u32[]{:S(2)}) collective-permute-start(bf16[192,1280]{1,0:T(8,128)(2,1)S(1)} %dynamic-slice_bitcast_fusion.6), channel_id=1, source_target_pairs={{0,2},{2,0},{1,3},{3,1},{4,6},{6,4},{5,7},{7,5},{8,10},{10,8},{9,1... | collective-permute-start | bytes 1474568 | tf_op jit(solution)/shard_map/ppermute | solution.py:285
  286.3 36.0 %collective-permute-start.5 = (bf16[192,1280]{1,0:T(8,128)(2,1)S(1)}, bf16[192,1280]{1,0:T(8,128)(2,1)S(1)}, u32[]{:S(2)}, u32[]{:S(2)}) collective-permute-start(bf16[192,1280]{1,0:T(8,128)(2,1)S(1)} %dynamic-slice_bitcast_fusion.5), channel_id=1, source_target_pairs={{0,2},{2,0},{1,3},{3,1},{4,6},{6,4},{5,7},{7,5},{8,10},{10,8},{9,1... | collective-permute-start | bytes 1474568 | tf_op jit(solution)/shard_map/ppermute | solution.py:285

commit v9 on v7

--- a/solution.py
+++ b/solution.py
@@ -217,10 +217,11 @@
     count, width = queries.shape
     heads_here = width // HDIM
     head, whole, swap = specs(count)
+    value_spec = pl.BlockSpec((count, HDIM), lambda h, flags: (1, h))
     grid_spec = pltpu.PrefetchScalarGridSpec(
         num_scalar_prefetch=1,
         grid=(heads_here,),
-        in_specs=[head] * 5 + [swap] + [whole] * 2,
+        in_specs=[head] * 4 + [value_spec, swap] + [whole] * 2,
         out_specs=[head] * 3,
     )
     cost = pl.CostEstimate(
@@ -240,12 +241,13 @@
     rows = count // halves
     part = pl.BlockSpec((rows, HDIM), lambda h, flags: (half, h))
     part_table = pl.BlockSpec((rows, HDIM), lambda h, flags: (half, 0))
-    head = pl.BlockSpec((count, HDIM), lambda h, flags: (0, h))
+    key_spec = pl.BlockSpec((count, HDIM), lambda h, flags: (0, h))
+    value_spec = pl.BlockSpec((count, HDIM), lambda h, flags: (1, h))
     swap = pl.BlockSpec((HDIM, HDIM), lambda h, flags: (0, 0))
     grid_spec = pltpu.PrefetchScalarGridSpec(
         num_scalar_prefetch=1,
         grid=(heads_here,),
-        in_specs=[part] + [head] * 2 + [swap] + [part_table] * 2 + [part] * 3,
+        in_specs=[part, key_spec, value_spec, swap] + [part_table] * 2 + [part] * 3,
         out_specs=pl.BlockSpec((rows, HDIM), lambda h, flags: (0, h)),
     )
     cost = pl.CostEstimate(
@@ -297,12 +299,12 @@
     prev_used = (place >= 1) & (place - 1 != sink)
     sink_used = sink < place
     flags = jnp.stack([prev_used, sink_used]).astype(jnp.int32)
-    near = near_attention(flags, queries, (rot_k, values, prev_kv[:count], prev_kv[count:]), own_tables)
+    near = near_attention(flags, queries, (rot_k, values, prev_kv, prev_kv), own_tables)
     halves = 2
     mine_w, other_w = weight_blocks(out_weight)
     outs = []
     for half in range(halves):
-        attended = sink_attention(flags, queries, (sink_kv[:count], sink_kv[count:]), own_tables, near, half, halves)
+        attended = sink_attention(flags, queries, (sink_kv, sink_kv), own_tables, near, half, halves)
         outs.append(head_reduce(attended, mine_w, other_w))
     mixed = jnp.concatenate(outs, axis=0)
     return mixed

time: 315 us -> 307 us (0.975); the launches traced: 310 us -> 306 us
  local copies, waits for them, and re-layouts: 38.1 us -> 29.6 us
  waiting for transfers between devices: 85.2 us -> 88.5 us
    slice x2 -> x0, local copies, waits for them, and re-layouts: 8.6 us -> none  [the longest x1 4.33 us: shards(): sink_kv[count:]]
  transfers between devices with their start and end apart: 6 -> 6, of which waited for: 3 -> 4; matrix products, arithmetic and copies ran while one was open for 14% -> 13% of each run, Pallas kernels for 15% -> 15%
where the time goes in v9:
time: 307 us; the launch traced here: 306 us
  waiting for transfers between devices  88.5 us (29%)
  Pallas kernels  72.4 us (24%)
  blocking collectives  59 us (19%)
  local copies, waits for them, and re-layouts  29.6 us (10%)
  matrix products  23.2 us (8%)
  starting transfers between devices  23 us (7%)
  other arithmetic  9.33 us (3%)
    all_to_all x1, blocking collectives, exchange(): spread = lax.all_to_all(data, FRAME_AXES, 0, 0, tiled=True)  59 us
    all_to_all x1, waiting for transfers between devices, exchange(): prev_full = lax.all_to_all(before, FRAME_AXES, 0, 0, tiled=True)  49.5 us
    pallas_call x2, Pallas kernels, sink_attention(): pl.pallas_call(sink_kernel, grid_spec=grid_spec, out_shape=jax.ShapeDtype...  36.7 us
    ppermute x2, waiting for transfers between devices, head_reduce(): got = lax.ppermute(send, 'xl', [(0, 1), (1, 0)])  36.3 us
    pallas_call x1, Pallas kernels, near_attention(): pl.pallas_call(near_kernel, grid_spec=grid_spec, out_shape=[f32] * 3, cos...  28 us
    dot_general x2, matrix products, head_reduce(): jnp.einsum('rk,xkn->xrn', attended, other_w, preferred_element_type=jnp.f...  12.4 us
    dot_general x2, matrix products, head_reduce(): jnp.einsum('rk,xkn->xrn', attended, mine_w, preferred_element_type=jnp.fl...  10.8 us
    all_to_all x1, starting transfers between devices, exchange(): return (prev_full, lax.all_to_all(copies, FRAME_AXES, 0, 0, tiled=True))  9.87 us
  transfers between devices with their start and end apart: 6, of which 4 were waited for; matrix products, arithmetic and copies ran while one was open for 13% of the time, Pallas kernels for 15%

profile of v9, /device:TPU:1, one launch (start us, length us, event | category | flops | bytes accessed | tf_op | source)
XLA Modules:
  0.0 306.0 jit_solution(4976039113699927237)
XLA Ops:
  0.7 0.6 fusion.20.swap_ref
  1.3 0.8 fusion.21
  2.1 0.3 copy.24
  2.5 0.3 reshape.409
  2.7 0.9 copy.26.sin_ref.sq
  3.7 0.3 copy.23
  4.0 0.0 copy-start.6
  4.0 0.3 reshape.408
  4.3 1.0 copy.25.cos_ref.cq
  5.3 7.7 %shard_map.64.ks_ref = bf16[768,1280]{1,0:T(8,128)(2,1)} custom-call(bf16[768,1280]{1,0:T(8,128)(2,1)} %x_ref.1, bf16[128,128]{1,0:T(8,128)(2,1)} %fusion.20.swap_ref, f32[768,128]{1,0:T(8,128)} %copy.25.cos_ref.cq, f32[768,128]{1,0:T(8,128)} %copy.26.sin_ref.sq), custom_call_target="tpu_custom_call" | custom-call | flops 251658240 | bytes 3932160 | tf_op jit(solution)/shard_map/pallas_call | solution.py:180
  12.9 1.8 pad_maximum_fusion.6
  14.7 59.0 %all_to_all.32 = bf16[32,48,1280]{2,1,0:T(8,128)(2,1)S(1)} all-to-all(bf16[32,48,1280]{2,1,0:T(8,128)(2,1)S(1)} %bitcast.54), channel_id=1, replica_groups=mesh['z'=4,'xh'=2,'y'=4,'xl'=2,'c'=2] {'z','xh','y'}, dimensions={0} | all-to-all | bytes 7864320 | tf_op jit(solution)/shard_map/all_to_all | solution.py:121
  73.7 1.8 copy-done
  75.6 0.2 slice.17
  75.8 2.3 pad_maximum_fusion.7
  78.1 6.6 %all-to-all-start.1 = ((bf16[32,48,1280]{2,1,0:T(8,128)(2,1)}), bf16[32,48,1280]{2,1,0:T(8,128)(2,1)}, u32[]{:S(2)}, u32[]{:S(2)}) async-start(bf16[32,48,1280]{2,1,0:T(8,128)(2,1)} %pad_maximum_fusion.7), calls=%async_computation.1 | async-start | bytes 7864320 | tf_op jit(solution)/shard_map/all_to_all | solution.py:124
  84.8 0.9 constant_dynamic-slice_fusion.2
  85.7 49.5 %all-to-all-done.1 = bf16[32,48,1280]{2,1,0:T(8,128)(2,1)} async-done(((bf16[32,48,1280]{2,1,0:T(8,128)(2,1)}), bf16[32,48,1280]{2,1,0:T(8,128)(2,1)}, u32[]{:S(2)}, u32[]{:S(2)}) %all-to-all-start.1) | async-done | bytes 3932192 | tf_op jit(solution)/shard_map/all_to_all | solution.py:124
  135.2 2.2 broadcast_in_dim.64
  137.4 9.9 %all-to-all-start.2 = ((bf16[32,48,1280]{2,1,0:T(8,128)(2,1)}), bf16[32,48,1280]{2,1,0:T(8,128)(2,1)}, u32[]{:S(2)}, u32[]{:S(2)}) async-start(bf16[32,48,1280]{2,1,0:T(8,128)(2,1)} %broadcast_in_dim.64), calls=%async_computation.2 | async-start | bytes 7864320 | tf_op jit(solution)/shard_map/all_to_all | solution.py:128
  147.3 9.0 %dynamic-slice_bitcast_fusion.1 = (bf16[1,1280,1280]{2,1,0:T(8,128)(2,1)}, bf16[1,1280,1280]{2,1,0:T(8,128)(2,1)}, bf16[1280,1280]{1,0:T(8,128)(2,1)}, bf16[1280,1280]{1,0:T(8,128)(2,1)S(1)}) fusion(bf16[1280,5120]{1,0:T(8,128)(2,1)} %param.9, s32[]{:T(128)S(6)} %select_n.103, s32[]{:T(128)S(6)} %select_n.104, s32[]{:T(128)S(6)} %select_n.114, s32[]{:T(128)S(6)} %select_n.113), kind=kLoop, calls=%fused_computation.17 | loop fusion | bytes 26214416 | tf_op jit(solution)/shard_map/stack | solution.py:272
  156.3 5.7 %copy.32 = bf16[1280,1280]{0,1:T(8,128)(2,1)} copy(bf16[1280,1280]{1,0:T(8,128)(2,1)} %get-tuple-element.17) | data formatting | bytes 6553600 | tf_op jit(solution)/shard_map/dynamic_slice | solution.py:273
  162.0 3.4 %copy.31 = bf16[1280,1280]{0,1:T(8,128)(2,1)} copy(bf16[1280,1280]{1,0:T(8,128)(2,1)S(1)} %get-tuple-element.18) | data formatting | bytes 6553600 | tf_op jit(solution)/shard_map/dynamic_slice | solution.py:273
  165.4 0.6 add_convert_fusion.flags
  166.0 28.0 %shard_map.65 = (f32[768,1280]{1,0:T(8,128)}, f32[768,1280]{1,0:T(8,128)}, f32[768,1280]{1,0:T(8,128)}) custom-call(s32[2]{0:T(128)} %add_convert_fusion.flags, bf16[768,1280]{1,0:T(8,128)(2,1)} %q_ref.5, bf16[768,1280]{1,0:T(8,128)(2,1)} %shard_map.64.ks_ref, bf16[768,1280]{1,0:T(8,128)(2,1)} %vs_ref.1, bf16[1536,1280]{1,0:T(8,128)(2,1)} %bitcast.9.kp_ref.vp_ref, ...), custom_call_target="tpu_custom_call" | custom-call | flops 6039797760 | bytes 21626880 | tf_op jit(solution)/shard_map/pallas_call | solution.py:233
  194.0 2.7 all-to-all-done.2
  196.7 18.5 %shard_map.66 = bf16[384,1280]{1,0:T(8,128)(2,1)} custom-call(s32[2]{0:T(128)} %add_convert_fusion.flags, bf16[768,1280]{1,0:T(8,128)(2,1)} %q_ref.5, bf16[1536,1280]{1,0:T(8,128)(2,1)} %bitcast.11.kk_ref.vk_ref, bf16[1536,1280]{1,0:T(8,128)(2,1)} %bitcast.11.kk_ref.vk_ref, bf16[128,128]{1,0:T(8,128)(2,1)} %fusion.20.swap_ref, f32[768,128]{1,0:T(8,128)} %copy.25.cos_ref.cq, ...), custom_call_target="tpu_custom_call" | custom-call | flops 1509949440 | bytes 10813440 | tf_op jit(solution)/shard_map/pallas_call | solution.py:258
  215.2 0.0 copy-done.1
  215.2 6.2 %fusion.11 = bf16[2,384,1280]{2,1,0:T(8,128)(2,1)} fusion(bf16[1,1280,1280]{1,2,0:T(8,128)(2,1)S(1)} %bitcast.55, bf16[1,1280,1280]{1,2,0:T(8,128)(2,1)} %bitcast.57, bf16[384,1280]{1,0:T(8,128)(2,1)} %shard_map.66), kind=kOutput, calls=%fused_computation.19 | convolution fusion | flops 2520842240 | bytes 9502720 | tf_op jit(solution)/shard_map/rk,xkn->xrn/dot_general | solution.py:282
  221.4 4.3 %collective-permute-start = (bf16[2,384,1280]{2,1,0:T(8,128)(2,1)}, bf16[2,384,1280]{2,1,0:T(8,128)(2,1)}, u32[]{:S(2)}, u32[]{:S(2)}) collective-permute-start(bf16[2,384,1280]{2,1,0:T(8,128)(2,1)} %fusion.11), channel_id=1, source_target_pairs={{0,1},{1,0},{2,3},{3,2},{4,5},{5,4},{6,7},{7,6},{8,9},{9,8},{10,11... | collective-permute-start | bytes 5898248 | tf_op jit(solution)/shard_map/ppermute | solution.py:283
  225.7 18.2 %shard_map.67 = bf16[384,1280]{1,0:T(8,128)(2,1)} custom-call(s32[2]{0:T(128)} %add_convert_fusion.flags, bf16[768,1280]{1,0:T(8,128)(2,1)} %q_ref.5, bf16[1536,1280]{1,0:T(8,128)(2,1)} %bitcast.11.kk_ref.vk_ref, bf16[1536,1280]{1,0:T(8,128)(2,1)} %bitcast.11.kk_ref.vk_ref, bf16[128,128]{1,0:T(8,128)(2,1)} %fusion.20.swap_ref, f32[768,128]{1,0:T(8,128)} %copy.25.cos_ref.cq, ...), custom_call_target="tpu_custom_call" | custom-call | flops 1509949440 | bytes 10813440 | tf_op jit(solution)/shard_map/pallas_call | solution.py:258
  243.9 6.2 %fusion.10 = bf16[2,384,1280]{2,1,0:T(8,128)(2,1)} fusion(bf16[1,1280,1280]{1,2,0:T(8,128)(2,1)S(1)} %bitcast.56, bf16[1,1280,1280]{1,2,0:T(8,128)(2,1)} %bitcast.58, bf16[384,1280]{1,0:T(8,128)(2,1)} %shard_map.67), kind=kOutput, calls=%fused_computation.18 | convolution fusion | flops 2520842240 | bytes 9502720 | tf_op jit(solution)/shard_map/rk,xkn->xrn/dot_general | solution.py:282
  250.1 0.0 collective-permute-start.2
  250.1 0.0 collective-permute-done
  250.2 6.6 %fusion.5 = bf16[2,384,1280]{2,1,0:T(8,128)(2,1)S(1)} fusion(bf16[2,384,1280]{2,1,0:T(8,128)(2,1)} %collective-permute-done, bf16[1,1280,1280]{2,1,0:T(8,128)(2,1)} %get-tuple-element.16, bf16[1,1280,1280]{2,1,0:T(8,128)(2,1)} %get-tuple-element.15, bf16[384,1280]{1,0:T(8,128)(2,1)} %shard_map.66), kind=kOutput, calls=%fused_computation.11 | convolution fusion | flops 2534604800 | bytes 11468800 | tf_op jit(solution)/shard_map/rk,xkn->xrn/dot_general | solution.py:281
  256.8 1.0 dynamic-slice_bitcast_fusion.3
  257.8 2.2 collective-permute-start.1
  260.1 0.0 collective-permute-done.2
  260.1 4.2 %fusion.4 = bf16[2,384,1280]{2,1,0:T(8,128)(2,1)S(1)} fusion(bf16[2,384,1280]{2,1,0:T(8,128)(2,1)} %collective-permute-done.2, bf16[1,1280,1280]{2,1,0:T(8,128)(2,1)S(1)} %copy-done.3, bf16[1,1280,1280]{2,1,0:T(8,128)(2,1)S(1)} %copy-done.2, bf16[384,1280]{1,0:T(8,128)(2,1)S(1)} %copy-done.7), kind=kOutput, calls=%fused_computation.9 | convolution fusion | flops 2534604800 | bytes 11468800 | tf_op jit(solution)/shard_map/rk,xkn->xrn/dot_general | solution.py:281
  264.3 0.0 copy-start.4
  264.3 1.3 copy-done.4
  265.5 1.0 dynamic-slice_bitcast_fusion.2
  266.6 0.0 collective-permute-start.3
  266.6 15.4 %collective-permute-done.1 = bf16[384,1280]{1,0:T(8,128)(2,1)S(1)} collective-permute-done((bf16[384,1280]{1,0:T(8,128)(2,1)}, bf16[384,1280]{1,0:T(8,128)(2,1)S(1)}, u32[]{:S(2)}, u32[]{:S(2)}) %collective-permute-start.1) | collective-permute-done | bytes 983072 | tf_op jit(solution)/shard_map/ppermute | solution.py:287
  281.9 0.2 fusion.13
  282.2 20.9 %collective-permute-done.3 = bf16[384,1280]{1,0:T(8,128)(2,1)} collective-permute-done((bf16[384,1280]{1,0:T(8,128)(2,1)}, bf16[384,1280]{1,0:T(8,128)(2,1)}, u32[]{:S(2)}, u32[]{:S(2)}) %collective-permute-start.3) | collective-permute-done | bytes 983072 | tf_op jit(solution)/shard_map/ppermute | solution.py:287
  303.1 1.5 fusion.12
  304.6 1.4 pad_maximum_fusion.24
  (20 shorter events, 0.1 us)
Async XLA Ops:
  4.0 8.9 %copy-start.6 = (bf16[768,1280]{1,0:T(8,128)(2,1)S(1)}, bf16[768,1280]{1,0:T(8,128)(2,1)}, u32[]{:S(2)}) copy-start(bf16[768,1280]{1,0:T(8,128)(2,1)} %vs_ref.1) | copy-start | bytes 5898244
  73.7 1.9 copy-start
  78.1 6.6 %copy-start.8 = (s32[32]{0:T(128)S(1)}, s32[32]{0:T(128)}, u32[]{:S(2)}) copy-start(s32[32]{0:T(128)} %param.10) | copy-start | bytes 388
  78.1 57.1 %all-to-all-start.1 = ((bf16[32,48,1280]{2,1,0:T(8,128)(2,1)}), bf16[32,48,1280]{2,1,0:T(8,128)(2,1)}, u32[]{:S(2)}, u32[]{:S(2)}) async-start(bf16[32,48,1280]{2,1,0:T(8,128)(2,1)} %pad_maximum_fusion.7), calls=%async_computation.1 | async-start | bytes 7864320 | tf_op jit(solution)/shard_map/all_to_all | solution.py:124
  137.4 59.3 %all-to-all-start.2 = ((bf16[32,48,1280]{2,1,0:T(8,128)(2,1)}), bf16[32,48,1280]{2,1,0:T(8,128)(2,1)}, u32[]{:S(2)}, u32[]{:S(2)}) async-start(bf16[32,48,1280]{2,1,0:T(8,128)(2,1)} %broadcast_in_dim.64), calls=%async_computation.2 | async-start | bytes 7864320 | tf_op jit(solution)/shard_map/all_to_all | solution.py:128
  196.7 18.5 %copy-start.1 = (bf16[1280,1280]{0,1:T(8,128)(2,1)S(1)}, bf16[1280,1280]{0,1:T(8,128)(2,1)}, u32[]{:S(2)}) copy-start(bf16[1280,1280]{0,1:T(8,128)(2,1)} %copy.32) | copy-start | bytes 9830404
  221.4 28.7 %collective-permute-start = (bf16[2,384,1280]{2,1,0:T(8,128)(2,1)}, bf16[2,384,1280]{2,1,0:T(8,128)(2,1)}, u32[]{:S(2)}, u32[]{:S(2)}) collective-permute-start(bf16[2,384,1280]{2,1,0:T(8,128)(2,1)} %fusion.11), channel_id=1, source_target_pairs={{0,1},{1,0},{2,3},{3,2},{4,5},{5,4},{6,7},{7,6},{8,9},{9,8},{10,11... | collective-permute-start | bytes 5898248 | tf_op jit(solution)/shard_map/ppermute | solution.py:283
  250.1 9.9 %collective-permute-start.2 = (bf16[2,384,1280]{2,1,0:T(8,128)(2,1)}, bf16[2,384,1280]{2,1,0:T(8,128)(2,1)}, u32[]{:S(2)}, u32[]{:S(2)}) collective-permute-start(bf16[2,384,1280]{2,1,0:T(8,128)(2,1)} %fusion.10), channel_id=1, source_target_pairs={{0,1},{1,0},{2,3},{3,2},{4,5},{5,4},{6,7},{7,6},{8,9},{9,8},{10,11... | collective-permute-start | bytes 5898248 | tf_op jit(solution)/shard_map/ppermute | solution.py:283
  250.1 9.9 %copy-start.2 = (bf16[1,1280,1280]{2,1,0:T(8,128)(2,1)S(1)}, bf16[1,1280,1280]{2,1,0:T(8,128)(2,1)}, u32[]{:S(2)}) copy-start(bf16[1,1280,1280]{2,1,0:T(8,128)(2,1)} %get-tuple-element.15) | copy-start | bytes 9830404
  250.2 9.9 %copy-start.3 = (bf16[1,1280,1280]{2,1,0:T(8,128)(2,1)S(1)}, bf16[1,1280,1280]{2,1,0:T(8,128)(2,1)}, u32[]{:S(2)}) copy-start(bf16[1,1280,1280]{2,1,0:T(8,128)(2,1)} %get-tuple-element.16) | copy-start | bytes 9830404
  250.2 9.9 %copy-start.7 = (bf16[384,1280]{1,0:T(8,128)(2,1)S(1)}, bf16[384,1280]{1,0:T(8,128)(2,1)}, u32[]{:S(2)}) copy-start(bf16[384,1280]{1,0:T(8,128)(2,1)} %shard_map.67) | copy-start | bytes 2949124
  257.8 24.1 %collective-permute-start.1 = (bf16[384,1280]{1,0:T(8,128)(2,1)}, bf16[384,1280]{1,0:T(8,128)(2,1)S(1)}, u32[]{:S(2)}, u32[]{:S(2)}) collective-permute-start(bf16[384,1280]{1,0:T(8,128)(2,1)} %dynamic-slice_bitcast_fusion.3), channel_id=1, source_target_pairs={{0,2},{2,0},{1,3},{3,1},{4,6},{6,4},{5,7},{7,5},{8,10},{10,8},{9,1... | collective-permute-start | bytes 2949128 | tf_op jit(solution)/shard_map/ppermute | solution.py:287
  264.3 1.3 copy-start.4
  266.6 36.6 %collective-permute-start.3 = (bf16[384,1280]{1,0:T(8,128)(2,1)}, bf16[384,1280]{1,0:T(8,128)(2,1)}, u32[]{:S(2)}, u32[]{:S(2)}) collective-permute-start(bf16[384,1280]{1,0:T(8,128)(2,1)} %dynamic-slice_bitcast_fusion.2), channel_id=1, source_target_pairs={{0,2},{2,0},{1,3},{3,1},{4,6},{6,4},{5,7},{7,5},{8,10},{10,8},{9,1... | collective-permute-start | bytes 2949128 | tf_op jit(solution)/shard_map/ppermute | solution.py:287
  266.6 36.6 %copy-start.5 = (bf16[2,384,1280]{2,1,0:T(8,128)(2,1)S(1)}, bf16[2,384,1280]{2,1,0:T(8,128)(2,1)}, u32[]{:S(2)}) copy-start(bf16[2,384,1280]{2,1,0:T(8,128)(2,1)} %copy-done.4) | copy-start | bytes 5898244

commit v10 on v9

--- a/solution.py
+++ b/solution.py
@@ -115,7 +115,7 @@
     return jnp.concatenate([out0, out1], axis=0)
 
 
-def exchange(data, sink):
+def exchange(data, sink, early):
     n_frame = lax.axis_size(FRAME_AXES)
     piece = data.shape[0] // n_frame
     spread = lax.all_to_all(data, FRAME_AXES, 0, 0, tiled=True)
@@ -124,8 +124,8 @@
     prev_full = lax.all_to_all(before, FRAME_AXES, 0, 0, tiled=True)
     mine = lax.dynamic_slice_in_dim(spread, sink * piece, piece, axis=0)
     copies = jnp.broadcast_to(mine[None], (n_frame,) + mine.shape).reshape(data.shape)
-    copies, prev_full = lax.optimization_barrier((copies, prev_full))
-    return prev_full, lax.all_to_all(copies, FRAME_AXES, 0, 0, tiled=True)
+    copies, prev_full, early = lax.optimization_barrier((copies, prev_full, early))
+    return prev_full, lax.all_to_all(copies, FRAME_AXES, 0, 0, tiled=True), early
 
 
 def rope_tables(frame_value, count):
@@ -295,13 +295,14 @@
     sink = sink_owner[0] % (n_frame // 2)
     own_tables = rope_tables(frame_pos[0], count)
     rot_k = rope(keys, own_tables)
-    prev_kv, sink_kv = exchange(jnp.concatenate([rot_k, values], axis=0), sink)
+    prev_kv, sink_kv, (mine_w, other_w) = exchange(
+        jnp.concatenate([rot_k, values], axis=0), sink, weight_blocks(out_weight)
+    )
     prev_used = (place >= 1) & (place - 1 != sink)
     sink_used = sink < place
     flags = jnp.stack([prev_used, sink_used]).astype(jnp.int32)
     near = near_attention(flags, queries, (rot_k, values, prev_kv, prev_kv), own_tables)
     halves = 2
-    mine_w, other_w = weight_blocks(out_weight)
     outs = []
     for half in range(halves):
         attended = sink_attention(flags, queries, (sink_kv, sink_kv), own_tables, near, half, halves)

time: 307 us -> 308 us (level)
  local copies, waits for them, and re-layouts: 29.6 us -> 15.6 us
  waiting for transfers between devices: 88.5 us -> 96 us
  other arithmetic: 9.33 us -> 15.6 us
    all_to_all x1, waiting for transfers between devices: 2.72 us -> 20.9 us  [exchange(): lax.all_to_all(copies, FRAME_AXES, 0, 0, tiled=True)]
    all_to_all x1, waiting for transfers between devices: 49.5 us -> 39.1 us  [exchange(): prev_full = lax.all_to_all(before, FRAME_AXES, 0, 0, tiled=True)]
    dynamic_slice x2 -> x0, local copies, waits for them, and re-layouts: 9.08 us -> none  [columns(): lax.dynamic_slice_in_dim(out_weight, (x * n_c + core) * block, block, axi...]
    another operation x0 -> x1, other arithmetic: none -> 5.16 us  [columns(): jnp.stack([lax.dynamic_slice_in_dim(out_weight, (x * n_c + core) * block,...]
    another operation x1, local copies, waits for them, and re-layouts: 8.96 us -> 5.28 us  [columns(): jnp.stack([lax.dynamic_slice_in_dim(out_weight, (x * n_c + core) * block,...]
  transfers between devices with their start and end apart: 6 -> 6, of which waited for: 4 -> 4; matrix products, arithmetic and copies ran while one was open for 13% -> 11% of each run, Pallas kernels for 15% -> 15%
where the time goes in v10:
time: 308 us; the launch traced here: 307 us
  waiting for transfers between devices  96 us (31%)
  Pallas kernels  72.1 us (23%)
  blocking collectives  59 us (19%)
  matrix products  24.8 us (8%)
  starting transfers between devices  22.7 us (7%)
  other arithmetic  15.6 us (5%)
  local copies, waits for them, and re-layouts  15.6 us (5%)
    all_to_all x1, blocking collectives, exchange(): spread = lax.all_to_all(data, FRAME_AXES, 0, 0, tiled=True)  59 us
    all_to_all x1, waiting for transfers between devices, exchange(): prev_full = lax.all_to_all(before, FRAME_AXES, 0, 0, tiled=True)  39.1 us
    pallas_call x2, Pallas kernels, sink_attention(): pl.pallas_call(sink_kernel, grid_spec=grid_spec, out_shape=jax.ShapeDtype...  36.4 us
    ppermute x2, waiting for transfers between devices, head_reduce(): got = lax.ppermute(send, 'xl', [(0, 1), (1, 0)])  36 us
    pallas_call x1, Pallas kernels, near_attention(): pl.pallas_call(near_kernel, grid_spec=grid_spec, out_shape=[f32] * 3, cos...  28 us
    all_to_all x1, waiting for transfers between devices, exchange(): lax.all_to_all(copies, FRAME_AXES, 0, 0, tiled=True)  20.9 us
    dot_general x2, matrix products, head_reduce(): jnp.einsum('rk,xkn->xrn', attended, other_w, preferred_element_type=jnp.f...  14.4 us
    dot_general x2, matrix products, head_reduce(): jnp.einsum('rk,xkn->xrn', attended, mine_w, preferred_element_type=jnp.fl...  10.4 us
  transfers between devices with their start and end apart: 6, of which 4 were waited for; matrix products, arithmetic and copies ran while one was open for 11% of the time, Pallas kernels for 15%

profile of v10, /device:TPU:1, one launch (start us, length us, event | category | flops | bytes accessed | tf_op | source)
XLA Modules:
  0.0 306.8 jit_solution(18151764469855083109)
XLA Ops:
  0.7 0.8 fusion.13
  1.5 0.3 copy.22
  1.8 0.3 reshape.409
  2.1 0.9 copy.24.sin_ref.sq
  3.1 0.3 copy.21
  3.4 0.3 reshape.408
  3.7 0.9 copy.23.cos_ref.cq
  4.6 0.6 fusion.12.swap_ref
  5.2 7.7 %shard_map.64.ks_ref = bf16[768,1280]{1,0:T(8,128)(2,1)} custom-call(bf16[768,1280]{1,0:T(8,128)(2,1)} %x_ref.1, bf16[128,128]{1,0:T(8,128)(2,1)} %fusion.12.swap_ref, f32[768,128]{1,0:T(8,128)} %copy.23.cos_ref.cq, f32[768,128]{1,0:T(8,128)} %copy.24.sin_ref.sq), custom_call_target="tpu_custom_call" | custom-call | flops 251658240 | bytes 3932160 | tf_op jit(solution)/shard_map/pallas_call | solution.py:180
  12.9 0.0 copy-done.3
  12.9 1.8 pad_maximum_fusion.2
  14.7 59.0 %all_to_all.32 = bf16[32,48,1280]{2,1,0:T(8,128)(2,1)S(1)} all-to-all(bf16[32,48,1280]{2,1,0:T(8,128)(2,1)S(1)} %bitcast.60), channel_id=1, replica_groups=mesh['z'=4,'xh'=2,'y'=4,'xl'=2,'c'=2] {'z','xh','y'}, dimensions={0} | all-to-all | bytes 7864320 | tf_op jit(solution)/shard_map/all_to_all | solution.py:121
  73.7 0.2 slice.17
  73.9 1.6 copy-done
  75.6 2.2 pad_maximum_fusion.3
  77.8 6.6 %all-to-all-start.1 = ((bf16[32,48,1280]{2,1,0:T(8,128)(2,1)}), bf16[32,48,1280]{2,1,0:T(8,128)(2,1)}, u32[]{:S(2)}, u32[]{:S(2)}) async-start(bf16[32,48,1280]{2,1,0:T(8,128)(2,1)} %pad_maximum_fusion.3), calls=%async_computation.1 | async-start | bytes 7864320 | tf_op jit(solution)/shard_map/all_to_all | solution.py:124
  84.4 0.0 copy-done.6
  84.5 5.3 %dynamic-slice_bitcast_fusion.1 = (bf16[1,1280,1280]{2,1,0:T(8,128)(2,1)S(1)}, bf16[1,1280,1280]{2,1,0:T(8,128)(2,1)S(1)}, bf16[1,1280,1280]{2,1,0:T(8,128)(2,1)S(1)}, bf16[1,1280,1280]{2,1,0:T(8,128)(2,1)S(1)}) fusion(bf16[1280,5120]{1,0:T(8,128)(2,1)} %param.9, s32[]{:T(128)S(6)} %select_n.113, s32[]{:T(128)S(6)} %select_n.112, s32[]{:T(128)S(6)} %select_n.111, ...), kind=kLoop, calls=%fused_computation.13 | loop fusion | bytes 26214416 | tf_op jit(solution)/shard_map/stack | solution.py:272
  89.8 5.2 %pad_maximum_fusion = (bf16[2,1280,1280]{2,1,0:T(8,128)(2,1)}, bf16[2,1280,1280]{2,1,0:T(8,128)(2,1)}) fusion(bf16[1,1280,1280]{2,1,0:T(8,128)(2,1)S(1)} %get-tuple-element.20, bf16[1,1280,1280]{2,1,0:T(8,128)(2,1)S(1)} %get-tuple-element.21, bf16[1,1280,1280]{2,1,0:T(8,128)(2,1)S(1)} %get-tuple-element.22, bf16[1,1280,1280]{2,1,0:T(8,128)(2,1)S(1)} %get-tuple-element.19), kind=kLoop, calls=%fused_computation | loop fusion | flops 6553600 | bytes 26214400 | tf_op jit(solution)/shard_map/stack | solution.py:272
  95.0 0.9 constant_dynamic-slice_fusion
  95.9 39.1 %all-to-all-done.1 = bf16[32,48,1280]{2,1,0:T(8,128)(2,1)} async-done(((bf16[32,48,1280]{2,1,0:T(8,128)(2,1)}), bf16[32,48,1280]{2,1,0:T(8,128)(2,1)}, u32[]{:S(2)}, u32[]{:S(2)}) %all-to-all-start.1) | async-done | bytes 3932192 | tf_op jit(solution)/shard_map/all_to_all | solution.py:124
  134.9 2.1 broadcast_in_dim.64
  137.1 9.7 %all-to-all-start.2 = ((bf16[32,48,1280]{2,1,0:T(8,128)(2,1)}), bf16[32,48,1280]{2,1,0:T(8,128)(2,1)}, u32[]{:S(2)}, u32[]{:S(2)}) async-start(bf16[32,48,1280]{2,1,0:T(8,128)(2,1)} %broadcast_in_dim.64), calls=%async_computation.2 | async-start | bytes 7864320 | tf_op jit(solution)/shard_map/all_to_all | solution.py:128
  146.8 0.7 add_convert_fusion.flags
  147.5 28.0 %shard_map.65 = (f32[768,1280]{1,0:T(8,128)}, f32[768,1280]{1,0:T(8,128)}, f32[768,1280]{1,0:T(8,128)}) custom-call(s32[2]{0:T(128)} %add_convert_fusion.flags, bf16[768,1280]{1,0:T(8,128)(2,1)} %q_ref.5, bf16[768,1280]{1,0:T(8,128)(2,1)} %shard_map.64.ks_ref, bf16[768,1280]{1,0:T(8,128)(2,1)} %vs_ref.1, bf16[1536,1280]{1,0:T(8,128)(2,1)} %bitcast.5.kp_ref.vp_ref, ...), custom_call_target="tpu_custom_call" | custom-call | flops 6039797760 | bytes 21626880 | tf_op jit(solution)/shard_map/pallas_call | solution.py:233
  175.5 20.9 %all-to-all-done.2 = bf16[32,48,1280]{2,1,0:T(8,128)(2,1)} async-done(((bf16[32,48,1280]{2,1,0:T(8,128)(2,1)}), bf16[32,48,1280]{2,1,0:T(8,128)(2,1)}, u32[]{:S(2)}, u32[]{:S(2)}) %all-to-all-start.2) | async-done | bytes 3932192 | tf_op jit(solution)/shard_map/all_to_all | solution.py:128
  196.4 18.2 %shard_map.66 = bf16[384,1280]{1,0:T(8,128)(2,1)} custom-call(s32[2]{0:T(128)} %add_convert_fusion.flags, bf16[768,1280]{1,0:T(8,128)(2,1)} %q_ref.5, bf16[1536,1280]{1,0:T(8,128)(2,1)} %bitcast.13.kk_ref.vk_ref, bf16[1536,1280]{1,0:T(8,128)(2,1)} %bitcast.13.kk_ref.vk_ref, bf16[128,128]{1,0:T(8,128)(2,1)} %fusion.12.swap_ref, f32[768,128]{1,0:T(8,128)} %copy.23.cos_ref.cq, ...), custom_call_target="tpu_custom_call" | custom-call | flops 1509949440 | bytes 10813440 | tf_op jit(solution)/shard_map/pallas_call | solution.py:258
  214.5 7.2 %fusion.2 = bf16[2,384,1280]{2,1,0:T(8,128)(2,1)} fusion(bf16[2,1280,1280]{2,1,0:T(8,128)(2,1)} %get-tuple-element.18, bf16[384,1280]{1,0:T(8,128)(2,1)} %shard_map.66), kind=kOutput, calls=%fused_computation.16 | convolution fusion | flops 2517565440 | bytes 9502720 | tf_op jit(solution)/shard_map/rk,xkn->xrn/dot_general | solution.py:282
  221.7 4.3 %collective-permute-start = (bf16[2,384,1280]{2,1,0:T(8,128)(2,1)}, bf16[2,384,1280]{2,1,0:T(8,128)(2,1)}, u32[]{:S(2)}, u32[]{:S(2)}) collective-permute-start(bf16[2,384,1280]{2,1,0:T(8,128)(2,1)} %fusion.2), channel_id=1, source_target_pairs={{0,1},{1,0},{2,3},{3,2},{4,5},{5,4},{6,7},{7,6},{8,9},{9,8},{10,11... | collective-permute-start | bytes 5898248 | tf_op jit(solution)/shard_map/ppermute | solution.py:283
  226.0 18.2 %shard_map.67 = bf16[384,1280]{1,0:T(8,128)(2,1)} custom-call(s32[2]{0:T(128)} %add_convert_fusion.flags, bf16[768,1280]{1,0:T(8,128)(2,1)} %q_ref.5, bf16[1536,1280]{1,0:T(8,128)(2,1)} %bitcast.13.kk_ref.vk_ref, bf16[1536,1280]{1,0:T(8,128)(2,1)} %bitcast.13.kk_ref.vk_ref, bf16[128,128]{1,0:T(8,128)(2,1)} %fusion.12.swap_ref, f32[768,128]{1,0:T(8,128)} %copy.23.cos_ref.cq, ...), custom_call_target="tpu_custom_call" | custom-call | flops 1509949440 | bytes 10813440 | tf_op jit(solution)/shard_map/pallas_call | solution.py:258
  244.2 7.2 %fusion.3 = bf16[2,384,1280]{2,1,0:T(8,128)(2,1)} fusion(bf16[2,1280,1280]{2,1,0:T(8,128)(2,1)} %get-tuple-element.18, bf16[384,1280]{1,0:T(8,128)(2,1)} %shard_map.67), kind=kOutput, calls=%fused_computation.17 | convolution fusion | flops 2517565440 | bytes 9502720 | tf_op jit(solution)/shard_map/rk,xkn->xrn/dot_general | solution.py:282
  251.4 0.0 collective-permute-start.2
  251.5 0.0 collective-permute-done
  251.5 6.3 %fusion.1 = bf16[2,384,1280]{2,1,0:T(8,128)(2,1)S(1)} fusion(bf16[2,384,1280]{2,1,0:T(8,128)(2,1)} %collective-permute-done, bf16[2,1280,1280]{2,1,0:T(8,128)(2,1)} %get-tuple-element.12, bf16[384,1280]{1,0:T(8,128)(2,1)S(1)} %copy-done.5), kind=kOutput, calls=%fused_computation.7 | convolution fusion | flops 2521497600 | bytes 11468800 | tf_op jit(solution)/shard_map/rk,xkn->xrn/dot_general | solution.py:281
  257.7 0.0 copy-start.1
  257.8 1.1 dynamic-slice_bitcast_fusion.5
  258.9 2.1 collective-permute-start.1
  261.0 0.0 collective-permute-done.2
  261.0 4.2 %fusion = bf16[2,384,1280]{2,1,0:T(8,128)(2,1)S(1)} fusion(bf16[2,384,1280]{2,1,0:T(8,128)(2,1)} %collective-permute-done.2, bf16[2,1280,1280]{2,1,0:T(8,128)(2,1)S(1)} %bitcast.62, bf16[384,1280]{1,0:T(8,128)(2,1)S(1)} %copy-done.4), kind=kOutput, calls=%fused_computation.5 | convolution fusion | flops 2521497600 | bytes 11468800 | tf_op jit(solution)/shard_map/rk,xkn->xrn/dot_general | solution.py:281
  265.2 0.0 copy-start.2
  265.2 0.1 dynamic-slice_bitcast_fusion.4
  265.3 1.2 copy-done.2
  266.5 0.0 collective-permute-start.3
  266.5 16.4 %collective-permute-done.1 = bf16[384,1280]{1,0:T(8,128)(2,1)S(1)} collective-permute-done((bf16[384,1280]{1,0:T(8,128)(2,1)}, bf16[384,1280]{1,0:T(8,128)(2,1)S(1)}, u32[]{:S(2)}, u32[]{:S(2)}) %collective-permute-start.1) | collective-permute-done | bytes 983072 | tf_op jit(solution)/shard_map/ppermute | solution.py:287
  282.9 1.4 fusion.5
  284.3 19.6 %collective-permute-done.3 = bf16[384,1280]{1,0:T(8,128)(2,1)S(1)} collective-permute-done((bf16[384,1280]{1,0:T(8,128)(2,1)S(1)}, bf16[384,1280]{1,0:T(8,128)(2,1)S(1)}, u32[]{:S(2)}, u32[]{:S(2)}) %collective-permute-start.3) | collective-permute-done | bytes 983072 | tf_op jit(solution)/shard_map/ppermute | solution.py:287
  304.0 1.4 fusion.4
  305.4 1.4 pad_maximum_fusion.4
  (20 shorter events, 0.1 us)
Async XLA Ops:
  3.1 9.8 %copy-start.3 = (bf16[768,1280]{1,0:T(8,128)(2,1)S(1)}, bf16[768,1280]{1,0:T(8,128)(2,1)}, u32[]{:S(2)}) copy-start(bf16[768,1280]{1,0:T(8,128)(2,1)} %vs_ref.1) | copy-start | bytes 5898244
  73.7 1.9 copy-start
  77.8 6.6 %copy-start.6 = (s32[32]{0:T(128)S(1)}, s32[32]{0:T(128)}, u32[]{:S(2)}) copy-start(s32[32]{0:T(128)} %param.10) | copy-start | bytes 388
  77.8 57.1 %all-to-all-start.1 = ((bf16[32,48,1280]{2,1,0:T(8,128)(2,1)}), bf16[32,48,1280]{2,1,0:T(8,128)(2,1)}, u32[]{:S(2)}, u32[]{:S(2)}) async-start(bf16[32,48,1280]{2,1,0:T(8,128)(2,1)} %pad_maximum_fusion.3), calls=%async_computation.1 | async-start | bytes 7864320 | tf_op jit(solution)/shard_map/all_to_all | solution.py:124
  137.1 59.3 %all-to-all-start.2 = ((bf16[32,48,1280]{2,1,0:T(8,128)(2,1)}), bf16[32,48,1280]{2,1,0:T(8,128)(2,1)}, u32[]{:S(2)}, u32[]{:S(2)}) async-start(bf16[32,48,1280]{2,1,0:T(8,128)(2,1)} %broadcast_in_dim.64), calls=%async_computation.2 | async-start | bytes 7864320 | tf_op jit(solution)/shard_map/all_to_all | solution.py:128
  221.7 29.8 %collective-permute-start = (bf16[2,384,1280]{2,1,0:T(8,128)(2,1)}, bf16[2,384,1280]{2,1,0:T(8,128)(2,1)}, u32[]{:S(2)}, u32[]{:S(2)}) collective-permute-start(bf16[2,384,1280]{2,1,0:T(8,128)(2,1)} %fusion.2), channel_id=1, source_target_pairs={{0,1},{1,0},{2,3},{3,2},{4,5},{5,4},{6,7},{7,6},{8,9},{9,8},{10,11... | collective-permute-start | bytes 5898248 | tf_op jit(solution)/shard_map/ppermute | solution.py:283
  244.2 7.2 %copy-start.5 = (bf16[384,1280]{1,0:T(8,128)(2,1)S(1)}, bf16[384,1280]{1,0:T(8,128)(2,1)}, u32[]{:S(2)}) copy-start(bf16[384,1280]{1,0:T(8,128)(2,1)} %shard_map.66) | copy-start | bytes 2949124
  251.4 9.6 %collective-permute-start.2 = (bf16[2,384,1280]{2,1,0:T(8,128)(2,1)}, bf16[2,384,1280]{2,1,0:T(8,128)(2,1)}, u32[]{:S(2)}, u32[]{:S(2)}) collective-permute-start(bf16[2,384,1280]{2,1,0:T(8,128)(2,1)} %fusion.3), channel_id=1, source_target_pairs={{0,1},{1,0},{2,3},{3,2},{4,5},{5,4},{6,7},{7,6},{8,9},{9,8},{10,11... | collective-permute-start | bytes 5898248 | tf_op jit(solution)/shard_map/ppermute | solution.py:283
  251.4 9.6 %slice-start = ((s8[6553600]{0:T(1024)(128)(4,1)}), s8[2359296]{0:T(1024)(128)(4,1)S(1)}, s32[]{:S(2)}) async-start(s8[6553600]{0:T(1024)(128)(4,1)} %bitcast.61), calls=%async_computation.3 | async-start | bytes 4718592
  251.4 9.6 %slice-start.1 = ((s8[6553600]{0:T(1024)(128)(4,1)}), s8[4194304]{0:T(1024)(128)(4,1)S(1)}, s32[]{:S(2)}) async-start(s8[6553600]{0:T(1024)(128)(4,1)} %bitcast.61), calls=%async_computation.4 | async-start | bytes 8388608
  251.4 9.6 %copy-start.4 = (bf16[384,1280]{1,0:T(8,128)(2,1)S(1)}, bf16[384,1280]{1,0:T(8,128)(2,1)}, u32[]{:S(2)}) copy-start(bf16[384,1280]{1,0:T(8,128)(2,1)} %shard_map.67) | copy-start | bytes 2949124
  257.7 7.5 %copy-start.1 = (bf16[2,384,1280]{2,1,0:T(8,128)(2,1)}, bf16[2,384,1280]{2,1,0:T(8,128)(2,1)S(1)}, u32[]{:S(2)}) copy-start(bf16[2,384,1280]{2,1,0:T(8,128)(2,1)S(1)} %fusion.1) | copy-start | bytes 5898244
  258.9 24.0 %collective-permute-start.1 = (bf16[384,1280]{1,0:T(8,128)(2,1)}, bf16[384,1280]{1,0:T(8,128)(2,1)S(1)}, u32[]{:S(2)}, u32[]{:S(2)}) collective-permute-start(bf16[384,1280]{1,0:T(8,128)(2,1)} %dynamic-slice_bitcast_fusion.5), channel_id=1, source_target_pairs={{0,2},{2,0},{1,3},{3,1},{4,6},{6,4},{5,7},{7,5},{8,10},{10,8},{9,1... | collective-permute-start | bytes 2949128 | tf_op jit(solution)/shard_map/ppermute | solution.py:287
  265.2 1.3 copy-start.2
  266.5 37.5 %collective-permute-start.3 = (bf16[384,1280]{1,0:T(8,128)(2,1)S(1)}, bf16[384,1280]{1,0:T(8,128)(2,1)S(1)}, u32[]{:S(2)}, u32[]{:S(2)}) collective-permute-start(bf16[384,1280]{1,0:T(8,128)(2,1)S(1)} %dynamic-slice_bitcast_fusion.4), channel_id=1, source_target_pairs={{0,2},{2,0},{1,3},{3,1},{4,6},{6,4},{5,7},{7,5},{8,10},{10,8},{9,1... | collective-permute-start | bytes 2949128 | tf_op jit(solution)/shard_map/ppermute | solution.py:287

commit v11 on v9

--- a/solution.py
+++ b/solution.py
@@ -189,16 +189,18 @@
 
 def sink_kernel(flags, q_ref, kk_ref, vk_ref, swap_ref, cq, sq, m_ref, l_ref, o_ref, out_ref):
     swap = swap_ref[...]
-    q = rotate_ref(q_ref, cq, sq, swap)
-    m_sink, l_sink, o_sink = attend_ref(q, kk_ref[...], vk_ref)
     sink_used = flags[1] != 0
-    m_near = m_ref[:, :1]
-    top = jnp.maximum(m_near, jnp.where(sink_used, m_sink, m_near))
-    c_near = jnp.exp(m_near - top)
-    c_sink = jnp.where(sink_used, jnp.exp(m_sink - top), 0.0)
-    numer = o_ref[...] * c_near + o_sink * c_sink
-    denom = l_ref[:, :1] * c_near + l_sink * c_sink
-    out_ref[...] = (numer / denom).astype(out_ref.dtype)
+    for j in range(q_ref.shape[1] // HDIM):
+        cols = slice(j * HDIM, (j + 1) * HDIM)
+        q = rotate_ref(q_ref.at[:, cols], cq, sq, swap)
+        m_sink, l_sink, o_sink = attend_ref(q, kk_ref[:, cols], vk_ref.at[:, cols])
+        m_near = m_ref[:, j * HDIM : j * HDIM + 1]
+        top = jnp.maximum(m_near, jnp.where(sink_used, m_sink, m_near))
+        c_near = jnp.exp(m_near - top)
+        c_sink = jnp.where(sink_used, jnp.exp(m_sink - top), 0.0)
+        numer = o_ref[:, cols] * c_near + o_sink * c_sink
+        denom = l_ref[:, j * HDIM : j * HDIM + 1] * c_near + l_sink * c_sink
+        out_ref[:, cols] = (numer / denom).astype(out_ref.dtype)
 
 
 def specs(count):
@@ -237,22 +239,24 @@
 
 def sink_attention(flags, queries, blocks, tables, near, half, halves):
     count, width = queries.shape
-    heads_here = width // HDIM
+    group = 2
+    heads_here = width // HDIM // group
     rows = count // halves
-    part = pl.BlockSpec((rows, HDIM), lambda h, flags: (half, h))
+    wide = group * HDIM
+    part = pl.BlockSpec((rows, wide), lambda h, flags: (half, h))
     part_table = pl.BlockSpec((rows, HDIM), lambda h, flags: (half, 0))
-    key_spec = pl.BlockSpec((count, HDIM), lambda h, flags: (0, h))
-    value_spec = pl.BlockSpec((count, HDIM), lambda h, flags: (1, h))
+    key_spec = pl.BlockSpec((count, wide), lambda h, flags: (0, h))
+    value_spec = pl.BlockSpec((count, wide), lambda h, flags: (1, h))
     swap = pl.BlockSpec((HDIM, HDIM), lambda h, flags: (0, 0))
     grid_spec = pltpu.PrefetchScalarGridSpec(
         num_scalar_prefetch=1,
         grid=(heads_here,),
         in_specs=[part, key_spec, value_spec, swap] + [part_table] * 2 + [part] * 3,
-        out_specs=pl.BlockSpec((rows, HDIM), lambda h, flags: (0, h)),
+        out_specs=pl.BlockSpec((rows, wide), lambda h, flags: (0, h)),
     )
     cost = pl.CostEstimate(
-        flops=heads_here * 4 * rows * count * HDIM,
-        transcendentals=heads_here * rows * count,
+        flops=heads_here * group * 4 * rows * count * HDIM,
+        transcendentals=heads_here * group * rows * count,
         bytes_accessed=(rows + 2 * count) * width * 2 + 3 * rows * width * 4,
     )
     return pl.pallas_call(

time: 307 us -> 302 us (0.984)
  Pallas kernels: 72.4 us -> 67.2 us
    pallas_call x2, Pallas kernels: 36.7 us -> 31.6 us  [sink_attention(): pl.pallas_call(sink_kernel, grid_spec=grid_spec, out_shape=jax.ShapeDtype...]
  transfers between devices with their start and end apart: 6 -> 6, of which waited for: 4 -> 4; matrix products, arithmetic and copies ran while one was open for 13% -> 13% of each run, Pallas kernels for 15% -> 14%
where the time goes in v11:
time: 302 us; the launch traced here: 301 us
  waiting for transfers between devices  88.5 us (29%)
  Pallas kernels  67.2 us (22%)
  blocking collectives  59 us (20%)
  local copies, waits for them, and re-layouts  29.6 us (10%)
  matrix products  23.2 us (8%)
  starting transfers between devices  23 us (8%)
  other arithmetic  9.33 us (3%)
    all_to_all x1, blocking collectives, exchange(): spread = lax.all_to_all(data, FRAME_AXES, 0, 0, tiled=True)  59 us
    all_to_all x1, waiting for transfers between devices, exchange(): prev_full = lax.all_to_all(before, FRAME_AXES, 0, 0, tiled=True)  49.5 us
    ppermute x2, waiting for transfers between devices, head_reduce(): got = lax.ppermute(send, 'xl', [(0, 1), (1, 0)])  36.3 us
    pallas_call x2, Pallas kernels, sink_attention(): pl.pallas_call(sink_kernel, grid_spec=grid_spec, out_shape=jax.ShapeDtype...  31.6 us
    pallas_call x1, Pallas kernels, near_attention(): pl.pallas_call(near_kernel, grid_spec=grid_spec, out_shape=[f32] * 3, cos...  28 us
    dot_general x2, matrix products, head_reduce(): jnp.einsum('rk,xkn->xrn', attended, other_w, preferred_element_type=jnp.f...  12.4 us
    dot_general x2, matrix products, head_reduce(): jnp.einsum('rk,xkn->xrn', attended, mine_w, preferred_element_type=jnp.fl...  10.8 us
    all_to_all x1, starting transfers between devices, exchange(): return (prev_full, lax.all_to_all(copies, FRAME_AXES, 0, 0, tiled=True))  9.87 us
  transfers between devices with their start and end apart: 6, of which 4 were waited for; matrix products, arithmetic and copies ran while one was open for 13% of the time, Pallas kernels for 14%

profile of v11, /device:TPU:1, one launch (start us, length us, event | category | flops | bytes accessed | tf_op | source)
XLA Modules:
  0.0 300.9 jit_solution(9734673759438598660)
XLA Ops:
  0.7 0.6 fusion.20.swap_ref
  1.3 0.8 fusion.21
  2.1 0.3 copy.24
  2.5 0.3 reshape.409
  2.7 0.9 copy.26.sin_ref.sq
  3.7 0.3 copy.23
  4.0 0.0 copy-start.6
  4.0 0.3 reshape.408
  4.3 1.0 copy.25.cos_ref.cq
  5.3 7.7 %shard_map.64.ks_ref = bf16[768,1280]{1,0:T(8,128)(2,1)} custom-call(bf16[768,1280]{1,0:T(8,128)(2,1)} %x_ref.1, bf16[128,128]{1,0:T(8,128)(2,1)} %fusion.20.swap_ref, f32[768,128]{1,0:T(8,128)} %copy.25.cos_ref.cq, f32[768,128]{1,0:T(8,128)} %copy.26.sin_ref.sq), custom_call_target="tpu_custom_call" | custom-call | flops 251658240 | bytes 3932160 | tf_op jit(solution)/shard_map/pallas_call | solution.py:180
  12.9 1.8 pad_maximum_fusion.6
  14.7 59.0 %all_to_all.32 = bf16[32,48,1280]{2,1,0:T(8,128)(2,1)S(1)} all-to-all(bf16[32,48,1280]{2,1,0:T(8,128)(2,1)S(1)} %bitcast.54), channel_id=1, replica_groups=mesh['z'=4,'xh'=2,'y'=4,'xl'=2,'c'=2] {'z','xh','y'}, dimensions={0} | all-to-all | bytes 7864320 | tf_op jit(solution)/shard_map/all_to_all | solution.py:121
  73.7 1.8 copy-done
  75.6 0.2 slice.17
  75.8 2.3 pad_maximum_fusion.7
  78.1 6.6 %all-to-all-start.1 = ((bf16[32,48,1280]{2,1,0:T(8,128)(2,1)}), bf16[32,48,1280]{2,1,0:T(8,128)(2,1)}, u32[]{:S(2)}, u32[]{:S(2)}) async-start(bf16[32,48,1280]{2,1,0:T(8,128)(2,1)} %pad_maximum_fusion.7), calls=%async_computation.1 | async-start | bytes 7864320 | tf_op jit(solution)/shard_map/all_to_all | solution.py:124
  84.7 0.0 copy-done.8
  84.8 0.9 constant_dynamic-slice_fusion.2
  85.7 49.5 %all-to-all-done.1 = bf16[32,48,1280]{2,1,0:T(8,128)(2,1)} async-done(((bf16[32,48,1280]{2,1,0:T(8,128)(2,1)}), bf16[32,48,1280]{2,1,0:T(8,128)(2,1)}, u32[]{:S(2)}, u32[]{:S(2)}) %all-to-all-start.1) | async-done | bytes 3932192 | tf_op jit(solution)/shard_map/all_to_all | solution.py:124
  135.2 2.2 broadcast_in_dim.64
  137.4 9.9 %all-to-all-start.2 = ((bf16[32,48,1280]{2,1,0:T(8,128)(2,1)}), bf16[32,48,1280]{2,1,0:T(8,128)(2,1)}, u32[]{:S(2)}, u32[]{:S(2)}) async-start(bf16[32,48,1280]{2,1,0:T(8,128)(2,1)} %broadcast_in_dim.64), calls=%async_computation.2 | async-start | bytes 7864320 | tf_op jit(solution)/shard_map/all_to_all | solution.py:128
  147.3 9.0 %dynamic-slice_bitcast_fusion.1 = (bf16[1,1280,1280]{2,1,0:T(8,128)(2,1)}, bf16[1,1280,1280]{2,1,0:T(8,128)(2,1)}, bf16[1280,1280]{1,0:T(8,128)(2,1)}, bf16[1280,1280]{1,0:T(8,128)(2,1)S(1)}) fusion(bf16[1280,5120]{1,0:T(8,128)(2,1)} %param.9, s32[]{:T(128)S(6)} %select_n.103, s32[]{:T(128)S(6)} %select_n.104, s32[]{:T(128)S(6)} %select_n.114, s32[]{:T(128)S(6)} %select_n.113), kind=kLoop, calls=%fused_computation.17 | loop fusion | bytes 26214416 | tf_op jit(solution)/shard_map/stack | solution.py:276
  156.3 5.7 %copy.32 = bf16[1280,1280]{0,1:T(8,128)(2,1)} copy(bf16[1280,1280]{1,0:T(8,128)(2,1)} %get-tuple-element.17) | data formatting | bytes 6553600 | tf_op jit(solution)/shard_map/dynamic_slice | solution.py:277
  162.0 3.4 %copy.31 = bf16[1280,1280]{0,1:T(8,128)(2,1)} copy(bf16[1280,1280]{1,0:T(8,128)(2,1)S(1)} %get-tuple-element.18) | data formatting | bytes 6553600 | tf_op jit(solution)/shard_map/dynamic_slice | solution.py:277
  165.4 0.6 add_convert_fusion.flags
  166.0 28.0 %shard_map.65 = (f32[768,1280]{1,0:T(8,128)}, f32[768,1280]{1,0:T(8,128)}, f32[768,1280]{1,0:T(8,128)}) custom-call(s32[2]{0:T(128)} %add_convert_fusion.flags, bf16[768,1280]{1,0:T(8,128)(2,1)} %q_ref.5, bf16[768,1280]{1,0:T(8,128)(2,1)} %shard_map.64.ks_ref, bf16[768,1280]{1,0:T(8,128)(2,1)} %vs_ref.1, bf16[1536,1280]{1,0:T(8,128)(2,1)} %bitcast.9.kp_ref.vp_ref, ...), custom_call_target="tpu_custom_call" | custom-call | flops 6039797760 | bytes 21626880 | tf_op jit(solution)/shard_map/pallas_call | solution.py:235
  194.0 2.7 all-to-all-done.2
  196.7 15.9 %shard_map.66 = bf16[384,1280]{1,0:T(8,128)(2,1)} custom-call(s32[2]{0:T(128)} %add_convert_fusion.flags, bf16[768,1280]{1,0:T(8,128)(2,1)} %q_ref.5, bf16[1536,1280]{1,0:T(8,128)(2,1)} %bitcast.11.kk_ref.vk_ref, bf16[1536,1280]{1,0:T(8,128)(2,1)} %bitcast.11.kk_ref.vk_ref, bf16[128,128]{1,0:T(8,128)(2,1)} %fusion.20.swap_ref, f32[768,128]{1,0:T(8,128)} %copy.25.cos_ref.cq, ...), custom_call_target="tpu_custom_call" | custom-call | flops 1509949440 | bytes 10813440 | tf_op jit(solution)/shard_map/pallas_call | solution.py:262
  212.7 6.2 %fusion.11 = bf16[2,384,1280]{2,1,0:T(8,128)(2,1)} fusion(bf16[1,1280,1280]{1,2,0:T(8,128)(2,1)S(1)} %bitcast.55, bf16[1,1280,1280]{1,2,0:T(8,128)(2,1)} %bitcast.57, bf16[384,1280]{1,0:T(8,128)(2,1)} %shard_map.66), kind=kOutput, calls=%fused_computation.19 | convolution fusion | flops 2520842240 | bytes 9502720 | tf_op jit(solution)/shard_map/rk,xkn->xrn/dot_general | solution.py:286
  218.9 4.3 %collective-permute-start = (bf16[2,384,1280]{2,1,0:T(8,128)(2,1)}, bf16[2,384,1280]{2,1,0:T(8,128)(2,1)}, u32[]{:S(2)}, u32[]{:S(2)}) collective-permute-start(bf16[2,384,1280]{2,1,0:T(8,128)(2,1)} %fusion.11), channel_id=1, source_target_pairs={{0,1},{1,0},{2,3},{3,2},{4,5},{5,4},{6,7},{7,6},{8,9},{9,8},{10,11... | collective-permute-start | bytes 5898248 | tf_op jit(solution)/shard_map/ppermute | solution.py:287
  223.2 15.6 %shard_map.67 = bf16[384,1280]{1,0:T(8,128)(2,1)} custom-call(s32[2]{0:T(128)} %add_convert_fusion.flags, bf16[768,1280]{1,0:T(8,128)(2,1)} %q_ref.5, bf16[1536,1280]{1,0:T(8,128)(2,1)} %bitcast.11.kk_ref.vk_ref, bf16[1536,1280]{1,0:T(8,128)(2,1)} %bitcast.11.kk_ref.vk_ref, bf16[128,128]{1,0:T(8,128)(2,1)} %fusion.20.swap_ref, f32[768,128]{1,0:T(8,128)} %copy.25.cos_ref.cq, ...), custom_call_target="tpu_custom_call" | custom-call | flops 1509949440 | bytes 10813440 | tf_op jit(solution)/shard_map/pallas_call | solution.py:262
  238.8 6.2 %fusion.10 = bf16[2,384,1280]{2,1,0:T(8,128)(2,1)} fusion(bf16[1,1280,1280]{1,2,0:T(8,128)(2,1)S(1)} %bitcast.56, bf16[1,1280,1280]{1,2,0:T(8,128)(2,1)} %bitcast.58, bf16[384,1280]{1,0:T(8,128)(2,1)} %shard_map.67), kind=kOutput, calls=%fused_computation.18 | convolution fusion | flops 2520842240 | bytes 9502720 | tf_op jit(solution)/shard_map/rk,xkn->xrn/dot_general | solution.py:286
  245.0 0.0 collective-permute-start.2
  245.0 0.0 collective-permute-done
  245.0 6.6 %fusion.5 = bf16[2,384,1280]{2,1,0:T(8,128)(2,1)S(1)} fusion(bf16[2,384,1280]{2,1,0:T(8,128)(2,1)} %collective-permute-done, bf16[1,1280,1280]{2,1,0:T(8,128)(2,1)} %get-tuple-element.16, bf16[1,1280,1280]{2,1,0:T(8,128)(2,1)} %get-tuple-element.15, bf16[384,1280]{1,0:T(8,128)(2,1)} %shard_map.66), kind=kOutput, calls=%fused_computation.11 | convolution fusion | flops 2534604800 | bytes 11468800 | tf_op jit(solution)/shard_map/rk,xkn->xrn/dot_general | solution.py:285
  251.6 1.0 dynamic-slice_bitcast_fusion.3
  252.7 2.2 collective-permute-start.1
  254.9 0.0 collective-permute-done.2
  254.9 4.2 %fusion.4 = bf16[2,384,1280]{2,1,0:T(8,128)(2,1)S(1)} fusion(bf16[2,384,1280]{2,1,0:T(8,128)(2,1)} %collective-permute-done.2, bf16[1,1280,1280]{2,1,0:T(8,128)(2,1)S(1)} %copy-done.3, bf16[1,1280,1280]{2,1,0:T(8,128)(2,1)S(1)} %copy-done.2, bf16[384,1280]{1,0:T(8,128)(2,1)S(1)} %copy-done.7), kind=kOutput, calls=%fused_computation.9 | convolution fusion | flops 2534604800 | bytes 11468800 | tf_op jit(solution)/shard_map/rk,xkn->xrn/dot_general | solution.py:285
  259.1 0.0 copy-start.4
  259.1 1.3 copy-done.4
  260.4 1.0 dynamic-slice_bitcast_fusion.2
  261.4 0.0 collective-permute-start.3
  261.4 15.4 %collective-permute-done.1 = bf16[384,1280]{1,0:T(8,128)(2,1)S(1)} collective-permute-done((bf16[384,1280]{1,0:T(8,128)(2,1)}, bf16[384,1280]{1,0:T(8,128)(2,1)S(1)}, u32[]{:S(2)}, u32[]{:S(2)}) %collective-permute-start.1) | collective-permute-done | bytes 983072 | tf_op jit(solution)/shard_map/ppermute | solution.py:291
  276.8 0.2 fusion.13
  277.0 20.9 %collective-permute-done.3 = bf16[384,1280]{1,0:T(8,128)(2,1)} collective-permute-done((bf16[384,1280]{1,0:T(8,128)(2,1)}, bf16[384,1280]{1,0:T(8,128)(2,1)}, u32[]{:S(2)}, u32[]{:S(2)}) %collective-permute-start.3) | collective-permute-done | bytes 983072 | tf_op jit(solution)/shard_map/ppermute | solution.py:291
  298.0 1.5 fusion.12
  299.4 1.4 pad_maximum_fusion.24
  (20 shorter events, 0.1 us)
Async XLA Ops:
  4.0 8.9 %copy-start.6 = (bf16[768,1280]{1,0:T(8,128)(2,1)S(1)}, bf16[768,1280]{1,0:T(8,128)(2,1)}, u32[]{:S(2)}) copy-start(bf16[768,1280]{1,0:T(8,128)(2,1)} %vs_ref.1) | copy-start | bytes 5898244
  73.7 1.9 copy-start
  78.1 6.6 %copy-start.8 = (s32[32]{0:T(128)S(1)}, s32[32]{0:T(128)}, u32[]{:S(2)}) copy-start(s32[32]{0:T(128)} %param.10) | copy-start | bytes 388
  78.1 57.1 %all-to-all-start.1 = ((bf16[32,48,1280]{2,1,0:T(8,128)(2,1)}), bf16[32,48,1280]{2,1,0:T(8,128)(2,1)}, u32[]{:S(2)}, u32[]{:S(2)}) async-start(bf16[32,48,1280]{2,1,0:T(8,128)(2,1)} %pad_maximum_fusion.7), calls=%async_computation.1 | async-start | bytes 7864320 | tf_op jit(solution)/shard_map/all_to_all | solution.py:124
  137.4 59.3 %all-to-all-start.2 = ((bf16[32,48,1280]{2,1,0:T(8,128)(2,1)}), bf16[32,48,1280]{2,1,0:T(8,128)(2,1)}, u32[]{:S(2)}, u32[]{:S(2)}) async-start(bf16[32,48,1280]{2,1,0:T(8,128)(2,1)} %broadcast_in_dim.64), calls=%async_computation.2 | async-start | bytes 7864320 | tf_op jit(solution)/shard_map/all_to_all | solution.py:128
  196.7 15.9 %copy-start.1 = (bf16[1280,1280]{0,1:T(8,128)(2,1)S(1)}, bf16[1280,1280]{0,1:T(8,128)(2,1)}, u32[]{:S(2)}) copy-start(bf16[1280,1280]{0,1:T(8,128)(2,1)} %copy.32) | copy-start | bytes 9830404
  218.9 26.1 %collective-permute-start = (bf16[2,384,1280]{2,1,0:T(8,128)(2,1)}, bf16[2,384,1280]{2,1,0:T(8,128)(2,1)}, u32[]{:S(2)}, u32[]{:S(2)}) collective-permute-start(bf16[2,384,1280]{2,1,0:T(8,128)(2,1)} %fusion.11), channel_id=1, source_target_pairs={{0,1},{1,0},{2,3},{3,2},{4,5},{5,4},{6,7},{7,6},{8,9},{9,8},{10,11... | collective-permute-start | bytes 5898248 | tf_op jit(solution)/shard_map/ppermute | solution.py:287
  245.0 9.9 %collective-permute-start.2 = (bf16[2,384,1280]{2,1,0:T(8,128)(2,1)}, bf16[2,384,1280]{2,1,0:T(8,128)(2,1)}, u32[]{:S(2)}, u32[]{:S(2)}) collective-permute-start(bf16[2,384,1280]{2,1,0:T(8,128)(2,1)} %fusion.10), channel_id=1, source_target_pairs={{0,1},{1,0},{2,3},{3,2},{4,5},{5,4},{6,7},{7,6},{8,9},{9,8},{10,11... | collective-permute-start | bytes 5898248 | tf_op jit(solution)/shard_map/ppermute | solution.py:287
  245.0 9.9 %copy-start.2 = (bf16[1,1280,1280]{2,1,0:T(8,128)(2,1)S(1)}, bf16[1,1280,1280]{2,1,0:T(8,128)(2,1)}, u32[]{:S(2)}) copy-start(bf16[1,1280,1280]{2,1,0:T(8,128)(2,1)} %get-tuple-element.15) | copy-start | bytes 9830404
  245.0 9.9 %copy-start.3 = (bf16[1,1280,1280]{2,1,0:T(8,128)(2,1)S(1)}, bf16[1,1280,1280]{2,1,0:T(8,128)(2,1)}, u32[]{:S(2)}) copy-start(bf16[1,1280,1280]{2,1,0:T(8,128)(2,1)} %get-tuple-element.16) | copy-start | bytes 9830404
  245.0 9.9 %copy-start.7 = (bf16[384,1280]{1,0:T(8,128)(2,1)S(1)}, bf16[384,1280]{1,0:T(8,128)(2,1)}, u32[]{:S(2)}) copy-start(bf16[384,1280]{1,0:T(8,128)(2,1)} %shard_map.67) | copy-start | bytes 2949124
  252.7 24.1 %collective-permute-start.1 = (bf16[384,1280]{1,0:T(8,128)(2,1)}, bf16[384,1280]{1,0:T(8,128)(2,1)S(1)}, u32[]{:S(2)}, u32[]{:S(2)}) collective-permute-start(bf16[384,1280]{1,0:T(8,128)(2,1)} %dynamic-slice_bitcast_fusion.3), channel_id=1, source_target_pairs={{0,2},{2,0},{1,3},{3,1},{4,6},{6,4},{5,7},{7,5},{8,10},{10,8},{9,1... | collective-permute-start | bytes 2949128 | tf_op jit(solution)/shard_map/ppermute | solution.py:291
  259.1 1.3 copy-start.4
  261.4 36.6 %collective-permute-start.3 = (bf16[384,1280]{1,0:T(8,128)(2,1)}, bf16[384,1280]{1,0:T(8,128)(2,1)}, u32[]{:S(2)}, u32[]{:S(2)}) collective-permute-start(bf16[384,1280]{1,0:T(8,128)(2,1)} %dynamic-slice_bitcast_fusion.2), channel_id=1, source_target_pairs={{0,2},{2,0},{1,3},{3,1},{4,6},{6,4},{5,7},{7,5},{8,10},{10,8},{9,1... | collective-permute-start | bytes 2949128 | tf_op jit(solution)/shard_map/ppermute | solution.py:291
  261.4 36.6 %copy-start.5 = (bf16[2,384,1280]{2,1,0:T(8,128)(2,1)S(1)}, bf16[2,384,1280]{2,1,0:T(8,128)(2,1)}, u32[]{:S(2)}) copy-start(bf16[2,384,1280]{2,1,0:T(8,128)(2,1)} %copy-done.4) | copy-start | bytes 5898244

commit v12 on v11

--- a/solution.py
+++ b/solution.py
@@ -239,7 +239,7 @@
 
 def sink_attention(flags, queries, blocks, tables, near, half, halves):
     count, width = queries.shape
-    group = 2
+    group = 5
     heads_here = width // HDIM // group
     rows = count // halves
     wide = group * HDIM

time: 302 us -> 302 us (level)
  transfers between devices with their start and end apart: 6 -> 6, of which waited for: 4 -> 4; matrix products, arithmetic and copies ran while one was open for 13% -> 13% of each run, Pallas kernels for 14% -> 15%
where the time goes in v12:
time: 302 us; the launch traced here: 301 us
  waiting for transfers between devices  88.5 us (29%)
  Pallas kernels  67.3 us (22%)
  blocking collectives  59 us (20%)
  local copies, waits for them, and re-layouts  29.6 us (10%)
  matrix products  23.2 us (8%)
  starting transfers between devices  23 us (8%)
  other arithmetic  9.33 us (3%)
    all_to_all x1, blocking collectives, exchange(): spread = lax.all_to_all(data, FRAME_AXES, 0, 0, tiled=True)  59 us
    all_to_all x1, waiting for transfers between devices, exchange(): prev_full = lax.all_to_all(before, FRAME_AXES, 0, 0, tiled=True)  49.5 us
    ppermute x2, waiting for transfers between devices, head_reduce(): got = lax.ppermute(send, 'xl', [(0, 1), (1, 0)])  36.3 us
    pallas_call x2, Pallas kernels, sink_attention(): pl.pallas_call(sink_kernel, grid_spec=grid_spec, out_shape=jax.ShapeDtype...  31.7 us
    pallas_call x1, Pallas kernels, near_attention(): pl.pallas_call(near_kernel, grid_spec=grid_spec, out_shape=[f32] * 3, cos...  28 us
    dot_general x2, matrix products, head_reduce(): jnp.einsum('rk,xkn->xrn', attended, other_w, preferred_element_type=jnp.f...  12.4 us
    dot_general x2, matrix products, head_reduce(): jnp.einsum('rk,xkn->xrn', attended, mine_w, preferred_element_type=jnp.fl...  10.8 us
    all_to_all x1, starting transfers between devices, exchange(): return (prev_full, lax.all_to_all(copies, FRAME_AXES, 0, 0, tiled=True))  9.87 us
  transfers between devices with their start and end apart: 6, of which 4 were waited for; matrix products, arithmetic and copies ran while one was open for 13% of the time, Pallas kernels for 15%

profile of v12, /device:TPU:1, one launch (start us, length us, event | category | flops | bytes accessed | tf_op | source)
XLA Modules:
  0.0 301.0 jit_solution(15602670038064185436)
XLA Ops:
  0.7 0.6 fusion.20.swap_ref
  1.3 0.8 fusion.21
  2.1 0.3 copy.24
  2.5 0.3 reshape.409
  2.7 0.9 copy.26.sin_ref.sq
  3.7 0.3 copy.23
  4.0 0.0 copy-start.6
  4.0 0.3 reshape.408
  4.3 1.0 copy.25.cos_ref.cq
  5.3 7.7 %shard_map.64.ks_ref = bf16[768,1280]{1,0:T(8,128)(2,1)} custom-call(bf16[768,1280]{1,0:T(8,128)(2,1)} %x_ref.1, bf16[128,128]{1,0:T(8,128)(2,1)} %fusion.20.swap_ref, f32[768,128]{1,0:T(8,128)} %copy.25.cos_ref.cq, f32[768,128]{1,0:T(8,128)} %copy.26.sin_ref.sq), custom_call_target="tpu_custom_call" | custom-call | flops 251658240 | bytes 3932160 | tf_op jit(solution)/shard_map/pallas_call | solution.py:180
  12.9 0.0 copy-done.6
  12.9 1.8 pad_maximum_fusion.6
  14.7 59.0 %all_to_all.32 = bf16[32,48,1280]{2,1,0:T(8,128)(2,1)S(1)} all-to-all(bf16[32,48,1280]{2,1,0:T(8,128)(2,1)S(1)} %bitcast.54), channel_id=1, replica_groups=mesh['z'=4,'xh'=2,'y'=4,'xl'=2,'c'=2] {'z','xh','y'}, dimensions={0} | all-to-all | bytes 7864320 | tf_op jit(solution)/shard_map/all_to_all | solution.py:121
  73.7 1.8 copy-done
  75.6 0.2 slice.17
  75.8 2.3 pad_maximum_fusion.7
  78.1 6.6 %all-to-all-start.1 = ((bf16[32,48,1280]{2,1,0:T(8,128)(2,1)}), bf16[32,48,1280]{2,1,0:T(8,128)(2,1)}, u32[]{:S(2)}, u32[]{:S(2)}) async-start(bf16[32,48,1280]{2,1,0:T(8,128)(2,1)} %pad_maximum_fusion.7), calls=%async_computation.1 | async-start | bytes 7864320 | tf_op jit(solution)/shard_map/all_to_all | solution.py:124
  84.8 0.9 constant_dynamic-slice_fusion.2
  85.7 49.5 %all-to-all-done.1 = bf16[32,48,1280]{2,1,0:T(8,128)(2,1)} async-done(((bf16[32,48,1280]{2,1,0:T(8,128)(2,1)}), bf16[32,48,1280]{2,1,0:T(8,128)(2,1)}, u32[]{:S(2)}, u32[]{:S(2)}) %all-to-all-start.1) | async-done | bytes 3932192 | tf_op jit(solution)/shard_map/all_to_all | solution.py:124
  135.2 2.2 broadcast_in_dim.64
  137.4 9.9 %all-to-all-start.2 = ((bf16[32,48,1280]{2,1,0:T(8,128)(2,1)}), bf16[32,48,1280]{2,1,0:T(8,128)(2,1)}, u32[]{:S(2)}, u32[]{:S(2)}) async-start(bf16[32,48,1280]{2,1,0:T(8,128)(2,1)} %broadcast_in_dim.64), calls=%async_computation.2 | async-start | bytes 7864320 | tf_op jit(solution)/shard_map/all_to_all | solution.py:128
  147.3 9.0 %dynamic-slice_bitcast_fusion.1 = (bf16[1,1280,1280]{2,1,0:T(8,128)(2,1)}, bf16[1,1280,1280]{2,1,0:T(8,128)(2,1)}, bf16[1280,1280]{1,0:T(8,128)(2,1)}, bf16[1280,1280]{1,0:T(8,128)(2,1)S(1)}) fusion(bf16[1280,5120]{1,0:T(8,128)(2,1)} %param.9, s32[]{:T(128)S(6)} %select_n.103, s32[]{:T(128)S(6)} %select_n.104, s32[]{:T(128)S(6)} %select_n.114, s32[]{:T(128)S(6)} %select_n.113), kind=kLoop, calls=%fused_computation.17 | loop fusion | bytes 26214416 | tf_op jit(solution)/shard_map/stack | solution.py:276
  156.3 5.7 %copy.32 = bf16[1280,1280]{0,1:T(8,128)(2,1)} copy(bf16[1280,1280]{1,0:T(8,128)(2,1)} %get-tuple-element.17) | data formatting | bytes 6553600 | tf_op jit(solution)/shard_map/dynamic_slice | solution.py:277
  162.0 3.4 %copy.31 = bf16[1280,1280]{0,1:T(8,128)(2,1)} copy(bf16[1280,1280]{1,0:T(8,128)(2,1)S(1)} %get-tuple-element.18) | data formatting | bytes 6553600 | tf_op jit(solution)/shard_map/dynamic_slice | solution.py:277
  165.4 0.6 add_convert_fusion.flags
  166.0 28.0 %shard_map.65 = (f32[768,1280]{1,0:T(8,128)}, f32[768,1280]{1,0:T(8,128)}, f32[768,1280]{1,0:T(8,128)}) custom-call(s32[2]{0:T(128)} %add_convert_fusion.flags, bf16[768,1280]{1,0:T(8,128)(2,1)} %q_ref.5, bf16[768,1280]{1,0:T(8,128)(2,1)} %shard_map.64.ks_ref, bf16[768,1280]{1,0:T(8,128)(2,1)} %vs_ref.1, bf16[1536,1280]{1,0:T(8,128)(2,1)} %bitcast.9.kp_ref.vp_ref, ...), custom_call_target="tpu_custom_call" | custom-call | flops 6039797760 | bytes 21626880 | tf_op jit(solution)/shard_map/pallas_call | solution.py:235
  194.0 2.7 all-to-all-done.2
  196.7 16.0 %shard_map.66 = bf16[384,1280]{1,0:T(8,128)(2,1)} custom-call(s32[2]{0:T(128)} %add_convert_fusion.flags, bf16[768,1280]{1,0:T(8,128)(2,1)} %q_ref.5, bf16[1536,1280]{1,0:T(8,128)(2,1)} %bitcast.11.kk_ref.vk_ref, bf16[1536,1280]{1,0:T(8,128)(2,1)} %bitcast.11.kk_ref.vk_ref, bf16[128,128]{1,0:T(8,128)(2,1)} %fusion.20.swap_ref, f32[768,128]{1,0:T(8,128)} %copy.25.cos_ref.cq, ...), custom_call_target="tpu_custom_call" | custom-call | flops 1509949440 | bytes 10813440 | tf_op jit(solution)/shard_map/pallas_call | solution.py:262
  212.7 6.2 %fusion.11 = bf16[2,384,1280]{2,1,0:T(8,128)(2,1)} fusion(bf16[1,1280,1280]{1,2,0:T(8,128)(2,1)S(1)} %bitcast.55, bf16[1,1280,1280]{1,2,0:T(8,128)(2,1)} %bitcast.57, bf16[384,1280]{1,0:T(8,128)(2,1)} %shard_map.66), kind=kOutput, calls=%fused_computation.19 | convolution fusion | flops 2520842240 | bytes 9502720 | tf_op jit(solution)/shard_map/rk,xkn->xrn/dot_general | solution.py:286
  218.9 4.3 %collective-permute-start = (bf16[2,384,1280]{2,1,0:T(8,128)(2,1)}, bf16[2,384,1280]{2,1,0:T(8,128)(2,1)}, u32[]{:S(2)}, u32[]{:S(2)}) collective-permute-start(bf16[2,384,1280]{2,1,0:T(8,128)(2,1)} %fusion.11), channel_id=1, source_target_pairs={{0,1},{1,0},{2,3},{3,2},{4,5},{5,4},{6,7},{7,6},{8,9},{9,8},{10,11... | collective-permute-start | bytes 5898248 | tf_op jit(solution)/shard_map/ppermute | solution.py:287
  223.2 15.7 %shard_map.67 = bf16[384,1280]{1,0:T(8,128)(2,1)} custom-call(s32[2]{0:T(128)} %add_convert_fusion.flags, bf16[768,1280]{1,0:T(8,128)(2,1)} %q_ref.5, bf16[1536,1280]{1,0:T(8,128)(2,1)} %bitcast.11.kk_ref.vk_ref, bf16[1536,1280]{1,0:T(8,128)(2,1)} %bitcast.11.kk_ref.vk_ref, bf16[128,128]{1,0:T(8,128)(2,1)} %fusion.20.swap_ref, f32[768,128]{1,0:T(8,128)} %copy.25.cos_ref.cq, ...), custom_call_target="tpu_custom_call" | custom-call | flops 1509949440 | bytes 10813440 | tf_op jit(solution)/shard_map/pallas_call | solution.py:262
  238.9 6.2 %fusion.10 = bf16[2,384,1280]{2,1,0:T(8,128)(2,1)} fusion(bf16[1,1280,1280]{1,2,0:T(8,128)(2,1)S(1)} %bitcast.56, bf16[1,1280,1280]{1,2,0:T(8,128)(2,1)} %bitcast.58, bf16[384,1280]{1,0:T(8,128)(2,1)} %shard_map.67), kind=kOutput, calls=%fused_computation.18 | convolution fusion | flops 2520842240 | bytes 9502720 | tf_op jit(solution)/shard_map/rk,xkn->xrn/dot_general | solution.py:286
  245.1 0.0 collective-permute-start.2
  245.1 0.0 collective-permute-done
  245.2 6.6 %fusion.5 = bf16[2,384,1280]{2,1,0:T(8,128)(2,1)S(1)} fusion(bf16[2,384,1280]{2,1,0:T(8,128)(2,1)} %collective-permute-done, bf16[1,1280,1280]{2,1,0:T(8,128)(2,1)} %get-tuple-element.16, bf16[1,1280,1280]{2,1,0:T(8,128)(2,1)} %get-tuple-element.15, bf16[384,1280]{1,0:T(8,128)(2,1)} %shard_map.66), kind=kOutput, calls=%fused_computation.11 | convolution fusion | flops 2534604800 | bytes 11468800 | tf_op jit(solution)/shard_map/rk,xkn->xrn/dot_general | solution.py:285
  251.8 1.0 dynamic-slice_bitcast_fusion.3
  252.8 2.2 collective-permute-start.1
  255.0 0.0 collective-permute-done.2
  255.1 4.2 %fusion.4 = bf16[2,384,1280]{2,1,0:T(8,128)(2,1)S(1)} fusion(bf16[2,384,1280]{2,1,0:T(8,128)(2,1)} %collective-permute-done.2, bf16[1,1280,1280]{2,1,0:T(8,128)(2,1)S(1)} %copy-done.3, bf16[1,1280,1280]{2,1,0:T(8,128)(2,1)S(1)} %copy-done.2, bf16[384,1280]{1,0:T(8,128)(2,1)S(1)} %copy-done.7), kind=kOutput, calls=%fused_computation.9 | convolution fusion | flops 2534604800 | bytes 11468800 | tf_op jit(solution)/shard_map/rk,xkn->xrn/dot_general | solution.py:285
  259.2 0.0 copy-start.4
  259.2 1.3 copy-done.4
  260.5 1.0 dynamic-slice_bitcast_fusion.2
  261.5 0.0 collective-permute-start.3
  261.6 15.4 %collective-permute-done.1 = bf16[384,1280]{1,0:T(8,128)(2,1)S(1)} collective-permute-done((bf16[384,1280]{1,0:T(8,128)(2,1)}, bf16[384,1280]{1,0:T(8,128)(2,1)S(1)}, u32[]{:S(2)}, u32[]{:S(2)}) %collective-permute-start.1) | collective-permute-done | bytes 983072 | tf_op jit(solution)/shard_map/ppermute | solution.py:291
  276.9 0.2 fusion.13
  277.2 20.9 %collective-permute-done.3 = bf16[384,1280]{1,0:T(8,128)(2,1)} collective-permute-done((bf16[384,1280]{1,0:T(8,128)(2,1)}, bf16[384,1280]{1,0:T(8,128)(2,1)}, u32[]{:S(2)}, u32[]{:S(2)}) %collective-permute-start.3) | collective-permute-done | bytes 983072 | tf_op jit(solution)/shard_map/ppermute | solution.py:291
  298.1 1.5 fusion.12
  299.6 1.4 pad_maximum_fusion.24
  (20 shorter events, 0.1 us)
Async XLA Ops:
  4.0 8.9 %copy-start.6 = (bf16[768,1280]{1,0:T(8,128)(2,1)S(1)}, bf16[768,1280]{1,0:T(8,128)(2,1)}, u32[]{:S(2)}) copy-start(bf16[768,1280]{1,0:T(8,128)(2,1)} %vs_ref.1) | copy-start | bytes 5898244
  73.7 1.9 copy-start
  78.1 6.6 %copy-start.8 = (s32[32]{0:T(128)S(1)}, s32[32]{0:T(128)}, u32[]{:S(2)}) copy-start(s32[32]{0:T(128)} %param.10) | copy-start | bytes 388
  78.1 57.1 %all-to-all-start.1 = ((bf16[32,48,1280]{2,1,0:T(8,128)(2,1)}), bf16[32,48,1280]{2,1,0:T(8,128)(2,1)}, u32[]{:S(2)}, u32[]{:S(2)}) async-start(bf16[32,48,1280]{2,1,0:T(8,128)(2,1)} %pad_maximum_fusion.7), calls=%async_computation.1 | async-start | bytes 7864320 | tf_op jit(solution)/shard_map/all_to_all | solution.py:124
  137.4 59.3 %all-to-all-start.2 = ((bf16[32,48,1280]{2,1,0:T(8,128)(2,1)}), bf16[32,48,1280]{2,1,0:T(8,128)(2,1)}, u32[]{:S(2)}, u32[]{:S(2)}) async-start(bf16[32,48,1280]{2,1,0:T(8,128)(2,1)} %broadcast_in_dim.64), calls=%async_computation.2 | async-start | bytes 7864320 | tf_op jit(solution)/shard_map/all_to_all | solution.py:128
  196.7 16.0 %copy-start.1 = (bf16[1280,1280]{0,1:T(8,128)(2,1)S(1)}, bf16[1280,1280]{0,1:T(8,128)(2,1)}, u32[]{:S(2)}) copy-start(bf16[1280,1280]{0,1:T(8,128)(2,1)} %copy.32) | copy-start | bytes 9830404
  218.9 26.2 %collective-permute-start = (bf16[2,384,1280]{2,1,0:T(8,128)(2,1)}, bf16[2,384,1280]{2,1,0:T(8,128)(2,1)}, u32[]{:S(2)}, u32[]{:S(2)}) collective-permute-start(bf16[2,384,1280]{2,1,0:T(8,128)(2,1)} %fusion.11), channel_id=1, source_target_pairs={{0,1},{1,0},{2,3},{3,2},{4,5},{5,4},{6,7},{7,6},{8,9},{9,8},{10,11... | collective-permute-start | bytes 5898248 | tf_op jit(solution)/shard_map/ppermute | solution.py:287
  245.1 9.9 %collective-permute-start.2 = (bf16[2,384,1280]{2,1,0:T(8,128)(2,1)}, bf16[2,384,1280]{2,1,0:T(8,128)(2,1)}, u32[]{:S(2)}, u32[]{:S(2)}) collective-permute-start(bf16[2,384,1280]{2,1,0:T(8,128)(2,1)} %fusion.10), channel_id=1, source_target_pairs={{0,1},{1,0},{2,3},{3,2},{4,5},{5,4},{6,7},{7,6},{8,9},{9,8},{10,11... | collective-permute-start | bytes 5898248 | tf_op jit(solution)/shard_map/ppermute | solution.py:287
  245.1 9.9 %copy-start.2 = (bf16[1,1280,1280]{2,1,0:T(8,128)(2,1)S(1)}, bf16[1,1280,1280]{2,1,0:T(8,128)(2,1)}, u32[]{:S(2)}) copy-start(bf16[1,1280,1280]{2,1,0:T(8,128)(2,1)} %get-tuple-element.15) | copy-start | bytes 9830404
  245.1 9.9 %copy-start.3 = (bf16[1,1280,1280]{2,1,0:T(8,128)(2,1)S(1)}, bf16[1,1280,1280]{2,1,0:T(8,128)(2,1)}, u32[]{:S(2)}) copy-start(bf16[1,1280,1280]{2,1,0:T(8,128)(2,1)} %get-tuple-element.16) | copy-start | bytes 9830404
  245.2 9.9 %copy-start.7 = (bf16[384,1280]{1,0:T(8,128)(2,1)S(1)}, bf16[384,1280]{1,0:T(8,128)(2,1)}, u32[]{:S(2)}) copy-start(bf16[384,1280]{1,0:T(8,128)(2,1)} %shard_map.67) | copy-start | bytes 2949124
  252.8 24.1 %collective-permute-start.1 = (bf16[384,1280]{1,0:T(8,128)(2,1)}, bf16[384,1280]{1,0:T(8,128)(2,1)S(1)}, u32[]{:S(2)}, u32[]{:S(2)}) collective-permute-start(bf16[384,1280]{1,0:T(8,128)(2,1)} %dynamic-slice_bitcast_fusion.3), channel_id=1, source_target_pairs={{0,2},{2,0},{1,3},{3,1},{4,6},{6,4},{5,7},{7,5},{8,10},{10,8},{9,1... | collective-permute-start | bytes 2949128 | tf_op jit(solution)/shard_map/ppermute | solution.py:291
  259.2 1.3 copy-start.4
  261.5 36.6 %collective-permute-start.3 = (bf16[384,1280]{1,0:T(8,128)(2,1)}, bf16[384,1280]{1,0:T(8,128)(2,1)}, u32[]{:S(2)}, u32[]{:S(2)}) collective-permute-start(bf16[384,1280]{1,0:T(8,128)(2,1)} %dynamic-slice_bitcast_fusion.2), channel_id=1, source_target_pairs={{0,2},{2,0},{1,3},{3,1},{4,6},{6,4},{5,7},{7,5},{8,10},{10,8},{9,1... | collective-permute-start | bytes 2949128 | tf_op jit(solution)/shard_map/ppermute | solution.py:291
  261.6 36.6 %copy-start.5 = (bf16[2,384,1280]{2,1,0:T(8,128)(2,1)S(1)}, bf16[2,384,1280]{2,1,0:T(8,128)(2,1)}, u32[]{:S(2)}) copy-start(bf16[2,384,1280]{2,1,0:T(8,128)(2,1)} %copy-done.4) | copy-start | bytes 5898244

commit v13 on v12

--- a/solution.py
+++ b/solution.py
@@ -169,17 +169,21 @@
 
 
 def rope_kernel(x_ref, swap_ref, cos_ref, sin_ref, out_ref):
-    out_ref[...] = rotate_ref(x_ref, cos_ref, sin_ref, swap_ref[...])
+    swap = swap_ref[...]
+    for j in range(x_ref.shape[1] // HDIM):
+        cols = slice(j * HDIM, (j + 1) * HDIM)
+        out_ref[:, cols] = rotate_ref(x_ref.at[:, cols], cos_ref, sin_ref, swap)
 
 
 def rope(x, tables):
     count, width = x.shape
-    head = pl.BlockSpec((count, HDIM), lambda h: (0, h))
+    wide = 5 * HDIM
+    head = pl.BlockSpec((count, wide), lambda h: (0, h))
     whole = pl.BlockSpec((count, HDIM), lambda h: (0, 0))
     swap = pl.BlockSpec((HDIM, HDIM), lambda h: (0, 0))
     return pl.pallas_call(
         rope_kernel,
-        grid=(width // HDIM,),
+        grid=(width // wide,),
         in_specs=[head, swap, whole, whole],
         out_specs=head,
         out_shape=jax.ShapeDtypeStruct((count, width), jnp.bfloat16),

time: 302 us -> 298 us (0.987)
  Pallas kernels: 67.3 us -> 63.2 us
    pallas_call x1, Pallas kernels: 7.66 us -> 3.49 us  [rope(): pl.pallas_call(rope_kernel, grid=(width // wide,), in_specs=[head, swap,...]
where the time goes in v13:
time: 298 us; the launch traced here: 297 us
  waiting for transfers between devices  89.1 us (30%)
  Pallas kernels  63.2 us (21%)
  blocking collectives  59 us (20%)
  local copies, waits for them, and re-layouts  29.6 us (10%)
  matrix products  23.2 us (8%)
  starting transfers between devices  22.9 us (8%)
  other arithmetic  9.33 us (3%)
    all_to_all x1, blocking collectives, exchange(): spread = lax.all_to_all(data, FRAME_AXES, 0, 0, tiled=True)  59 us
    all_to_all x1, waiting for transfers between devices, exchange(): prev_full = lax.all_to_all(before, FRAME_AXES, 0, 0, tiled=True)  49.7 us
    ppermute x2, waiting for transfers between devices, head_reduce(): got = lax.ppermute(send, 'xl', [(0, 1), (1, 0)])  36.3 us
    pallas_call x2, Pallas kernels, sink_attention(): pl.pallas_call(sink_kernel, grid_spec=grid_spec, out_shape=jax.ShapeDtype...  31.7 us
    pallas_call x1, Pallas kernels, near_attention(): pl.pallas_call(near_kernel, grid_spec=grid_spec, out_shape=[f32] * 3, cos...  28 us
    dot_general x2, matrix products, head_reduce(): jnp.einsum('rk,xkn->xrn', attended, other_w, preferred_element_type=jnp.f...  12.4 us
    dot_general x2, matrix products, head_reduce(): jnp.einsum('rk,xkn->xrn', attended, mine_w, preferred_element_type=jnp.fl...  10.8 us
    all_to_all x1, starting transfers between devices, exchange(): return (prev_full, lax.all_to_all(copies, FRAME_AXES, 0, 0, tiled=True))  9.37 us
  transfers between devices with their start and end apart: 6, of which 4 were waited for; matrix products, arithmetic and copies ran while one was open for 13% of the time, Pallas kernels for 15%

profile of v13, /device:TPU:1, one launch (start us, length us, event | category | flops | bytes accessed | tf_op | source)
XLA Modules:
  0.0 297.3 jit_solution(17268280984638109734)
XLA Ops:
  0.7 0.6 fusion.20.swap_ref
  1.3 0.8 fusion.21
  2.1 0.3 copy.24
  2.5 0.3 reshape.409
  2.7 0.9 copy.26.sin_ref.sq
  3.7 0.3 copy.23
  4.0 0.0 copy-start.6
  4.0 0.3 reshape.408
  4.3 1.0 copy.25.cos_ref.cq
  5.3 3.5 %shard_map.64.ks_ref = bf16[768,1280]{1,0:T(8,128)(2,1)} custom-call(bf16[768,1280]{1,0:T(8,128)(2,1)} %x_ref.1, bf16[128,128]{1,0:T(8,128)(2,1)} %fusion.20.swap_ref, f32[768,128]{1,0:T(8,128)} %copy.25.cos_ref.cq, f32[768,128]{1,0:T(8,128)} %copy.26.sin_ref.sq), custom_call_target="tpu_custom_call" | custom-call | flops 251658240 | bytes 3932160 | tf_op jit(solution)/shard_map/pallas_call | solution.py:184
  8.7 0.0 copy-done.6
  8.8 1.8 pad_maximum_fusion.6
  10.6 59.0 %all_to_all.32 = bf16[32,48,1280]{2,1,0:T(8,128)(2,1)S(1)} all-to-all(bf16[32,48,1280]{2,1,0:T(8,128)(2,1)S(1)} %bitcast.54), channel_id=1, replica_groups=mesh['z'=4,'xh'=2,'y'=4,'xl'=2,'c'=2] {'z','xh','y'}, dimensions={0} | all-to-all | bytes 7864320 | tf_op jit(solution)/shard_map/all_to_all | solution.py:121
  69.5 1.8 copy-done
  71.4 0.2 slice.17
  71.6 2.3 pad_maximum_fusion.7
  73.9 6.5 %all-to-all-start.1 = ((bf16[32,48,1280]{2,1,0:T(8,128)(2,1)}), bf16[32,48,1280]{2,1,0:T(8,128)(2,1)}, u32[]{:S(2)}, u32[]{:S(2)}) async-start(bf16[32,48,1280]{2,1,0:T(8,128)(2,1)} %pad_maximum_fusion.7), calls=%async_computation.1 | async-start | bytes 7864320 | tf_op jit(solution)/shard_map/all_to_all | solution.py:124
  80.6 0.9 constant_dynamic-slice_fusion.2
  81.5 49.7 %all-to-all-done.1 = bf16[32,48,1280]{2,1,0:T(8,128)(2,1)} async-done(((bf16[32,48,1280]{2,1,0:T(8,128)(2,1)}), bf16[32,48,1280]{2,1,0:T(8,128)(2,1)}, u32[]{:S(2)}, u32[]{:S(2)}) %all-to-all-start.1) | async-done | bytes 3932192 | tf_op jit(solution)/shard_map/all_to_all | solution.py:124
  131.2 2.2 broadcast_in_dim.64
  133.4 9.4 %all-to-all-start.2 = ((bf16[32,48,1280]{2,1,0:T(8,128)(2,1)}), bf16[32,48,1280]{2,1,0:T(8,128)(2,1)}, u32[]{:S(2)}, u32[]{:S(2)}) async-start(bf16[32,48,1280]{2,1,0:T(8,128)(2,1)} %broadcast_in_dim.64), calls=%async_computation.2 | async-start | bytes 7864320 | tf_op jit(solution)/shard_map/all_to_all | solution.py:128
  142.8 9.0 %dynamic-slice_bitcast_fusion.1 = (bf16[1,1280,1280]{2,1,0:T(8,128)(2,1)}, bf16[1,1280,1280]{2,1,0:T(8,128)(2,1)}, bf16[1280,1280]{1,0:T(8,128)(2,1)}, bf16[1280,1280]{1,0:T(8,128)(2,1)S(1)}) fusion(bf16[1280,5120]{1,0:T(8,128)(2,1)} %param.9, s32[]{:T(128)S(6)} %select_n.103, s32[]{:T(128)S(6)} %select_n.104, s32[]{:T(128)S(6)} %select_n.114, s32[]{:T(128)S(6)} %select_n.113), kind=kLoop, calls=%fused_computation.17 | loop fusion | bytes 26214416 | tf_op jit(solution)/shard_map/stack | solution.py:280
  151.8 5.7 %copy.32 = bf16[1280,1280]{0,1:T(8,128)(2,1)} copy(bf16[1280,1280]{1,0:T(8,128)(2,1)} %get-tuple-element.17) | data formatting | bytes 6553600 | tf_op jit(solution)/shard_map/dynamic_slice | solution.py:281
  157.4 3.4 %copy.31 = bf16[1280,1280]{0,1:T(8,128)(2,1)} copy(bf16[1280,1280]{1,0:T(8,128)(2,1)S(1)} %get-tuple-element.18) | data formatting | bytes 6553600 | tf_op jit(solution)/shard_map/dynamic_slice | solution.py:281
  160.8 0.6 add_convert_fusion.flags
  161.5 28.0 %shard_map.65 = (f32[768,1280]{1,0:T(8,128)}, f32[768,1280]{1,0:T(8,128)}, f32[768,1280]{1,0:T(8,128)}) custom-call(s32[2]{0:T(128)} %add_convert_fusion.flags, bf16[768,1280]{1,0:T(8,128)(2,1)} %q_ref.5, bf16[768,1280]{1,0:T(8,128)(2,1)} %shard_map.64.ks_ref, bf16[768,1280]{1,0:T(8,128)(2,1)} %vs_ref.1, bf16[1536,1280]{1,0:T(8,128)(2,1)} %bitcast.9.kp_ref.vp_ref, ...), custom_call_target="tpu_custom_call" | custom-call | flops 6039797760 | bytes 21626880 | tf_op jit(solution)/shard_map/pallas_call | solution.py:239
  189.5 3.1 %all-to-all-done.2 = bf16[32,48,1280]{2,1,0:T(8,128)(2,1)} async-done(((bf16[32,48,1280]{2,1,0:T(8,128)(2,1)}), bf16[32,48,1280]{2,1,0:T(8,128)(2,1)}, u32[]{:S(2)}, u32[]{:S(2)}) %all-to-all-start.2) | async-done | bytes 3932192 | tf_op jit(solution)/shard_map/all_to_all | solution.py:128
  192.6 16.0 %shard_map.66 = bf16[384,1280]{1,0:T(8,128)(2,1)} custom-call(s32[2]{0:T(128)} %add_convert_fusion.flags, bf16[768,1280]{1,0:T(8,128)(2,1)} %q_ref.5, bf16[1536,1280]{1,0:T(8,128)(2,1)} %bitcast.11.kk_ref.vk_ref, bf16[1536,1280]{1,0:T(8,128)(2,1)} %bitcast.11.kk_ref.vk_ref, bf16[128,128]{1,0:T(8,128)(2,1)} %fusion.20.swap_ref, f32[768,128]{1,0:T(8,128)} %copy.25.cos_ref.cq, ...), custom_call_target="tpu_custom_call" | custom-call | flops 1509949440 | bytes 10813440 | tf_op jit(solution)/shard_map/pallas_call | solution.py:266
  208.6 6.2 %fusion.11 = bf16[2,384,1280]{2,1,0:T(8,128)(2,1)} fusion(bf16[1,1280,1280]{1,2,0:T(8,128)(2,1)S(1)} %bitcast.55, bf16[1,1280,1280]{1,2,0:T(8,128)(2,1)} %bitcast.57, bf16[384,1280]{1,0:T(8,128)(2,1)} %shard_map.66), kind=kOutput, calls=%fused_computation.19 | convolution fusion | flops 2520842240 | bytes 9502720 | tf_op jit(solution)/shard_map/rk,xkn->xrn/dot_general | solution.py:290
  214.8 3.8 %collective-permute-start = (bf16[2,384,1280]{2,1,0:T(8,128)(2,1)}, bf16[2,384,1280]{2,1,0:T(8,128)(2,1)}, u32[]{:S(2)}, u32[]{:S(2)}) collective-permute-start(bf16[2,384,1280]{2,1,0:T(8,128)(2,1)} %fusion.11), channel_id=1, source_target_pairs={{0,1},{1,0},{2,3},{3,2},{4,5},{5,4},{6,7},{7,6},{8,9},{9,8},{10,11... | collective-permute-start | bytes 5898248 | tf_op jit(solution)/shard_map/ppermute | solution.py:291
  218.6 15.7 %shard_map.67 = bf16[384,1280]{1,0:T(8,128)(2,1)} custom-call(s32[2]{0:T(128)} %add_convert_fusion.flags, bf16[768,1280]{1,0:T(8,128)(2,1)} %q_ref.5, bf16[1536,1280]{1,0:T(8,128)(2,1)} %bitcast.11.kk_ref.vk_ref, bf16[1536,1280]{1,0:T(8,128)(2,1)} %bitcast.11.kk_ref.vk_ref, bf16[128,128]{1,0:T(8,128)(2,1)} %fusion.20.swap_ref, f32[768,128]{1,0:T(8,128)} %copy.25.cos_ref.cq, ...), custom_call_target="tpu_custom_call" | custom-call | flops 1509949440 | bytes 10813440 | tf_op jit(solution)/shard_map/pallas_call | solution.py:266
  234.3 6.2 %fusion.10 = bf16[2,384,1280]{2,1,0:T(8,128)(2,1)} fusion(bf16[1,1280,1280]{1,2,0:T(8,128)(2,1)S(1)} %bitcast.56, bf16[1,1280,1280]{1,2,0:T(8,128)(2,1)} %bitcast.58, bf16[384,1280]{1,0:T(8,128)(2,1)} %shard_map.67), kind=kOutput, calls=%fused_computation.18 | convolution fusion | flops 2520842240 | bytes 9502720 | tf_op jit(solution)/shard_map/rk,xkn->xrn/dot_general | solution.py:290
  240.5 0.0 collective-permute-start.2
  240.5 0.0 collective-permute-done
  240.5 6.6 %fusion.5 = bf16[2,384,1280]{2,1,0:T(8,128)(2,1)S(1)} fusion(bf16[2,384,1280]{2,1,0:T(8,128)(2,1)} %collective-permute-done, bf16[1,1280,1280]{2,1,0:T(8,128)(2,1)} %get-tuple-element.16, bf16[1,1280,1280]{2,1,0:T(8,128)(2,1)} %get-tuple-element.15, bf16[384,1280]{1,0:T(8,128)(2,1)} %shard_map.66), kind=kOutput, calls=%fused_computation.11 | convolution fusion | flops 2534604800 | bytes 11468800 | tf_op jit(solution)/shard_map/rk,xkn->xrn/dot_general | solution.py:289
  247.1 1.0 dynamic-slice_bitcast_fusion.3
  248.1 3.2 %collective-permute-start.1 = (bf16[384,1280]{1,0:T(8,128)(2,1)}, bf16[384,1280]{1,0:T(8,128)(2,1)S(1)}, u32[]{:S(2)}, u32[]{:S(2)}) collective-permute-start(bf16[384,1280]{1,0:T(8,128)(2,1)} %dynamic-slice_bitcast_fusion.3), channel_id=1, source_target_pairs={{0,2},{2,0},{1,3},{3,1},{4,6},{6,4},{5,7},{7,5},{8,10},{10,8},{9,1... | collective-permute-start | bytes 2949128 | tf_op jit(solution)/shard_map/ppermute | solution.py:295
  251.4 0.0 collective-permute-done.2
  251.4 4.2 %fusion.4 = bf16[2,384,1280]{2,1,0:T(8,128)(2,1)S(1)} fusion(bf16[2,384,1280]{2,1,0:T(8,128)(2,1)} %collective-permute-done.2, bf16[1,1280,1280]{2,1,0:T(8,128)(2,1)S(1)} %copy-done.3, bf16[1,1280,1280]{2,1,0:T(8,128)(2,1)S(1)} %copy-done.2, bf16[384,1280]{1,0:T(8,128)(2,1)S(1)} %copy-done.7), kind=kOutput, calls=%fused_computation.9 | convolution fusion | flops 2534604800 | bytes 11468800 | tf_op jit(solution)/shard_map/rk,xkn->xrn/dot_general | solution.py:289
  255.6 0.0 copy-start.4
  255.6 1.3 copy-done.4
  256.9 1.0 dynamic-slice_bitcast_fusion.2
  257.9 0.0 collective-permute-start.3
  257.9 15.4 %collective-permute-done.1 = bf16[384,1280]{1,0:T(8,128)(2,1)S(1)} collective-permute-done((bf16[384,1280]{1,0:T(8,128)(2,1)}, bf16[384,1280]{1,0:T(8,128)(2,1)S(1)}, u32[]{:S(2)}, u32[]{:S(2)}) %collective-permute-start.1) | collective-permute-done | bytes 983072 | tf_op jit(solution)/shard_map/ppermute | solution.py:295
  273.3 0.2 fusion.13
  273.5 20.9 %collective-permute-done.3 = bf16[384,1280]{1,0:T(8,128)(2,1)} collective-permute-done((bf16[384,1280]{1,0:T(8,128)(2,1)}, bf16[384,1280]{1,0:T(8,128)(2,1)}, u32[]{:S(2)}, u32[]{:S(2)}) %collective-permute-start.3) | collective-permute-done | bytes 983072 | tf_op jit(solution)/shard_map/ppermute | solution.py:295
  294.5 1.5 fusion.12
  295.9 1.4 pad_maximum_fusion.24
  (20 shorter events, 0.1 us)
Async XLA Ops:
  4.0 4.7 %copy-start.6 = (bf16[768,1280]{1,0:T(8,128)(2,1)S(1)}, bf16[768,1280]{1,0:T(8,128)(2,1)}, u32[]{:S(2)}) copy-start(bf16[768,1280]{1,0:T(8,128)(2,1)} %vs_ref.1) | copy-start | bytes 5898244
  69.5 1.9 copy-start
  73.9 6.5 %copy-start.8 = (s32[32]{0:T(128)S(1)}, s32[32]{0:T(128)}, u32[]{:S(2)}) copy-start(s32[32]{0:T(128)} %param.10) | copy-start | bytes 388
  73.9 57.3 %all-to-all-start.1 = ((bf16[32,48,1280]{2,1,0:T(8,128)(2,1)}), bf16[32,48,1280]{2,1,0:T(8,128)(2,1)}, u32[]{:S(2)}, u32[]{:S(2)}) async-start(bf16[32,48,1280]{2,1,0:T(8,128)(2,1)} %pad_maximum_fusion.7), calls=%async_computation.1 | async-start | bytes 7864320 | tf_op jit(solution)/shard_map/all_to_all | solution.py:124
  133.4 59.2 %all-to-all-start.2 = ((bf16[32,48,1280]{2,1,0:T(8,128)(2,1)}), bf16[32,48,1280]{2,1,0:T(8,128)(2,1)}, u32[]{:S(2)}, u32[]{:S(2)}) async-start(bf16[32,48,1280]{2,1,0:T(8,128)(2,1)} %broadcast_in_dim.64), calls=%async_computation.2 | async-start | bytes 7864320 | tf_op jit(solution)/shard_map/all_to_all | solution.py:128
  192.6 16.0 %copy-start.1 = (bf16[1280,1280]{0,1:T(8,128)(2,1)S(1)}, bf16[1280,1280]{0,1:T(8,128)(2,1)}, u32[]{:S(2)}) copy-start(bf16[1280,1280]{0,1:T(8,128)(2,1)} %copy.32) | copy-start | bytes 9830404
  214.8 25.7 %collective-permute-start = (bf16[2,384,1280]{2,1,0:T(8,128)(2,1)}, bf16[2,384,1280]{2,1,0:T(8,128)(2,1)}, u32[]{:S(2)}, u32[]{:S(2)}) collective-permute-start(bf16[2,384,1280]{2,1,0:T(8,128)(2,1)} %fusion.11), channel_id=1, source_target_pairs={{0,1},{1,0},{2,3},{3,2},{4,5},{5,4},{6,7},{7,6},{8,9},{9,8},{10,11... | collective-permute-start | bytes 5898248 | tf_op jit(solution)/shard_map/ppermute | solution.py:291
  240.5 10.9 %collective-permute-start.2 = (bf16[2,384,1280]{2,1,0:T(8,128)(2,1)}, bf16[2,384,1280]{2,1,0:T(8,128)(2,1)}, u32[]{:S(2)}, u32[]{:S(2)}) collective-permute-start(bf16[2,384,1280]{2,1,0:T(8,128)(2,1)} %fusion.10), channel_id=1, source_target_pairs={{0,1},{1,0},{2,3},{3,2},{4,5},{5,4},{6,7},{7,6},{8,9},{9,8},{10,11... | collective-permute-start | bytes 5898248 | tf_op jit(solution)/shard_map/ppermute | solution.py:291
  240.5 10.9 %copy-start.2 = (bf16[1,1280,1280]{2,1,0:T(8,128)(2,1)S(1)}, bf16[1,1280,1280]{2,1,0:T(8,128)(2,1)}, u32[]{:S(2)}) copy-start(bf16[1,1280,1280]{2,1,0:T(8,128)(2,1)} %get-tuple-element.15) | copy-start | bytes 9830404
  240.5 10.9 %copy-start.3 = (bf16[1,1280,1280]{2,1,0:T(8,128)(2,1)S(1)}, bf16[1,1280,1280]{2,1,0:T(8,128)(2,1)}, u32[]{:S(2)}) copy-start(bf16[1,1280,1280]{2,1,0:T(8,128)(2,1)} %get-tuple-element.16) | copy-start | bytes 9830404
  240.5 10.9 %copy-start.7 = (bf16[384,1280]{1,0:T(8,128)(2,1)S(1)}, bf16[384,1280]{1,0:T(8,128)(2,1)}, u32[]{:S(2)}) copy-start(bf16[384,1280]{1,0:T(8,128)(2,1)} %shard_map.67) | copy-start | bytes 2949124
  248.1 25.1 %collective-permute-start.1 = (bf16[384,1280]{1,0:T(8,128)(2,1)}, bf16[384,1280]{1,0:T(8,128)(2,1)S(1)}, u32[]{:S(2)}, u32[]{:S(2)}) collective-permute-start(bf16[384,1280]{1,0:T(8,128)(2,1)} %dynamic-slice_bitcast_fusion.3), channel_id=1, source_target_pairs={{0,2},{2,0},{1,3},{3,1},{4,6},{6,4},{5,7},{7,5},{8,10},{10,8},{9,1... | collective-permute-start | bytes 2949128 | tf_op jit(solution)/shard_map/ppermute | solution.py:295
  255.6 1.3 copy-start.4
  257.9 36.6 %collective-permute-start.3 = (bf16[384,1280]{1,0:T(8,128)(2,1)}, bf16[384,1280]{1,0:T(8,128)(2,1)}, u32[]{:S(2)}, u32[]{:S(2)}) collective-permute-start(bf16[384,1280]{1,0:T(8,128)(2,1)} %dynamic-slice_bitcast_fusion.2), channel_id=1, source_target_pairs={{0,2},{2,0},{1,3},{3,1},{4,6},{6,4},{5,7},{7,5},{8,10},{10,8},{9,1... | collective-permute-start | bytes 2949128 | tf_op jit(solution)/shard_map/ppermute | solution.py:295
  257.9 36.6 %copy-start.5 = (bf16[2,384,1280]{2,1,0:T(8,128)(2,1)S(1)}, bf16[2,384,1280]{2,1,0:T(8,128)(2,1)}, u32[]{:S(2)}) copy-start(bf16[2,384,1280]{2,1,0:T(8,128)(2,1)} %copy-done.4) | copy-start | bytes 5898244

commit v14 on v13

--- a/solution.py
+++ b/solution.py
@@ -129,12 +129,34 @@
 
 
 def rope_tables(frame_value, count):
-    angle = pair_angles(frame_value, count)
-    cosine = jnp.cos(angle)
+    tdim = HDIM - 4 * (HDIM // 6)
+    sdim = 2 * (HDIM // 6)
+    tcount = tdim // 2
+    scount = sdim // 2
+    lane = jnp.arange(HDIM)
+    index = lane // 2
+    findex = index.astype(jnp.float32)
+    freq = jnp.where(
+        index < tcount,
+        jnp.power(10000.0, -2.0 * findex / tdim),
+        jnp.where(
+            index < tcount + scount,
+            jnp.power(10000.0, -2.0 * (findex - tcount) / sdim),
+            jnp.power(10000.0, -2.0 * (findex - tcount - scount) / sdim),
+        ),
+    )
+    token = jnp.arange(count)
+    row_pos = (token // GRID_W).astype(jnp.float32)[:, None]
+    col_pos = (token % GRID_W).astype(jnp.float32)[:, None]
+    frame_f = jnp.zeros((count, 1), jnp.float32) + frame_value.astype(jnp.float32)
+    pos = jnp.where(
+        index[None, :] < tcount,
+        frame_f,
+        jnp.where(index[None, :] < tcount + scount, row_pos, col_pos),
+    )
+    angle = pos * freq[None, :]
     sine = jnp.sin(angle)
-    cos_full = jnp.stack([cosine, cosine], axis=-1).reshape(count, HDIM)
-    sin_signed = jnp.stack([-sine, sine], axis=-1).reshape(count, HDIM)
-    return cos_full, sin_signed
+    return jnp.cos(angle), jnp.where(lane[None, :] % 2 == 0, -sine, sine)
 
 
 def rotate_ref(x_ref, cos_ref, sin_ref, swap):

time: 298 us -> 297 us (level)
  local copies, waits for them, and re-layouts: 29.6 us -> 26.6 us
where the time goes in v14:
time: 297 us; the launch traced here: 296 us
  waiting for transfers between devices  89.7 us (30%)
  Pallas kernels  63.2 us (21%)
  blocking collectives  59 us (20%)
  local copies, waits for them, and re-layouts  26.6 us (9%)
  matrix products  23.2 us (8%)
  starting transfers between devices  22.4 us (8%)
  other arithmetic  11 us (4%)
    all_to_all x1, blocking collectives, exchange(): spread = lax.all_to_all(data, FRAME_AXES, 0, 0, tiled=True)  59 us
    all_to_all x1, waiting for transfers between devices, exchange(): prev_full = lax.all_to_all(before, FRAME_AXES, 0, 0, tiled=True)  49.6 us
    ppermute x2, waiting for transfers between devices, head_reduce(): got = lax.ppermute(send, 'xl', [(0, 1), (1, 0)])  36.3 us
    pallas_call x2, Pallas kernels, sink_attention(): pl.pallas_call(sink_kernel, grid_spec=grid_spec, out_shape=jax.ShapeDtype...  31.7 us
    pallas_call x1, Pallas kernels, near_attention(): pl.pallas_call(near_kernel, grid_spec=grid_spec, out_shape=[f32] * 3, cos...  28 us
    dot_general x2, matrix products, head_reduce(): jnp.einsum('rk,xkn->xrn', attended, other_w, preferred_element_type=jnp.f...  12.4 us
    dot_general x2, matrix products, head_reduce(): jnp.einsum('rk,xkn->xrn', attended, mine_w, preferred_element_type=jnp.fl...  10.8 us
    all_to_all x1, starting transfers between devices, exchange(): return (prev_full, lax.all_to_all(copies, FRAME_AXES, 0, 0, tiled=True))  9.42 us
  transfers between devices with their start and end apart: 6, of which 4 were waited for; matrix products, arithmetic and copies ran while one was open for 13% of the time, Pallas kernels for 15%

profile of v14, /device:TPU:1, one launch (start us, length us, event | category | flops | bytes accessed | tf_op | source)
XLA Modules:
  0.0 296.1 jit_solution(13290629323397196676)
XLA Ops:
  0.8 0.6 fusion.19.swap_ref
  1.5 2.5 negate_select_fusion
  4.0 3.5 %shard_map.64.ks_ref = bf16[768,1280]{1,0:T(8,128)(2,1)} custom-call(bf16[768,1280]{1,0:T(8,128)(2,1)} %x_ref.1, bf16[128,128]{1,0:T(8,128)(2,1)} %fusion.19.swap_ref, f32[768,128]{1,0:T(8,128)} %get-tuple-element.20.cos_ref.cq, f32[768,128]{1,0:T(8,128)} %get-tuple-element.19.sin_ref.sq), custom_call_target="tpu_custom_call" | custom-call | flops 251658240 | bytes 3932160 | tf_op jit(solution)/shard_map/pallas_call | solution.py:206
  7.5 0.0 copy-done.6
  7.5 1.8 pad_maximum_fusion.6
  9.3 59.0 %all_to_all.32 = bf16[32,48,1280]{2,1,0:T(8,128)(2,1)S(1)} all-to-all(bf16[32,48,1280]{2,1,0:T(8,128)(2,1)S(1)} %bitcast.50), channel_id=1, replica_groups=mesh['z'=4,'xh'=2,'y'=4,'xl'=2,'c'=2] {'z','xh','y'}, dimensions={0} | all-to-all | bytes 7864320 | tf_op jit(solution)/shard_map/all_to_all | solution.py:121
  68.3 1.8 copy-done
  70.1 0.2 slice.17
  70.4 2.3 pad_maximum_fusion.7
  72.6 6.5 %all-to-all-start.1 = ((bf16[32,48,1280]{2,1,0:T(8,128)(2,1)}), bf16[32,48,1280]{2,1,0:T(8,128)(2,1)}, u32[]{:S(2)}, u32[]{:S(2)}) async-start(bf16[32,48,1280]{2,1,0:T(8,128)(2,1)} %pad_maximum_fusion.7), calls=%async_computation.1 | async-start | bytes 7864320 | tf_op jit(solution)/shard_map/all_to_all | solution.py:124
  79.2 0.0 copy-done.8
  79.3 0.9 constant_dynamic-slice_fusion.2
  80.2 49.6 %all-to-all-done.1 = bf16[32,48,1280]{2,1,0:T(8,128)(2,1)} async-done(((bf16[32,48,1280]{2,1,0:T(8,128)(2,1)}), bf16[32,48,1280]{2,1,0:T(8,128)(2,1)}, u32[]{:S(2)}, u32[]{:S(2)}) %all-to-all-start.1) | async-done | bytes 3932192 | tf_op jit(solution)/shard_map/all_to_all | solution.py:124
  129.8 2.2 broadcast_in_dim.74
  132.0 9.4 %all-to-all-start.2 = ((bf16[32,48,1280]{2,1,0:T(8,128)(2,1)}), bf16[32,48,1280]{2,1,0:T(8,128)(2,1)}, u32[]{:S(2)}, u32[]{:S(2)}) async-start(bf16[32,48,1280]{2,1,0:T(8,128)(2,1)} %broadcast_in_dim.74), calls=%async_computation.2 | async-start | bytes 7864320 | tf_op jit(solution)/shard_map/all_to_all | solution.py:128
  141.4 9.0 %dynamic-slice_bitcast_fusion.1 = (bf16[1,1280,1280]{2,1,0:T(8,128)(2,1)}, bf16[1,1280,1280]{2,1,0:T(8,128)(2,1)}, bf16[1280,1280]{1,0:T(8,128)(2,1)}, bf16[1280,1280]{1,0:T(8,128)(2,1)S(1)}) fusion(bf16[1280,5120]{1,0:T(8,128)(2,1)} %param.9, s32[]{:T(128)S(6)} %select_n.107, s32[]{:T(128)S(6)} %select_n.108, s32[]{:T(128)S(6)} %select_n.121, s32[]{:T(128)S(6)} %select_n.120), kind=kLoop, calls=%fused_computation.17 | loop fusion | bytes 26214416 | tf_op jit(solution)/shard_map/stack | solution.py:302
  150.4 5.7 %copy.8 = bf16[1280,1280]{0,1:T(8,128)(2,1)} copy(bf16[1280,1280]{1,0:T(8,128)(2,1)} %get-tuple-element.17) | data formatting | bytes 6553600 | tf_op jit(solution)/shard_map/dynamic_slice | solution.py:303
  156.1 3.4 %copy.7 = bf16[1280,1280]{0,1:T(8,128)(2,1)} copy(bf16[1280,1280]{1,0:T(8,128)(2,1)S(1)} %get-tuple-element.18) | data formatting | bytes 6553600 | tf_op jit(solution)/shard_map/dynamic_slice | solution.py:303
  159.5 0.6 add_convert_fusion.flags
  160.1 28.0 %shard_map.65 = (f32[768,1280]{1,0:T(8,128)}, f32[768,1280]{1,0:T(8,128)}, f32[768,1280]{1,0:T(8,128)}) custom-call(s32[2]{0:T(128)} %add_convert_fusion.flags, bf16[768,1280]{1,0:T(8,128)(2,1)} %q_ref.5, bf16[768,1280]{1,0:T(8,128)(2,1)} %shard_map.64.ks_ref, bf16[768,1280]{1,0:T(8,128)(2,1)} %vs_ref.1, bf16[1536,1280]{1,0:T(8,128)(2,1)} %bitcast.9.kp_ref.vp_ref, ...), custom_call_target="tpu_custom_call" | custom-call | flops 6039797760 | bytes 21626880 | tf_op jit(solution)/shard_map/pallas_call | solution.py:261
  188.1 3.8 %all-to-all-done.2 = bf16[32,48,1280]{2,1,0:T(8,128)(2,1)} async-done(((bf16[32,48,1280]{2,1,0:T(8,128)(2,1)}), bf16[32,48,1280]{2,1,0:T(8,128)(2,1)}, u32[]{:S(2)}, u32[]{:S(2)}) %all-to-all-start.2) | async-done | bytes 3932192 | tf_op jit(solution)/shard_map/all_to_all | solution.py:128
  191.9 16.0 %shard_map.66 = bf16[384,1280]{1,0:T(8,128)(2,1)} custom-call(s32[2]{0:T(128)} %add_convert_fusion.flags, bf16[768,1280]{1,0:T(8,128)(2,1)} %q_ref.5, bf16[1536,1280]{1,0:T(8,128)(2,1)} %bitcast.11.kk_ref.vk_ref, bf16[1536,1280]{1,0:T(8,128)(2,1)} %bitcast.11.kk_ref.vk_ref, bf16[128,128]{1,0:T(8,128)(2,1)} %fusion.19.swap_ref, ...), custom_call_target="tpu_custom_call" | custom-call | flops 1509949440 | bytes 10813440 | tf_op jit(solution)/shard_map/pallas_call | solution.py:288
  207.9 0.0 copy-done.1
  207.9 6.2 %fusion.11 = bf16[2,384,1280]{2,1,0:T(8,128)(2,1)} fusion(bf16[1,1280,1280]{1,2,0:T(8,128)(2,1)S(1)} %bitcast.51, bf16[1,1280,1280]{1,2,0:T(8,128)(2,1)} %bitcast.53, bf16[384,1280]{1,0:T(8,128)(2,1)} %shard_map.66), kind=kOutput, calls=%fused_computation.19 | convolution fusion | flops 2520842240 | bytes 9502720 | tf_op jit(solution)/shard_map/rk,xkn->xrn/dot_general | solution.py:312
  214.1 3.1 %collective-permute-start = (bf16[2,384,1280]{2,1,0:T(8,128)(2,1)}, bf16[2,384,1280]{2,1,0:T(8,128)(2,1)}, u32[]{:S(2)}, u32[]{:S(2)}) collective-permute-start(bf16[2,384,1280]{2,1,0:T(8,128)(2,1)} %fusion.11), channel_id=1, source_target_pairs={{0,1},{1,0},{2,3},{3,2},{4,5},{5,4},{6,7},{7,6},{8,9},{9,8},{10,11... | collective-permute-start | bytes 5898248 | tf_op jit(solution)/shard_map/ppermute | solution.py:313
  217.2 15.7 %shard_map.67 = bf16[384,1280]{1,0:T(8,128)(2,1)} custom-call(s32[2]{0:T(128)} %add_convert_fusion.flags, bf16[768,1280]{1,0:T(8,128)(2,1)} %q_ref.5, bf16[1536,1280]{1,0:T(8,128)(2,1)} %bitcast.11.kk_ref.vk_ref, bf16[1536,1280]{1,0:T(8,128)(2,1)} %bitcast.11.kk_ref.vk_ref, bf16[128,128]{1,0:T(8,128)(2,1)} %fusion.19.swap_ref, ...), custom_call_target="tpu_custom_call" | custom-call | flops 1509949440 | bytes 10813440 | tf_op jit(solution)/shard_map/pallas_call | solution.py:288
  232.9 6.2 %fusion.10 = bf16[2,384,1280]{2,1,0:T(8,128)(2,1)} fusion(bf16[1,1280,1280]{1,2,0:T(8,128)(2,1)S(1)} %bitcast.52, bf16[1,1280,1280]{1,2,0:T(8,128)(2,1)} %bitcast.54, bf16[384,1280]{1,0:T(8,128)(2,1)} %shard_map.67), kind=kOutput, calls=%fused_computation.18 | convolution fusion | flops 2520842240 | bytes 9502720 | tf_op jit(solution)/shard_map/rk,xkn->xrn/dot_general | solution.py:312
  239.1 0.0 collective-permute-start.2
  239.1 0.0 collective-permute-done
  239.2 0.0 copy-start.3
  239.2 0.0 copy-start.7
  239.2 6.6 %fusion.5 = bf16[2,384,1280]{2,1,0:T(8,128)(2,1)S(1)} fusion(bf16[2,384,1280]{2,1,0:T(8,128)(2,1)} %collective-permute-done, bf16[1,1280,1280]{2,1,0:T(8,128)(2,1)} %get-tuple-element.16, bf16[1,1280,1280]{2,1,0:T(8,128)(2,1)} %get-tuple-element.15, bf16[384,1280]{1,0:T(8,128)(2,1)} %shard_map.66), kind=kOutput, calls=%fused_computation.11 | convolution fusion | flops 2534604800 | bytes 11468800 | tf_op jit(solution)/shard_map/rk,xkn->xrn/dot_general | solution.py:311
  245.8 1.0 dynamic-slice_bitcast_fusion.3
  246.8 3.3 %collective-permute-start.1 = (bf16[384,1280]{1,0:T(8,128)(2,1)}, bf16[384,1280]{1,0:T(8,128)(2,1)S(1)}, u32[]{:S(2)}, u32[]{:S(2)}) collective-permute-start(bf16[384,1280]{1,0:T(8,128)(2,1)} %dynamic-slice_bitcast_fusion.3), channel_id=1, source_target_pairs={{0,2},{2,0},{1,3},{3,1},{4,6},{6,4},{5,7},{7,5},{8,10},{10,8},{9,1... | collective-permute-start | bytes 2949128 | tf_op jit(solution)/shard_map/ppermute | solution.py:317
  250.1 0.0 collective-permute-done.2
  250.1 0.0 copy-done.2
  250.1 0.0 copy-done.3
  250.1 0.0 copy-done.7
  250.2 4.2 %fusion.4 = bf16[2,384,1280]{2,1,0:T(8,128)(2,1)S(1)} fusion(bf16[2,384,1280]{2,1,0:T(8,128)(2,1)} %collective-permute-done.2, bf16[1,1280,1280]{2,1,0:T(8,128)(2,1)S(1)} %copy-done.3, bf16[1,1280,1280]{2,1,0:T(8,128)(2,1)S(1)} %copy-done.2, bf16[384,1280]{1,0:T(8,128)(2,1)S(1)} %copy-done.7), kind=kOutput, calls=%fused_computation.9 | convolution fusion | flops 2534604800 | bytes 11468800 | tf_op jit(solution)/shard_map/rk,xkn->xrn/dot_general | solution.py:311
  254.3 0.0 copy-start.4
  254.3 1.3 copy-done.4
  255.6 1.0 dynamic-slice_bitcast_fusion.2
  256.6 0.0 collective-permute-start.3
  256.7 15.4 %collective-permute-done.1 = bf16[384,1280]{1,0:T(8,128)(2,1)S(1)} collective-permute-done((bf16[384,1280]{1,0:T(8,128)(2,1)}, bf16[384,1280]{1,0:T(8,128)(2,1)S(1)}, u32[]{:S(2)}, u32[]{:S(2)}) %collective-permute-start.1) | collective-permute-done | bytes 983072 | tf_op jit(solution)/shard_map/ppermute | solution.py:317
  272.0 0.2 fusion.13
  272.3 20.9 %collective-permute-done.3 = bf16[384,1280]{1,0:T(8,128)(2,1)} collective-permute-done((bf16[384,1280]{1,0:T(8,128)(2,1)}, bf16[384,1280]{1,0:T(8,128)(2,1)}, u32[]{:S(2)}, u32[]{:S(2)}) %collective-permute-start.3) | collective-permute-done | bytes 983072 | tf_op jit(solution)/shard_map/ppermute | solution.py:317
  293.2 1.5 fusion.12
  294.7 1.4 pad_maximum_fusion.24
  (13 shorter events, 0.1 us)
Async XLA Ops:
  0.0 7.5 %copy-start.6 = (bf16[768,1280]{1,0:T(8,128)(2,1)S(1)}, bf16[768,1280]{1,0:T(8,128)(2,1)}, u32[]{:S(2)}) copy-start(bf16[768,1280]{1,0:T(8,128)(2,1)} %vs_ref.1) | copy-start | bytes 5898244
  68.3 1.9 copy-start
  72.6 6.5 %copy-start.8 = (s32[32]{0:T(128)S(1)}, s32[32]{0:T(128)}, u32[]{:S(2)}) copy-start(s32[32]{0:T(128)} %param.10) | copy-start | bytes 388
  72.6 57.1 %all-to-all-start.1 = ((bf16[32,48,1280]{2,1,0:T(8,128)(2,1)}), bf16[32,48,1280]{2,1,0:T(8,128)(2,1)}, u32[]{:S(2)}, u32[]{:S(2)}) async-start(bf16[32,48,1280]{2,1,0:T(8,128)(2,1)} %pad_maximum_fusion.7), calls=%async_computation.1 | async-start | bytes 7864320 | tf_op jit(solution)/shard_map/all_to_all | solution.py:124
  132.0 59.9 %all-to-all-start.2 = ((bf16[32,48,1280]{2,1,0:T(8,128)(2,1)}), bf16[32,48,1280]{2,1,0:T(8,128)(2,1)}, u32[]{:S(2)}, u32[]{:S(2)}) async-start(bf16[32,48,1280]{2,1,0:T(8,128)(2,1)} %broadcast_in_dim.74), calls=%async_computation.2 | async-start | bytes 7864320 | tf_op jit(solution)/shard_map/all_to_all | solution.py:128
  191.9 16.0 %copy-start.1 = (bf16[1280,1280]{0,1:T(8,128)(2,1)S(1)}, bf16[1280,1280]{0,1:T(8,128)(2,1)}, u32[]{:S(2)}) copy-start(bf16[1280,1280]{0,1:T(8,128)(2,1)} %copy.8) | copy-start | bytes 9830404
  214.1 25.0 %collective-permute-start = (bf16[2,384,1280]{2,1,0:T(8,128)(2,1)}, bf16[2,384,1280]{2,1,0:T(8,128)(2,1)}, u32[]{:S(2)}, u32[]{:S(2)}) collective-permute-start(bf16[2,384,1280]{2,1,0:T(8,128)(2,1)} %fusion.11), channel_id=1, source_target_pairs={{0,1},{1,0},{2,3},{3,2},{4,5},{5,4},{6,7},{7,6},{8,9},{9,8},{10,11... | collective-permute-start | bytes 5898248 | tf_op jit(solution)/shard_map/ppermute | solution.py:313
  239.1 11.0 %collective-permute-start.2 = (bf16[2,384,1280]{2,1,0:T(8,128)(2,1)}, bf16[2,384,1280]{2,1,0:T(8,128)(2,1)}, u32[]{:S(2)}, u32[]{:S(2)}) collective-permute-start(bf16[2,384,1280]{2,1,0:T(8,128)(2,1)} %fusion.10), channel_id=1, source_target_pairs={{0,1},{1,0},{2,3},{3,2},{4,5},{5,4},{6,7},{7,6},{8,9},{9,8},{10,11... | collective-permute-start | bytes 5898248 | tf_op jit(solution)/shard_map/ppermute | solution.py:313
  239.1 11.0 %copy-start.2 = (bf16[1,1280,1280]{2,1,0:T(8,128)(2,1)S(1)}, bf16[1,1280,1280]{2,1,0:T(8,128)(2,1)}, u32[]{:S(2)}) copy-start(bf16[1,1280,1280]{2,1,0:T(8,128)(2,1)} %get-tuple-element.15) | copy-start | bytes 9830404
  239.2 11.0 %copy-start.3 = (bf16[1,1280,1280]{2,1,0:T(8,128)(2,1)S(1)}, bf16[1,1280,1280]{2,1,0:T(8,128)(2,1)}, u32[]{:S(2)}) copy-start(bf16[1,1280,1280]{2,1,0:T(8,128)(2,1)} %get-tuple-element.16) | copy-start | bytes 9830404
  239.2 11.0 %copy-start.7 = (bf16[384,1280]{1,0:T(8,128)(2,1)S(1)}, bf16[384,1280]{1,0:T(8,128)(2,1)}, u32[]{:S(2)}) copy-start(bf16[384,1280]{1,0:T(8,128)(2,1)} %shard_map.67) | copy-start | bytes 2949124
  246.8 25.2 %collective-permute-start.1 = (bf16[384,1280]{1,0:T(8,128)(2,1)}, bf16[384,1280]{1,0:T(8,128)(2,1)S(1)}, u32[]{:S(2)}, u32[]{:S(2)}) collective-permute-start(bf16[384,1280]{1,0:T(8,128)(2,1)} %dynamic-slice_bitcast_fusion.3), channel_id=1, source_target_pairs={{0,2},{2,0},{1,3},{3,1},{4,6},{6,4},{5,7},{7,5},{8,10},{10,8},{9,1... | collective-permute-start | bytes 2949128 | tf_op jit(solution)/shard_map/ppermute | solution.py:317
  254.3 1.3 copy-start.4
  256.6 36.6 %collective-permute-start.3 = (bf16[384,1280]{1,0:T(8,128)(2,1)}, bf16[384,1280]{1,0:T(8,128)(2,1)}, u32[]{:S(2)}, u32[]{:S(2)}) collective-permute-start(bf16[384,1280]{1,0:T(8,128)(2,1)} %dynamic-slice_bitcast_fusion.2), channel_id=1, source_target_pairs={{0,2},{2,0},{1,3},{3,1},{4,6},{6,4},{5,7},{7,5},{8,10},{10,8},{9,1... | collective-permute-start | bytes 2949128 | tf_op jit(solution)/shard_map/ppermute | solution.py:317
  256.6 36.6 %copy-start.5 = (bf16[2,384,1280]{2,1,0:T(8,128)(2,1)S(1)}, bf16[2,384,1280]{2,1,0:T(8,128)(2,1)}, u32[]{:S(2)}) copy-start(bf16[2,384,1280]{2,1,0:T(8,128)(2,1)} %copy-done.4) | copy-start | bytes 5898244
